TPU v7x, 256 devices: a whole 4x4x8 slice. The times are simulated.
256 devices in a mesh: gx: 128 (over z, y, x_hi, core), gy: 2 (over x_lo).
Axes of the slice: x: 4 (x_hi: 2, x_lo: 2; x = x_hi * 2 + x_lo), y: 4, z: 8, core: 2. Of those that a mesh axis runs over, the one named last changes fastest.
Arguments:
- displacement: float32 [2, 4096, 16384], P(None, 'gx', 'gy'), may hold values from -4 to 4
- velocity: float32 [2, 4096, 16384], P(None, 'gx', 'gy'), may hold values from -6 to 6
- damage: float32 [4096, 16384], P('gx', 'gy'), may hold values from 0 to 0.9
- history: float32 [4096, 16384], P('gx', 'gy'), may hold values from 0.02 to 1
- toughness: float32 [4096, 16384], P('gx', 'gy'), may hold values from 0.3 to 3
Outputs:
- displacement_new: float32 [2, 4096, 16384], P(None, 'gx', 'gy')
- velocity_new: float32 [2, 4096, 16384], P(None, 'gx', 'gy')
- history_new: float32 [4096, 16384], P('gx', 'gy')
- damage_new: float32 [4096, 16384], P('gx', 'gy')
All inputs are finite; a program needn't handle non-finite values.
Results may differ from a plain program's by a relative error of at most 0.00002.
Values sent between devices are 32-bit elements; how exact they have to be, the bound alone decides.
No kernel may reach another device: no remote copies, remote signals or barrier semaphores. Data moves between devices by JAX's collectives and lax.ppermute only.
A program may use at most 128 MiB of HBM per device.

v0:
```python
import jax
import jax.numpy as jnp
from jax import lax
from jax.sharding import PartitionSpec as P

CHEB = 0.94
WEIGHT_TWO = 1.0 / (1.0 - CHEB * CHEB / 2.0)
WEIGHT_THREE = 1.0 / (1.0 - CHEB * CHEB * WEIGHT_TWO / 4.0)


def padded_2(block, sides, width):
    for axis, dim in sides:
        count = lax.axis_size(axis)
        forward = [(i, i + 1) for i in range(count - 1)]
        backward = [(target, source) for source, target in forward]
        low = lax.ppermute(
            lax.slice_in_dim(block, block.shape[dim] - width, None, axis=dim), axis, forward
        )
        high = lax.ppermute(lax.slice_in_dim(block, 0, width, axis=dim), axis, backward)
        block = jnp.concatenate([low, block, high], axis=dim)
    return block


def strain(first, second):
    exx = (first[2:, 1:-1] - first[:-2, 1:-1]) * 0.5
    eyy = (second[1:-1, 2:] - second[1:-1, :-2]) * 0.5
    exy = (first[1:-1, 2:] - first[1:-1, :-2] + (second[2:, 1:-1] - second[:-2, 1:-1])) * 0.25
    return (exx, eyy, exy)


def stress_of(eu, ev, dmg):
    exx = eu[0] + 0.5 * ev[0]
    eyy = eu[1] + 0.5 * ev[1]
    exy = eu[2] + 0.5 * ev[2]
    degrade = (1.0 - dmg) ** 2 + 0.001
    trace = exx + eyy
    return jnp.stack(
        [degrade * (trace + 2.0 * exx), degrade * (trace + 2.0 * eyy), degrade * 2.0 * exy]
    )


def accel(sxx, syy, sxy):
    first = (sxx[2:, 1:-1] - sxx[:-2, 1:-1] + (sxy[1:-1, 2:] - sxy[1:-1, :-2])) * 0.5
    second = (sxy[2:, 1:-1] - sxy[:-2, 1:-1] + (syy[1:-1, 2:] - syy[1:-1, :-2])) * 0.5
    return jnp.stack([first, second])


def energy(eu):
    trace = jnp.maximum(eu[0] + eu[1], 0.0)
    return 0.5 * trace * trace + eu[0] ** 2 + eu[1] ** 2 + 2.0 * eu[2] ** 2


def jacobi(field_pad, hist, tough_pad):
    tough = tough_pad[1:-1, 1:-1]
    k_down = tough + tough_pad[2:, 1:-1]
    k_up = tough + tough_pad[:-2, 1:-1]
    k_right = tough + tough_pad[1:-1, 2:]
    k_left = tough + tough_pad[1:-1, :-2]
    numer = 2.0 * hist + k_down * field_pad[2:, 1:-1] + k_up * field_pad[:-2, 1:-1]
    numer = numer + k_right * field_pad[1:-1, 2:] + k_left * field_pad[1:-1, :-2]
    denom = tough * 0.5 + 2.0 * hist + k_down + k_up + k_right + k_left
    return jnp.where(True, numer / jnp.where(True, denom, 1.0), 0.0)


def on_device(displacement, velocity, damage, history, toughness):

    def accel_of(disp, vel):
        padded = padded_2(jnp.concatenate([disp, vel], 0), (("gx", 1), ("gy", 2)), 1)
        eu = strain(padded[0], padded[1])
        ev = strain(padded[2], padded[3])
        sig = padded_2(stress_of(eu, ev, damage), (("gx", 1), ("gy", 2)), 1)
        return (accel(sig[0], sig[1], sig[2]), eu)

    first_acc, unused = accel_of(displacement, velocity)
    half = velocity + 0.1 * first_acc
    disp_new = displacement + 0.2 * half
    second_acc, eu_core = accel_of(disp_new, half)
    vel_new = half + 0.1 * second_acc
    hist_new = jnp.maximum(history, energy(eu_core))
    tough_pad = padded_2(toughness, (("gx", 0), ("gy", 1)), 1)
    iterates = [damage]
    for sweep in range(3):
        current = iterates[-1]
        mapped = jacobi(padded_2(current, (("gx", 0), ("gy", 1)), 1), hist_new, tough_pad)
        if sweep == 0:
            iterates.append(mapped)
        elif sweep == 1:
            iterates.append(iterates[0] + WEIGHT_TWO * (mapped - iterates[0]))
        else:
            iterates.append(iterates[1] + WEIGHT_THREE * (mapped - iterates[1]))
    dmg_new = iterates[-1]
    return (disp_new, vel_new, hist_new, dmg_new)


def solution(mesh):
    placed = (P(None, "gx", "gy"), P(None, "gx", "gy"), P("gx", "gy"), P("gx", "gy"), P("gx", "gy"))
    return jax.shard_map(
        on_device,
        mesh=mesh,
        in_specs=placed,
        out_specs=(P(None, "gx", "gy"), P(None, "gx", "gy"), P("gx", "gy"), P("gx", "gy")),
        check_vma=False,
    )
```

profile of v0, /device:TPU:127, one launch (start us, length us, event | category | flops | bytes accessed | tf_op | source)
XLA Modules:
  0.0 215.1 jit_solution(9435020243665694710)
XLA Ops:
  0.6 1.9 constant_dynamic-update-slice_fusion.1
  3.2 5.8 %collective-permute-start = (f32[4,1,8192]{2,1,0:T(1,128)S(1)}, f32[4,1,8192]{2,1,0:T(1,128)S(1)}, u32[]{:S(2)}, u32[]{:S(2)}) collective-permute-start(f32[4,1,8192]{2,1,0:T(1,128)S(1)} %get-tuple-element.30), channel_id=1, source_target_pairs={{0,2},{2,4},{4,6},{6,8},{8,10},{10,12},{12,14},{14,16},{16,18},{18... | collective-permute-start | bytes 393224 | tf_op jit(solution)/shard_map/ppermute | solution.py:16
  9.0 1.9 collective-permute-start.1
  11.0 10.1 %collective-permute-done.1 = f32[4,1,8192]{2,1,0:T(1,128)S(1)} collective-permute-done((f32[4,1,8192]{2,1,0:T(1,128)S(1)}, f32[4,1,8192]{2,1,0:T(1,128)S(1)}, u32[]{:S(2)}, u32[]{:S(2)}) %collective-permute-start.1) | collective-permute-done | bytes 131104 | tf_op jit(solution)/shard_map/ppermute | solution.py:19
  21.8 2.4 %copy-done.2 = f32[4,34,8192]{2,1,0:T(8,128)} copy-done((f32[4,34,8192]{2,1,0:T(8,128)}, f32[4,34,8192]{2,1,0:T(8,128)S(1)}, u32[]{:S(2)}) %copy-start.2) | copy-done | bytes 4456472
  25.5 4.0 %collective-permute-start.3 = (f32[4,34,1]{2,1,0:T(8,128)S(1)}, f32[4,34,1]{2,1,0:T(8,128)S(1)}, u32[]{:S(2)}, u32[]{:S(2)}) collective-permute-start(f32[4,34,1]{2,1,0:T(8,128)S(1)} %get-tuple-element.26), channel_id=1, source_target_pairs={{1,0},{3,2},{5,4},{7,6},{9,8},{11,10},{13,12},{15,14},{17,16},{19,... | collective-permute-start | bytes 1640 | tf_op jit(solution)/shard_map/ppermute | solution.py:19
  29.5 1.5 collective-permute-done.3
  31.0 8.0 %concatenate.96 = f32[4,34,8194]{2,1,0:T(8,128)} concatenate(f32[4,34,1]{2,1,0:T(8,128)S(1)} %collective-permute-done.2, f32[4,34,8192]{2,1,0:T(8,128)} %copy-done.2, f32[4,34,1]{2,1,0:T(8,128)S(1)} %collective-permute-done.3), dimensions={2} | concatenate | bytes 8915072 | tf_op jit(solution)/shard_map/concatenate | solution.py:20
  39.0 3.0 %slice_bitcast_fusion.13 = (f32[34,8194]{1,0:T(8,128)S(1)}, f32[34,8194]{1,0:T(8,128)S(1)}, f32[34,8194]{1,0:T(8,128)S(1)}, f32[34,8194]{1,0:T(8,128)S(1)}) fusion(f32[4,34,8194]{2,1,0:T(8,128)} %concatenate.96), kind=kLoop, calls=%fused_computation.23 | loop fusion | bytes 8915072 | tf_op jit(solution)/shard_map/squeeze | solution.py:69
  42.0 3.5 %multiply_bitcast_fusion.3 = (f32[1,32,8192]{2,1,0:T(8,128)S(1)}, f32[32,8192]{1,0:T(8,128)S(1)}, f32[32,8192]{1,0:T(8,128)S(1)}, f32[1,32,8192]{2,1,0:T(8,128)S(1)}) fusion(f32[32,8192]{1,0:T(8,128)S(1)} %copy-done, f32[34,8194]{1,0:T(8,128)S(1)} %get-tuple-element.23, f32[34,8194]{1,0:T(8,128)S(1)} %get-tuple-element.20, ...), kind=kLoop, calls=%fused_computation.163 | loop fusion | flops 7340032 | bytes 22020096 | tf_op jit(solution)/shard_map/stack | solution.py:37
  45.9 2.9 %collective-permute-start.4 = (f32[3,1,8192]{2,1,0:T(1,128)S(1)}, f32[3,1,8192]{2,1,0:T(1,128)S(1)}, u32[]{:S(2)}, u32[]{:S(2)}) collective-permute-start(f32[3,1,8192]{2,1,0:T(1,128)S(1)} %get-tuple-element.45), channel_id=1, source_target_pairs={{0,2},{2,4},{4,6},{6,8},{8,10},{10,12},{12,14},{14,16},{16,18},{18... | collective-permute-start | bytes 294920 | tf_op jit(solution)/shard_map/ppermute | solution.py:16
  48.8 1.9 collective-permute-start.5
  50.8 9.7 %collective-permute-done.5 = f32[3,1,8192]{2,1,0:T(1,128)S(1)} collective-permute-done((f32[3,1,8192]{2,1,0:T(1,128)S(1)}, f32[3,1,8192]{2,1,0:T(1,128)S(1)}, u32[]{:S(2)}, u32[]{:S(2)}) %collective-permute-start.5) | collective-permute-done | bytes 98336 | tf_op jit(solution)/shard_map/ppermute | solution.py:19
  61.0 1.9 copy-done.7
  64.3 4.0 %collective-permute-start.7 = (f32[3,34,1]{2,1,0:T(8,128)S(1)}, f32[3,34,1]{2,1,0:T(8,128)S(1)}, u32[]{:S(2)}, u32[]{:S(2)}) collective-permute-start(f32[3,34,1]{2,1,0:T(8,128)S(1)} %get-tuple-element.40), channel_id=1, source_target_pairs={{1,0},{3,2},{5,4},{7,6},{9,8},{11,10},{13,12},{15,14},{17,16},{19,... | collective-permute-start | bytes 1232 | tf_op jit(solution)/shard_map/ppermute | solution.py:19
  69.4 1.9 collective-permute-start.16
  71.3 9.4 %collective-permute-start.18 = (f32[1,8192]{1,0:T(1,128)S(1)}, f32[1,8192]{1,0:T(1,128)S(1)}, u32[]{:S(2)}, u32[]{:S(2)}) collective-permute-start(f32[1,8192]{1,0:T(1,128)S(1)} %get-tuple-element.63), channel_id=1, source_target_pairs={{0,2},{2,4},{4,6},{6,8},{8,10},{10,12},{12,14},{14,16},{16,18},{18... | collective-permute-start | bytes 98312 | tf_op jit(solution)/shard_map/ppermute | solution.py:16
  80.7 6.3 %concatenate.98 = f32[3,34,8194]{2,1,0:T(8,128)} concatenate(f32[3,34,1]{2,1,0:T(8,128)S(1)} %collective-permute-done.6, f32[3,34,8192]{2,1,0:T(8,128)} %copy-done.7, f32[3,34,1]{2,1,0:T(8,128)S(1)} %collective-permute-done.7), dimensions={2} | concatenate | bytes 6686304 | tf_op jit(solution)/shard_map/concatenate | solution.py:20
  87.0 2.4 %slice_bitcast_fusion.9 = (f32[34,8194]{1,0:T(8,128)S(1)}, f32[34,8194]{1,0:T(8,128)S(1)}, f32[34,8194]{1,0:T(8,128)S(1)}) fusion(f32[3,34,8194]{2,1,0:T(8,128)} %concatenate.98), kind=kLoop, calls=%fused_computation.19 | loop fusion | bytes 6686304 | tf_op jit(solution)/shard_map/squeeze | solution.py:72
  89.4 1.7 fusion.67
  92.4 2.2 %collective-permute-start.8 = (f32[4,1,8192]{2,1,0:T(1,128)S(1)}, f32[4,1,8192]{2,1,0:T(1,128)S(1)}, u32[]{:S(2)}, u32[]{:S(2)}) collective-permute-start(f32[4,1,8192]{2,1,0:T(1,128)S(1)} %get-tuple-element.28), channel_id=1, source_target_pairs={{0,2},{2,4},{4,6},{6,8},{8,10},{10,12},{12,14},{14,16},{16,18},{18... | collective-permute-start | bytes 393224 | tf_op jit(solution)/shard_map/ppermute | solution.py:16
  94.6 2.4 %collective-permute-start.9 = (f32[4,1,8192]{2,1,0:T(1,128)S(1)}, f32[4,1,8192]{2,1,0:T(1,128)S(1)}, u32[]{:S(2)}, u32[]{:S(2)}) collective-permute-start(f32[4,1,8192]{2,1,0:T(1,128)S(1)} %get-tuple-element.29), channel_id=1, source_target_pairs={{2,0},{4,2},{6,4},{8,6},{10,8},{12,10},{14,12},{16,14},{18,16},{20... | collective-permute-start | bytes 393224 | tf_op jit(solution)/shard_map/ppermute | solution.py:19
  97.0 1.9 collective-permute-start.17
  99.0 9.4 %collective-permute-start.19 = (f32[1,8192]{1,0:T(1,128)S(1)}, f32[1,8192]{1,0:T(1,128)S(1)}, u32[]{:S(2)}, u32[]{:S(2)}) collective-permute-start(f32[1,8192]{1,0:T(1,128)S(1)} %get-tuple-element.65), channel_id=1, source_target_pairs={{0,2},{2,4},{4,6},{6,8},{8,10},{10,12},{12,14},{14,16},{16,18},{18... | collective-permute-start | bytes 98312 | tf_op jit(solution)/shard_map/ppermute | solution.py:16
  112.4 2.4 %copy-done.1 = f32[4,34,8192]{2,1,0:T(8,128)} copy-done((f32[4,34,8192]{2,1,0:T(8,128)}, f32[4,34,8192]{2,1,0:T(8,128)S(1)}, u32[]{:S(2)}) %copy-start.1) | copy-done | bytes 4456472
  116.2 4.0 %collective-permute-start.11 = (f32[4,34,1]{2,1,0:T(8,128)S(1)}, f32[4,34,1]{2,1,0:T(8,128)S(1)}, u32[]{:S(2)}, u32[]{:S(2)}) collective-permute-start(f32[4,34,1]{2,1,0:T(8,128)S(1)} %get-tuple-element.24), channel_id=1, source_target_pairs={{1,0},{3,2},{5,4},{7,6},{9,8},{11,10},{13,12},{15,14},{17,16},{19,... | collective-permute-start | bytes 1640 | tf_op jit(solution)/shard_map/ppermute | solution.py:19
  122.1 1.5 collective-permute-start.23
  123.6 8.1 %concatenate.101 = f32[4,34,8194]{2,1,0:T(8,128)} concatenate(f32[4,34,1]{2,1,0:T(8,128)S(1)} %collective-permute-done.10, f32[4,34,8192]{2,1,0:T(8,128)} %copy-done.1, f32[4,34,1]{2,1,0:T(8,128)S(1)} %collective-permute-done.11), dimensions={2} | concatenate | bytes 8915072 | tf_op jit(solution)/shard_map/concatenate | solution.py:20
  131.7 3.0 %slice_bitcast_fusion.5 = (f32[34,8194]{1,0:T(8,128)S(1)}, f32[34,8194]{1,0:T(8,128)S(1)}, f32[34,8194]{1,0:T(8,128)S(1)}, f32[34,8194]{1,0:T(8,128)S(1)}) fusion(f32[4,34,8194]{2,1,0:T(8,128)} %concatenate.101), kind=kLoop, calls=%fused_computation.15 | loop fusion | bytes 8915072 | tf_op jit(solution)/shard_map/squeeze | solution.py:70
  134.8 5.6 %fusion.32 = (f32[32,8192]{1,0:T(8,128)S(1)}, f32[32,8192]{1,0:T(8,128)S(1)}, f32[32,8192]{1,0:T(8,128)}) fusion(f32[34,1]{1,0:T(8,128)S(1)} %collective-permute-done.23, f32[1,8192]{1,0:T(1,128)S(1)} %collective-permute-done.17, f32[32,8192]{1,0:T(8,128)S(1)} %copy-done, f32[1,8192]{1,0:T(1,128)S(1)} %collective-permute-done.19, ...), kind=kLoop, calls=%fused_computation.71 | loop fusion | flops 14680064 | bytes 14811680 | tf_op jit(solution)/shard_map/div | solution.py:62
  140.5 1.9 collective-permute-start.24
  142.4 9.4 %collective-permute-start.25 = (f32[1,8192]{1,0:T(1,128)S(1)}, f32[1,8192]{1,0:T(1,128)S(1)}, u32[]{:S(2)}, u32[]{:S(2)}) collective-permute-start(f32[1,8192]{1,0:T(1,128)S(1)} %get-tuple-element.61), channel_id=1, source_target_pairs={{0,2},{2,4},{4,6},{6,8},{8,10},{10,12},{12,14},{14,16},{16,18},{18... | collective-permute-start | bytes 98312 | tf_op jit(solution)/shard_map/ppermute | solution.py:16
  151.8 5.1 %multiply_bitcast_fusion.1 = (f32[1,32,8192]{2,1,0:T(8,128)S(1)}, f32[32,8192]{1,0:T(8,128)}, f32[32,8192]{1,0:T(8,128)}, f32[1,32,8192]{2,1,0:T(8,128)S(1)}) fusion(f32[32,8192]{1,0:T(8,128)S(1)} %copy-done, f32[34,8194]{1,0:T(8,128)S(1)} %get-tuple-element.16, f32[34,8194]{1,0:T(8,128)S(1)} %get-tuple-element.19, f32[34,8194]{1,0:T(8,128)S(1)} %get-tuple-element.17, ...), kind=kLoop, calls=%fused_computation.161 | loop fusion | flops 6291456 | bytes 18874368 | tf_op jit(solution)/shard_map/stack | solution.py:37
  157.0 4.0 %collective-permute-start.26 = (f32[34,1]{1,0:T(8,128)S(1)}, f32[34,1]{1,0:T(8,128)S(1)}, u32[]{:S(2)}, u32[]{:S(2)}) collective-permute-start(f32[34,1]{1,0:T(8,128)S(1)} %get-tuple-element.53), channel_id=1, source_target_pairs={{1,0},{3,2},{5,4},{7,6},{9,8},{11,10},{13,12},{15,14},{17,16},{19,... | collective-permute-start | bytes 416 | tf_op jit(solution)/shard_map/ppermute | solution.py:19
  162.3 1.8 multiply_bitcast_fusion
  165.5 2.7 %fusion.23 = f32[32,8192]{1,0:T(8,128)S(1)} fusion(f32[32,8192]{1,0:T(8,128)S(1)} %copy-done, f32[34,1]{1,0:T(8,128)S(1)} %collective-permute-done.27, f32[1,8192]{1,0:T(1,128)S(1)} %collective-permute-done.24, f32[32,8192]{1,0:T(8,128)S(1)} %get-tuple-element.4, f32[1,8192]{1,0:T(1,128)S(1)} %collective-permute-done.25, ...), kind=kLoop, calls=%fused_computation.54 | loop fusion | flops 10223616 | bytes 5374496 | tf_op jit(solution)/shard_map/add | solution.py:88
  168.3 1.9 collective-permute-start.28
  170.2 9.4 %collective-permute-start.29 = (f32[1,8192]{1,0:T(1,128)S(1)}, f32[1,8192]{1,0:T(1,128)S(1)}, u32[]{:S(2)}, u32[]{:S(2)}) collective-permute-start(f32[1,8192]{1,0:T(1,128)S(1)} %get-tuple-element.59), channel_id=1, source_target_pairs={{0,2},{2,4},{4,6},{6,8},{8,10},{10,12},{12,14},{14,16},{16,18},{18... | collective-permute-start | bytes 98312 | tf_op jit(solution)/shard_map/ppermute | solution.py:16
  179.7 1.9 collective-permute-start.12
  181.7 2.4 %collective-permute-start.13 = (f32[3,1,8192]{2,1,0:T(1,128)S(1)}, f32[3,1,8192]{2,1,0:T(1,128)S(1)}, u32[]{:S(2)}, u32[]{:S(2)}) collective-permute-start(f32[3,1,8192]{2,1,0:T(1,128)S(1)} %get-tuple-element.44), channel_id=1, source_target_pairs={{2,0},{4,2},{6,4},{8,6},{10,8},{12,10},{14,12},{16,14},{18,16},{20... | collective-permute-start | bytes 294920 | tf_op jit(solution)/shard_map/ppermute | solution.py:19
  184.2 2.6 %collective-permute-start.30 = (f32[34,1]{1,0:T(8,128)S(1)}, f32[34,1]{1,0:T(8,128)S(1)}, u32[]{:S(2)}, u32[]{:S(2)}) collective-permute-start(f32[34,1]{1,0:T(8,128)S(1)} %get-tuple-element.51), channel_id=1, source_target_pairs={{1,0},{3,2},{5,4},{7,6},{9,8},{11,10},{13,12},{15,14},{17,16},{19,... | collective-permute-start | bytes 416 | tf_op jit(solution)/shard_map/ppermute | solution.py:19
  188.1 5.3 %collective-permute-done.13 = f32[3,1,8192]{2,1,0:T(1,128)S(1)} collective-permute-done((f32[3,1,8192]{2,1,0:T(1,128)S(1)}, f32[3,1,8192]{2,1,0:T(1,128)S(1)}, u32[]{:S(2)}, u32[]{:S(2)}) %collective-permute-start.13) | collective-permute-done | bytes 98336 | tf_op jit(solution)/shard_map/ppermute | solution.py:19
  195.3 4.2 %collective-permute-start.15 = (f32[3,34,1]{2,1,0:T(8,128)S(1)}, f32[3,34,1]{2,1,0:T(8,128)S(1)}, u32[]{:S(2)}, u32[]{:S(2)}) collective-permute-start(f32[3,34,1]{2,1,0:T(8,128)S(1)} %get-tuple-element.38), channel_id=1, source_target_pairs={{1,0},{3,2},{5,4},{7,6},{9,8},{11,10},{13,12},{15,14},{17,16},{19,... | collective-permute-start | bytes 1232 | tf_op jit(solution)/shard_map/ppermute | solution.py:19
  199.5 3.5 %fusion.11 = f32[32,8192]{1,0:T(8,128)} fusion(f32[32,8192]{1,0:T(8,128)S(1)} %get-tuple-element.4, f32[34,1]{1,0:T(8,128)S(1)} %collective-permute-done.31, f32[1,8192]{1,0:T(1,128)S(1)} %collective-permute-done.28, f32[32,8192]{1,0:T(8,128)S(1)} %fusion.23, f32[1,8192]{1,0:T(1,128)S(1)} %collective-permute-done.29, ...), kind=kLoop, calls=%fused_computation.34 | loop fusion | flops 10223616 | bytes 5374496 | tf_op jit(solution)/shard_map/add | solution.py:90
  203.1 6.3 %concatenate.103 = f32[3,34,8194]{2,1,0:T(8,128)} concatenate(f32[3,34,1]{2,1,0:T(8,128)S(1)} %collective-permute-done.14, f32[3,34,8192]{2,1,0:T(8,128)} %copy-done.6, f32[3,34,1]{2,1,0:T(8,128)S(1)} %collective-permute-done.15), dimensions={2} | concatenate | bytes 6686304 | tf_op jit(solution)/shard_map/concatenate | solution.py:20
  209.4 2.4 %slice_bitcast_fusion.2 = (f32[34,8194]{1,0:T(8,128)S(1)}, f32[34,8194]{1,0:T(8,128)S(1)}, f32[34,8194]{1,0:T(8,128)S(1)}) fusion(f32[3,34,8194]{2,1,0:T(8,128)} %concatenate.103), kind=kLoop, calls=%fused_computation.12 | loop fusion | bytes 6686304 | tf_op jit(solution)/shard_map/squeeze | solution.py:72
  211.8 1.7 fusion.48
  213.5 1.6 fusion.1
  (83 shorter events, 21.1 us)
Async XLA Ops:
  0.6 2.2 %copy-start.10 = (f32[2,32,8192]{2,1,0:T(8,128)S(1)}, f32[2,32,8192]{2,1,0:T(8,128)}, u32[]{:S(2)}) copy-start(f32[2,32,8192]{2,1,0:T(8,128)} %param.6) | copy-start | bytes 6291460
  3.2 7.8 %collective-permute-start = (f32[4,1,8192]{2,1,0:T(1,128)S(1)}, f32[4,1,8192]{2,1,0:T(1,128)S(1)}, u32[]{:S(2)}, u32[]{:S(2)}) collective-permute-start(f32[4,1,8192]{2,1,0:T(1,128)S(1)} %get-tuple-element.30), channel_id=1, source_target_pairs={{0,2},{2,4},{4,6},{6,8},{8,10},{10,12},{12,14},{14,16},{16,18},{18... | collective-permute-start | bytes 393224 | tf_op jit(solution)/shard_map/ppermute | solution.py:16
  9.0 12.0 %collective-permute-start.1 = (f32[4,1,8192]{2,1,0:T(1,128)S(1)}, f32[4,1,8192]{2,1,0:T(1,128)S(1)}, u32[]{:S(2)}, u32[]{:S(2)}) collective-permute-start(f32[4,1,8192]{2,1,0:T(1,128)S(1)} %get-tuple-element.31), channel_id=1, source_target_pairs={{2,0},{4,2},{6,4},{8,6},{10,8},{12,10},{14,12},{16,14},{18,16},{20... | collective-permute-start | bytes 393224 | tf_op jit(solution)/shard_map/ppermute | solution.py:19
  21.8 2.4 %copy-start.2 = (f32[4,34,8192]{2,1,0:T(8,128)}, f32[4,34,8192]{2,1,0:T(8,128)S(1)}, u32[]{:S(2)}) copy-start(f32[4,34,8192]{2,1,0:T(8,128)S(1)} %pad_maximum_fusion) | copy-start | bytes 13369348
  24.2 5.3 %collective-permute-start.2 = (f32[4,34,1]{2,1,0:T(8,128)S(1)}, f32[4,34,1]{2,1,0:T(8,128)S(1)}, u32[]{:S(2)}, u32[]{:S(2)}) collective-permute-start(f32[4,34,1]{2,1,0:T(8,128)S(1)} %get-tuple-element.27), channel_id=1, source_target_pairs={{0,1},{2,3},{4,5},{6,7},{8,9},{10,11},{12,13},{14,15},{16,17},{18,... | collective-permute-start | bytes 1640 | tf_op jit(solution)/shard_map/ppermute | solution.py:16
  25.5 5.5 %collective-permute-start.3 = (f32[4,34,1]{2,1,0:T(8,128)S(1)}, f32[4,34,1]{2,1,0:T(8,128)S(1)}, u32[]{:S(2)}, u32[]{:S(2)}) collective-permute-start(f32[4,34,1]{2,1,0:T(8,128)S(1)} %get-tuple-element.26), channel_id=1, source_target_pairs={{1,0},{3,2},{5,4},{7,6},{9,8},{11,10},{13,12},{15,14},{17,16},{19,... | collective-permute-start | bytes 1640 | tf_op jit(solution)/shard_map/ppermute | solution.py:19
  39.0 3.0 %copy-start = (f32[32,8192]{1,0:T(8,128)S(1)}, f32[32,8192]{1,0:T(8,128)}, u32[]{:S(2)}) copy-start(f32[32,8192]{1,0:T(8,128)} %param.7) | copy-start | bytes 3145732
  45.9 4.9 %collective-permute-start.4 = (f32[3,1,8192]{2,1,0:T(1,128)S(1)}, f32[3,1,8192]{2,1,0:T(1,128)S(1)}, u32[]{:S(2)}, u32[]{:S(2)}) collective-permute-start(f32[3,1,8192]{2,1,0:T(1,128)S(1)} %get-tuple-element.45), channel_id=1, source_target_pairs={{0,2},{2,4},{4,6},{6,8},{8,10},{10,12},{12,14},{14,16},{16,18},{18... | collective-permute-start | bytes 294920 | tf_op jit(solution)/shard_map/ppermute | solution.py:16
  48.8 11.7 %collective-permute-start.5 = (f32[3,1,8192]{2,1,0:T(1,128)S(1)}, f32[3,1,8192]{2,1,0:T(1,128)S(1)}, u32[]{:S(2)}, u32[]{:S(2)}) collective-permute-start(f32[3,1,8192]{2,1,0:T(1,128)S(1)} %get-tuple-element.46), channel_id=1, source_target_pairs={{2,0},{4,2},{6,4},{8,6},{10,8},{12,10},{14,12},{16,14},{18,16},{20... | collective-permute-start | bytes 294920 | tf_op jit(solution)/shard_map/ppermute | solution.py:19
  61.0 2.0 copy-start.7
  63.0 17.7 %collective-permute-start.6 = (f32[3,34,1]{2,1,0:T(8,128)S(1)}, f32[3,34,1]{2,1,0:T(8,128)S(1)}, u32[]{:S(2)}, u32[]{:S(2)}) collective-permute-start(f32[3,34,1]{2,1,0:T(8,128)S(1)} %get-tuple-element.41), channel_id=1, source_target_pairs={{0,1},{2,3},{4,5},{6,7},{8,9},{10,11},{12,13},{14,15},{16,17},{18,... | collective-permute-start | bytes 1232 | tf_op jit(solution)/shard_map/ppermute | solution.py:16
  64.3 16.4 %collective-permute-start.7 = (f32[3,34,1]{2,1,0:T(8,128)S(1)}, f32[3,34,1]{2,1,0:T(8,128)S(1)}, u32[]{:S(2)}, u32[]{:S(2)}) collective-permute-start(f32[3,34,1]{2,1,0:T(8,128)S(1)} %get-tuple-element.40), channel_id=1, source_target_pairs={{1,0},{3,2},{5,4},{7,6},{9,8},{11,10},{13,12},{15,14},{17,16},{19,... | collective-permute-start | bytes 1232 | tf_op jit(solution)/shard_map/ppermute | solution.py:19
  69.4 29.6 %collective-permute-start.16 = (f32[1,8192]{1,0:T(1,128)S(1)}, f32[1,8192]{1,0:T(1,128)S(1)}, u32[]{:S(2)}, u32[]{:S(2)}) collective-permute-start(f32[1,8192]{1,0:T(1,128)S(1)} %get-tuple-element.64), channel_id=1, source_target_pairs={{2,0},{4,2},{6,4},{8,6},{10,8},{12,10},{14,12},{16,14},{18,16},{20... | collective-permute-start | bytes 98312 | tf_op jit(solution)/shard_map/ppermute | solution.py:19
  71.3 37.0 %collective-permute-start.18 = (f32[1,8192]{1,0:T(1,128)S(1)}, f32[1,8192]{1,0:T(1,128)S(1)}, u32[]{:S(2)}, u32[]{:S(2)}) collective-permute-start(f32[1,8192]{1,0:T(1,128)S(1)} %get-tuple-element.63), channel_id=1, source_target_pairs={{0,2},{2,4},{4,6},{6,8},{8,10},{10,12},{12,14},{14,16},{16,18},{18... | collective-permute-start | bytes 98312 | tf_op jit(solution)/shard_map/ppermute | solution.py:16
  89.4 1.7 copy-start.9
  89.4 2.2 %copy-start.11 = (f32[2,32,8192]{2,1,0:T(8,128)S(1)}, f32[2,32,8192]{2,1,0:T(8,128)}, u32[]{:S(2)}) copy-start(f32[2,32,8192]{2,1,0:T(8,128)} %param.6) | copy-start | bytes 6291460
  92.2 19.4 %copy-start.3 = (f32[2,32,8192]{2,1,0:T(8,128)}, f32[2,32,8192]{2,1,0:T(8,128)S(1)}, u32[]{:S(2)}) copy-start(f32[2,32,8192]{2,1,0:T(8,128)S(1)} %get-tuple-element.10) | copy-start | bytes 6291460
  92.2 16.2 %copy-start.4 = (f32[32,8192]{1,0:T(8,128)S(1)}, f32[32,8192]{1,0:T(8,128)}, u32[]{:S(2)}) copy-start(f32[32,8192]{1,0:T(8,128)} %param.9) | copy-start | bytes 3145732
  92.4 17.9 %collective-permute-start.8 = (f32[4,1,8192]{2,1,0:T(1,128)S(1)}, f32[4,1,8192]{2,1,0:T(1,128)S(1)}, u32[]{:S(2)}, u32[]{:S(2)}) collective-permute-start(f32[4,1,8192]{2,1,0:T(1,128)S(1)} %get-tuple-element.28), channel_id=1, source_target_pairs={{0,2},{2,4},{4,6},{6,8},{8,10},{10,12},{12,14},{14,16},{16,18},{18... | collective-permute-start | bytes 393224 | tf_op jit(solution)/shard_map/ppermute | solution.py:16
  94.6 17.0 %collective-permute-start.9 = (f32[4,1,8192]{2,1,0:T(1,128)S(1)}, f32[4,1,8192]{2,1,0:T(1,128)S(1)}, u32[]{:S(2)}, u32[]{:S(2)}) collective-permute-start(f32[4,1,8192]{2,1,0:T(1,128)S(1)} %get-tuple-element.29), channel_id=1, source_target_pairs={{2,0},{4,2},{6,4},{8,6},{10,8},{12,10},{14,12},{16,14},{18,16},{20... | collective-permute-start | bytes 393224 | tf_op jit(solution)/shard_map/ppermute | solution.py:19
  97.0 19.1 %collective-permute-start.17 = (f32[1,8192]{1,0:T(1,128)S(1)}, f32[1,8192]{1,0:T(1,128)S(1)}, u32[]{:S(2)}, u32[]{:S(2)}) collective-permute-start(f32[1,8192]{1,0:T(1,128)S(1)} %get-tuple-element.66), channel_id=1, source_target_pairs={{2,0},{4,2},{6,4},{8,6},{10,8},{12,10},{14,12},{16,14},{18,16},{20... | collective-permute-start | bytes 98312 | tf_op jit(solution)/shard_map/ppermute | solution.py:19
  99.0 21.2 %collective-permute-start.19 = (f32[1,8192]{1,0:T(1,128)S(1)}, f32[1,8192]{1,0:T(1,128)S(1)}, u32[]{:S(2)}, u32[]{:S(2)}) collective-permute-start(f32[1,8192]{1,0:T(1,128)S(1)} %get-tuple-element.65), channel_id=1, source_target_pairs={{0,2},{2,4},{4,6},{6,8},{8,10},{10,12},{12,14},{14,16},{16,18},{18... | collective-permute-start | bytes 98312 | tf_op jit(solution)/shard_map/ppermute | solution.py:16
  109.0 25.7 %collective-permute-start.20 = (f32[34,1]{1,0:T(8,128)}, f32[34,1]{1,0:T(8,128)S(1)}, u32[]{:S(2)}, u32[]{:S(2)}) collective-permute-start(f32[34,1]{1,0:T(8,128)} %get-tuple-element.56), channel_id=1, source_target_pairs={{1,0},{3,2},{5,4},{7,6},{9,8},{11,10},{13,12},{15,14},{17,16},{19,... | collective-permute-start | bytes 416 | tf_op jit(solution)/shard_map/ppermute | solution.py:19
  110.3 24.4 %collective-permute-start.22 = (f32[34,1]{1,0:T(8,128)S(1)}, f32[34,1]{1,0:T(8,128)S(1)}, u32[]{:S(2)}, u32[]{:S(2)}) collective-permute-start(f32[34,1]{1,0:T(8,128)S(1)} %get-tuple-element.55), channel_id=1, source_target_pairs={{0,1},{2,3},{4,5},{6,7},{8,9},{10,11},{12,13},{14,15},{16,17},{18,... | collective-permute-start | bytes 416 | tf_op jit(solution)/shard_map/ppermute | solution.py:16
  112.4 2.4 %copy-start.1 = (f32[4,34,8192]{2,1,0:T(8,128)}, f32[4,34,8192]{2,1,0:T(8,128)S(1)}, u32[]{:S(2)}) copy-start(f32[4,34,8192]{2,1,0:T(8,128)S(1)} %pad_maximum_fusion.1) | copy-start | bytes 13369348
  114.8 7.3 %collective-permute-start.10 = (f32[4,34,1]{2,1,0:T(8,128)S(1)}, f32[4,34,1]{2,1,0:T(8,128)S(1)}, u32[]{:S(2)}, u32[]{:S(2)}) collective-permute-start(f32[4,34,1]{2,1,0:T(8,128)S(1)} %get-tuple-element.25), channel_id=1, source_target_pairs={{0,1},{2,3},{4,5},{6,7},{8,9},{10,11},{12,13},{14,15},{16,17},{18,... | collective-permute-start | bytes 1640 | tf_op jit(solution)/shard_map/ppermute | solution.py:16
  116.2 7.5 %collective-permute-start.11 = (f32[4,34,1]{2,1,0:T(8,128)S(1)}, f32[4,34,1]{2,1,0:T(8,128)S(1)}, u32[]{:S(2)}, u32[]{:S(2)}) collective-permute-start(f32[4,34,1]{2,1,0:T(8,128)S(1)} %get-tuple-element.24), channel_id=1, source_target_pairs={{1,0},{3,2},{5,4},{7,6},{9,8},{11,10},{13,12},{15,14},{17,16},{19,... | collective-permute-start | bytes 1640 | tf_op jit(solution)/shard_map/ppermute | solution.py:19
  120.8 13.9 %collective-permute-start.21 = (f32[34,1]{1,0:T(8,128)}, f32[34,1]{1,0:T(8,128)S(1)}, u32[]{:S(2)}, u32[]{:S(2)}) collective-permute-start(f32[34,1]{1,0:T(8,128)} %get-tuple-element.57), channel_id=1, source_target_pairs={{1,0},{3,2},{5,4},{7,6},{9,8},{11,10},{13,12},{15,14},{17,16},{19,... | collective-permute-start | bytes 416 | tf_op jit(solution)/shard_map/ppermute | solution.py:19
  122.1 12.6 %collective-permute-start.23 = (f32[34,1]{1,0:T(8,128)}, f32[34,1]{1,0:T(8,128)S(1)}, u32[]{:S(2)}, u32[]{:S(2)}) collective-permute-start(f32[34,1]{1,0:T(8,128)} %get-tuple-element.58), channel_id=1, source_target_pairs={{0,1},{2,3},{4,5},{6,7},{8,9},{10,11},{12,13},{14,15},{16,17},{18,... | collective-permute-start | bytes 416 | tf_op jit(solution)/shard_map/ppermute | solution.py:16
  131.7 3.1 %copy-start.5 = (f32[32,8192]{1,0:T(8,128)S(1)}, f32[32,8192]{1,0:T(8,128)}, u32[]{:S(2)}) copy-start(f32[32,8192]{1,0:T(8,128)} %param.9) | copy-start | bytes 3145732
  131.7 3.1 %copy-start.12 = (f32[32,8192]{1,0:T(8,128)S(1)}, f32[32,8192]{1,0:T(8,128)}, u32[]{:S(2)}) copy-start(f32[32,8192]{1,0:T(8,128)} %param.8) | copy-start | bytes 3145732
  140.4 59.1 %copy-start.8 = (f32[32,8192]{1,0:T(8,128)}, f32[32,8192]{1,0:T(8,128)S(1)}, u32[]{:S(2)}) copy-start(f32[32,8192]{1,0:T(8,128)S(1)} %get-tuple-element.5) | copy-start | bytes 3145732
  140.5 16.4 %collective-permute-start.24 = (f32[1,8192]{1,0:T(1,128)S(1)}, f32[1,8192]{1,0:T(1,128)S(1)}, u32[]{:S(2)}, u32[]{:S(2)}) collective-permute-start(f32[1,8192]{1,0:T(1,128)S(1)} %get-tuple-element.62), channel_id=1, source_target_pairs={{2,0},{4,2},{6,4},{8,6},{10,8},{12,10},{14,12},{16,14},{18,16},{20... | collective-permute-start | bytes 98312 | tf_op jit(solution)/shard_map/ppermute | solution.py:19
  142.4 14.5 %collective-permute-start.25 = (f32[1,8192]{1,0:T(1,128)S(1)}, f32[1,8192]{1,0:T(1,128)S(1)}, u32[]{:S(2)}, u32[]{:S(2)}) collective-permute-start(f32[1,8192]{1,0:T(1,128)S(1)} %get-tuple-element.61), channel_id=1, source_target_pairs={{0,2},{2,4},{4,6},{6,8},{8,10},{10,12},{12,14},{14,16},{16,18},{18... | collective-permute-start | bytes 98312 | tf_op jit(solution)/shard_map/ppermute | solution.py:16
  157.0 7.1 %collective-permute-start.26 = (f32[34,1]{1,0:T(8,128)S(1)}, f32[34,1]{1,0:T(8,128)S(1)}, u32[]{:S(2)}, u32[]{:S(2)}) collective-permute-start(f32[34,1]{1,0:T(8,128)S(1)} %get-tuple-element.53), channel_id=1, source_target_pairs={{1,0},{3,2},{5,4},{7,6},{9,8},{11,10},{13,12},{15,14},{17,16},{19,... | collective-permute-start | bytes 416 | tf_op jit(solution)/shard_map/ppermute | solution.py:19
  161.0 4.5 %collective-permute-start.27 = (f32[34,1]{1,0:T(8,128)S(1)}, f32[34,1]{1,0:T(8,128)S(1)}, u32[]{:S(2)}, u32[]{:S(2)}) collective-permute-start(f32[34,1]{1,0:T(8,128)S(1)} %get-tuple-element.54), channel_id=1, source_target_pairs={{0,1},{2,3},{4,5},{6,7},{8,9},{10,11},{12,13},{14,15},{16,17},{18,... | collective-permute-start | bytes 416 | tf_op jit(solution)/shard_map/ppermute | solution.py:16
  168.3 15.8 %collective-permute-start.28 = (f32[1,8192]{1,0:T(1,128)S(1)}, f32[1,8192]{1,0:T(1,128)S(1)}, u32[]{:S(2)}, u32[]{:S(2)}) collective-permute-start(f32[1,8192]{1,0:T(1,128)S(1)} %get-tuple-element.60), channel_id=1, source_target_pairs={{2,0},{4,2},{6,4},{8,6},{10,8},{12,10},{14,12},{16,14},{18,16},{20... | collective-permute-start | bytes 98312 | tf_op jit(solution)/shard_map/ppermute | solution.py:19
  170.2 13.9 %collective-permute-start.29 = (f32[1,8192]{1,0:T(1,128)S(1)}, f32[1,8192]{1,0:T(1,128)S(1)}, u32[]{:S(2)}, u32[]{:S(2)}) collective-permute-start(f32[1,8192]{1,0:T(1,128)S(1)} %get-tuple-element.59), channel_id=1, source_target_pairs={{0,2},{2,4},{4,6},{6,8},{8,10},{10,12},{12,14},{14,16},{16,18},{18... | collective-permute-start | bytes 98312 | tf_op jit(solution)/shard_map/ppermute | solution.py:16
  179.7 8.3 %collective-permute-start.12 = (f32[3,1,8192]{2,1,0:T(1,128)S(1)}, f32[3,1,8192]{2,1,0:T(1,128)S(1)}, u32[]{:S(2)}, u32[]{:S(2)}) collective-permute-start(f32[3,1,8192]{2,1,0:T(1,128)S(1)} %get-tuple-element.43), channel_id=1, source_target_pairs={{0,2},{2,4},{4,6},{6,8},{8,10},{10,12},{12,14},{14,16},{16,18},{18... | collective-permute-start | bytes 294920 | tf_op jit(solution)/shard_map/ppermute | solution.py:16
  181.7 11.7 %collective-permute-start.13 = (f32[3,1,8192]{2,1,0:T(1,128)S(1)}, f32[3,1,8192]{2,1,0:T(1,128)S(1)}, u32[]{:S(2)}, u32[]{:S(2)}) collective-permute-start(f32[3,1,8192]{2,1,0:T(1,128)S(1)} %get-tuple-element.44), channel_id=1, source_target_pairs={{2,0},{4,2},{6,4},{8,6},{10,8},{12,10},{14,12},{16,14},{18,16},{20... | collective-permute-start | bytes 294920 | tf_op jit(solution)/shard_map/ppermute | solution.py:19
  184.2 15.3 %collective-permute-start.30 = (f32[34,1]{1,0:T(8,128)S(1)}, f32[34,1]{1,0:T(8,128)S(1)}, u32[]{:S(2)}, u32[]{:S(2)}) collective-permute-start(f32[34,1]{1,0:T(8,128)S(1)} %get-tuple-element.51), channel_id=1, source_target_pairs={{1,0},{3,2},{5,4},{7,6},{9,8},{11,10},{13,12},{15,14},{17,16},{19,... | collective-permute-start | bytes 416 | tf_op jit(solution)/shard_map/ppermute | solution.py:19
  186.8 12.7 %collective-permute-start.31 = (f32[34,1]{1,0:T(8,128)S(1)}, f32[34,1]{1,0:T(8,128)S(1)}, u32[]{:S(2)}, u32[]{:S(2)}) collective-permute-start(f32[34,1]{1,0:T(8,128)S(1)} %get-tuple-element.52), channel_id=1, source_target_pairs={{0,1},{2,3},{4,5},{6,7},{8,9},{10,11},{12,13},{14,15},{16,17},{18,... | collective-permute-start | bytes 416 | tf_op jit(solution)/shard_map/ppermute | solution.py:16
  193.9 9.2 %copy-start.6 = (f32[3,34,8192]{2,1,0:T(8,128)}, f32[3,34,8192]{2,1,0:T(8,128)S(1)}, u32[]{:S(2)}) copy-start(f32[3,34,8192]{2,1,0:T(8,128)S(1)} %pad_maximum_fusion.3) | copy-start | bytes 10027012
  194.0 9.1 %collective-permute-start.14 = (f32[3,34,1]{2,1,0:T(8,128)S(1)}, f32[3,34,1]{2,1,0:T(8,128)S(1)}, u32[]{:S(2)}, u32[]{:S(2)}) collective-permute-start(f32[3,34,1]{2,1,0:T(8,128)S(1)} %get-tuple-element.39), channel_id=1, source_target_pairs={{0,1},{2,3},{4,5},{6,7},{8,9},{10,11},{12,13},{14,15},{16,17},{18,... | collective-permute-start | bytes 1232 | tf_op jit(solution)/shard_map/ppermute | solution.py:16
  195.3 7.8 %collective-permute-start.15 = (f32[3,34,1]{2,1,0:T(8,128)S(1)}, f32[3,34,1]{2,1,0:T(8,128)S(1)}, u32[]{:S(2)}, u32[]{:S(2)}) collective-permute-start(f32[3,34,1]{2,1,0:T(8,128)S(1)} %get-tuple-element.38), channel_id=1, source_target_pairs={{1,0},{3,2},{5,4},{7,6},{9,8},{11,10},{13,12},{15,14},{17,16},{19,... | collective-permute-start | bytes 1232 | tf_op jit(solution)/shard_map/ppermute | solution.py:19
where the time goes:
time: 217 us; the launch traced here: 215 us
  starting transfers between devices  102 us (47%)
  local copies, waits for them, and re-layouts  50.8 us (23%)
  other arithmetic  32.5 us (15%)
  waiting for transfers between devices  28.1 us (13%)
    ppermute x16, starting transfers between devices, padded_2(): lax.ppermute(lax.slice_in_dim(block, block.shape[dim] - width, None, axis...  60.8 us
    ppermute x16, starting transfers between devices, padded_2(): lax.ppermute(lax.slice_in_dim(block, 0, width, axis=dim), axis, backward)  41.6 us
    concatenate x4, local copies, waits for them, and re-layouts, padded_2(): block = jnp.concatenate([low, block, high], axis=dim)  28.7 us
    ppermute x16, waiting for transfers between devices, padded_2(): lax.ppermute(lax.slice_in_dim(block, 0, width, axis=dim), axis, backward)  26.6 us
    another operation x4, other arithmetic, stress_of(): jnp.stack([degrade * (trace + 2.0 * exx), degrade * (trace + 2.0 * eyy),...  10.6 us
    unnamed x27, local copies, waits for them, and re-layouts  9.5 us
    div x1, other arithmetic, jacobi(): return jnp.where(True, numer / jnp.where(True, denom, 1.0), 0.0)  5.59 us
    squeeze x2, local copies, waits for them, and re-layouts, accel_of(): return (accel(sig[0], sig[1], sig[2]), eu)  4.76 us
  transfers between devices with their start and end apart: 32, of which 5 were waited for; matrix products, arithmetic and copies ran while one was open for 17% of the time, Pallas kernels for 0%

commit v1 on v0

v1 whole, which is shorter than its diff:
```python
import jax
import jax.numpy as jnp
from jax import lax
from jax.experimental import pallas as pl
from jax.experimental.pallas import tpu as pltpu
from jax.sharding import PartitionSpec as P

CHEB = 0.94
WEIGHT_TWO = 1.0 / (1.0 - CHEB * CHEB / 2.0)
WEIGHT_THREE = 1.0 / (1.0 - CHEB * CHEB * WEIGHT_TWO / 4.0)

RAD = 5
HR = 8
HC = 128
BW = 1024
INTERPRET = False


def roll_shift(x, d, axis):
    return pltpu.roll(x, (-d) % x.shape[axis], axis)


def jnp_shift(x, d, axis):
    return jnp.roll(x, -d, axis)


def step_fields(u0, u1, v0, v1, dmg, hist, tough, valid, sh):
    zero = jnp.zeros_like(dmg)

    def strain(first, second):
        exx = (sh(first, 1, 0) - sh(first, -1, 0)) * 0.5
        eyy = (sh(second, 1, 1) - sh(second, -1, 1)) * 0.5
        exy = ((sh(first, 1, 1) - sh(first, -1, 1)) + (sh(second, 1, 0) - sh(second, -1, 0))) * 0.25
        return exx, eyy, exy

    degrade = (1.0 - dmg) ** 2 + 0.001

    def accel(w0, w1, z0, z1):
        eu = strain(w0, w1)
        ev = strain(z0, z1)
        exx = eu[0] + 0.5 * ev[0]
        eyy = eu[1] + 0.5 * ev[1]
        exy = eu[2] + 0.5 * ev[2]
        trace = exx + eyy
        sxx = jnp.where(valid, degrade * (trace + 2.0 * exx), zero)
        syy = jnp.where(valid, degrade * (trace + 2.0 * eyy), zero)
        sxy = jnp.where(valid, degrade * 2.0 * exy, zero)
        a0 = ((sh(sxx, 1, 0) - sh(sxx, -1, 0)) + (sh(sxy, 1, 1) - sh(sxy, -1, 1))) * 0.5
        a1 = ((sh(sxy, 1, 0) - sh(sxy, -1, 0)) + (sh(syy, 1, 1) - sh(syy, -1, 1))) * 0.5
        return a0, a1

    a0, a1 = accel(u0, u1, v0, v1)
    h0 = jnp.where(valid, v0 + 0.1 * a0, zero)
    h1 = jnp.where(valid, v1 + 0.1 * a1, zero)
    n0 = jnp.where(valid, u0 + 0.2 * h0, zero)
    n1 = jnp.where(valid, u1 + 0.2 * h1, zero)
    b0, b1 = accel(n0, n1, h0, h1)
    vel0 = h0 + 0.1 * b0
    vel1 = h1 + 0.1 * b1
    e = strain(n0, n1)
    tr = jnp.maximum(e[0] + e[1], 0.0)
    hist_new = jnp.maximum(hist, 0.5 * tr * tr + e[0] * e[0] + e[1] * e[1] + 2.0 * e[2] * e[2])

    k_down = tough + sh(tough, 1, 0)
    k_up = tough + sh(tough, -1, 0)
    k_right = tough + sh(tough, 1, 1)
    k_left = tough + sh(tough, -1, 1)
    two_h = 2.0 * hist_new
    denom = tough * 0.5 + two_h + k_down + k_up + k_right + k_left

    def jacobi(f):
        numer = two_h + k_down * sh(f, 1, 0) + k_up * sh(f, -1, 0)
        numer = numer + k_right * sh(f, 1, 1) + k_left * sh(f, -1, 1)
        return numer / denom

    d1 = jnp.where(valid, jacobi(dmg), zero)
    d2 = jnp.where(valid, dmg + WEIGHT_TWO * (jacobi(d1) - dmg), zero)
    d3 = d1 + WEIGHT_THREE * (jacobi(d2) - d1)
    return n0, n1, vel0, vel1, hist_new, d3


def exchange(fields):
    rows, cols = fields[0].shape
    nf = len(fields)
    iy = lax.axis_index("gy")
    ny = lax.axis_size("gy")
    nx = lax.axis_size("gx")
    left = jnp.stack([f[:, :RAD] for f in fields])
    right = jnp.stack([f[:, cols - RAD:] for f in fields])
    if ny == 2:
        got = lax.ppermute(jnp.where(iy == 0, right, left), "gy", [(0, 1), (1, 0)])
        from_left = jnp.where(iy == 1, got, 0.0)
        from_right = jnp.where(iy == 0, got, 0.0)
    else:
        from_left = lax.ppermute(right, "gy", [(i, i + 1) for i in range(ny - 1)])
        from_right = lax.ppermute(left, "gy", [(i + 1, i) for i in range(ny - 1)])
    left_block = jnp.pad(from_left, ((0, 0), (0, 0), (HC - RAD, 0)))
    right_block = jnp.pad(from_right, ((0, 0), (0, 0), (0, HC - RAD)))

    def ext_rows(lo, hi):
        mid = jnp.stack([f[lo:hi] for f in fields])
        return jnp.concatenate([left_block[:, lo:hi], mid, right_block[:, lo:hi]], axis=2)

    top = ext_rows(0, RAD)
    bottom = ext_rows(rows - RAD, rows)
    from_above = lax.ppermute(bottom, "gx", [(i, i + 1) for i in range(nx - 1)])
    from_below = lax.ppermute(top, "gx", [(i + 1, i) for i in range(nx - 1)])
    gap = jnp.zeros((HR - RAD, cols + 2 * HC), fields[0].dtype)
    out = []
    for k in range(nf):
        core = jnp.concatenate([left_block[k], fields[k], right_block[k]], axis=1)
        out.append(jnp.concatenate([gap, from_above[k], core, from_below[k], gap], axis=0))
    return out


def on_device(displacement, velocity, damage, history, toughness):
    rows, cols = damage.shape
    nx = lax.axis_size("gx")
    ny = lax.axis_size("gy")
    ix = lax.axis_index("gx")
    iy = lax.axis_index("gy")
    total_rows, total_cols = rows * nx, cols * ny
    fields = [displacement[0], displacement[1], velocity[0], velocity[1], damage, history, toughness]
    ext = exchange(fields)
    eu = jnp.stack(ext[0:2])
    ev = jnp.stack(ext[2:4])
    ed, eh, et = ext[4], ext[5], ext[6]
    ext_rows = rows + 2 * HR
    pos = jnp.stack([ix, iy]).astype(jnp.int32)
    nblocks = cols // BW
    extra = 2 * HC

    def kernel(pos_ref, um, ue, vm, ve, dm, de, hm, he, tm, te, uo, vo, ho, do):
        j = pl.program_id(0)

        def cat(a, b):
            return jnp.concatenate([a, b], axis=-1)

        u0 = cat(um[0], ue[0])
        u1 = cat(um[1], ue[1])
        v0 = cat(vm[0], ve[0])
        v1 = cat(vm[1], ve[1])
        d = cat(dm[...], de[...])
        h = cat(hm[...], he[...])
        t = cat(tm[...], te[...])
        shape = d.shape
        grow = lax.broadcasted_iota(jnp.int32, shape, 0) + (pos_ref[0] * rows - HR)
        gcol = lax.broadcasted_iota(jnp.int32, shape, 1) + (pos_ref[1] * cols + j * BW - HC)
        valid = (grow >= 0) & (grow < total_rows) & (gcol >= 0) & (gcol < total_cols)
        sh = jnp_shift if INTERPRET else roll_shift
        n0, n1, w0, w1, hn, d3 = step_fields(u0, u1, v0, v1, d, h, t, valid, sh)

        def core(x):
            return x[HR:HR + rows, HC:HC + BW]

        uo[0] = core(n0)
        uo[1] = core(n1)
        vo[0] = core(w0)
        vo[1] = core(w1)
        ho[...] = core(hn)
        do[...] = core(d3)

    main2 = pl.BlockSpec((2, ext_rows, BW), lambda j: (0, 0, j))
    extra2 = pl.BlockSpec((2, ext_rows, extra), lambda j: (0, 0, (j + 1) * (BW // extra)))
    main1 = pl.BlockSpec((ext_rows, BW), lambda j: (0, j))
    extra1 = pl.BlockSpec((ext_rows, extra), lambda j: (0, (j + 1) * (BW // extra)))
    out2 = pl.BlockSpec((2, rows, BW), lambda j: (0, 0, j))
    out1 = pl.BlockSpec((rows, BW), lambda j: (0, j))
    f32 = damage.dtype
    outs = pl.pallas_call(
        kernel,
        grid=(nblocks,),
        in_specs=[pl.BlockSpec(memory_space=pltpu.SMEM), main2, extra2, main2, extra2,
                  main1, extra1, main1, extra1, main1, extra1],
        out_specs=[out2, out2, out1, out1],
        out_shape=[jax.ShapeDtypeStruct((2, rows, cols), f32), jax.ShapeDtypeStruct((2, rows, cols), f32),
                   jax.ShapeDtypeStruct((rows, cols), f32), jax.ShapeDtypeStruct((rows, cols), f32)],
        interpret=INTERPRET,
    )(pos, eu, eu, ev, ev, ed, ed, eh, eh, et, et)
    return tuple(outs)


def solution(mesh):
    placed = (P(None, "gx", "gy"), P(None, "gx", "gy"), P("gx", "gy"), P("gx", "gy"), P("gx", "gy"))
    return jax.shard_map(
        on_device,
        mesh=mesh,
        in_specs=placed,
        out_specs=(P(None, "gx", "gy"), P(None, "gx", "gy"), P("gx", "gy"), P("gx", "gy")),
        check_vma=False,
    )
```

time: 217 us -> 148 us (0.68)
  the two profiles are of different devices: /device:TPU:127 before, /device:TPU:89 now
where the time goes in v1:
time: 148 us; the launch traced here: 147 us
  local copies, waits for them, and re-layouts  77.3 us (52%)
  Pallas kernels  26.7 us (18%)
  waiting for transfers between devices  21.4 us (14%)
  other arithmetic  11.5 us (8%)
  starting transfers between devices  8.64 us (6%)
    concatenate x7, local copies, waits for them, and re-layouts, exchange(): jnp.concatenate([gap, from_above[k], core, from_below[k], gap], axis=0)  35.7 us
    pallas_call x1, Pallas kernels, on_device(): pl.pallas_call(kernel, grid=(nblocks,), in_specs=[pl.BlockSpec(memory_spa...  26.7 us
    ppermute x1, waiting for transfers between devices, exchange(): from_below = lax.ppermute(top, 'gx', [(i + 1, i) for i in range(nx - 1)])  21.3 us
    unnamed x74, local copies, waits for them, and re-layouts  16.3 us
    another operation x8, local copies, waits for them, and re-layouts, ext_rows(): mid = jnp.stack([f[lo:hi] for f in fields])  12 us
    slice x5, local copies, waits for them, and re-layouts, ext_rows(): mid = jnp.stack([f[lo:hi] for f in fields])  6.77 us
    concatenate x4, other arithmetic, exchange(): core = jnp.concatenate([left_block[k], fields[k], right_block[k]], axis=1)  5.25 us
    ppermute x1, starting transfers between devices, exchange(): from_above = lax.ppermute(bottom, 'gx', [(i, i + 1) for i in range(nx - 1)])  4.44 us
  transfers between devices with their start and end apart: 3, of which 1 were waited for; matrix products, arithmetic and copies ran while one was open for 21% of the time, Pallas kernels for 0%

profile of v1, /device:TPU:89, one launch (start us, length us, event | category | flops | bytes accessed | tf_op | source)
XLA Modules:
  0.0 146.7 jit_solution(1569528753092675674)
XLA Ops:
  0.6 2.8 %slice_bitcast_fusion.2 = (f32[32,8192]{1,0:T(8,128)}, f32[32,8192]{1,0:T(8,128)S(1)}) fusion(f32[2,32,8192]{2,1,0:T(8,128)} %param.5), kind=kLoop, calls=%fused_computation.13 | loop fusion | bytes 4194304 | tf_op jit(solution)/shard_map/squeeze | solution.py:123
  3.4 1.0 copy-done.6
  4.5 1.1 slice_bitcast_fusion
  5.6 0.9 constant_dynamic-update-slice_fusion.12
  6.5 0.8 constant_dynamic-update-slice_fusion.11
  7.3 0.8 constant_dynamic-update-slice_fusion.9
  8.2 0.8 constant_dynamic-update-slice_fusion.8
  9.0 0.8 constant_dynamic-update-slice_fusion.7
  10.4 1.2 collective-permute-start
  11.6 2.0 %fusion.20 = (f32[5,8192]{1,0:T(8,128)}, f32[5,8192]{1,0:T(8,128)}) fusion(f32[32,8192]{1,0:T(8,128)} %param.7), kind=kLoop, calls=%fused_computation.93 | loop fusion | bytes 655360 | tf_op jit(solution)/shard_map/slice | solution.py:101
  13.7 1.9 %fusion.19 = (f32[5,8192]{1,0:T(8,128)}, f32[5,8192]{1,0:T(8,128)}) fusion(f32[32,8192]{1,0:T(8,128)} %param.8), kind=kLoop, calls=%fused_computation.92 | loop fusion | bytes 655360 | tf_op jit(solution)/shard_map/slice | solution.py:101
  15.5 1.8 %fusion.18 = (f32[5,8192]{1,0:T(8,128)}, f32[5,8192]{1,0:T(8,128)S(1)}) fusion(f32[32,8192]{1,0:T(8,128)} %param.9), kind=kLoop, calls=%fused_computation.91 | loop fusion | bytes 655360 | tf_op jit(solution)/shard_map/slice | solution.py:101
  17.3 1.1 fusion.15
  19.1 1.7 %stack.132 = f32[1,5,8192]{2,0,1:T(1,128)} reshape(f32[5,8192]{1,0:T(8,128)} %get-tuple-element.30) | data formatting | bytes 327680 | tf_op jit(solution)/shard_map/stack | solution.py:101
  20.8 1.7 %stack.128 = f32[1,5,8192]{2,0,1:T(1,128)} reshape(f32[5,8192]{1,0:T(8,128)} %get-tuple-element.31) | data formatting | bytes 327680 | tf_op jit(solution)/shard_map/stack | solution.py:101
  22.6 1.8 %stack.133 = f32[1,5,8192]{2,0,1:T(1,128)} reshape(f32[5,8192]{1,0:T(8,128)} %get-tuple-element.28) | data formatting | bytes 327680 | tf_op jit(solution)/shard_map/stack | solution.py:101
  24.4 0.8 stack.129
  25.2 0.8 stack.134
  26.0 0.8 stack.130
  28.1 1.3 stack.135
  29.4 3.1 %stack.131 = f32[7,5,8192]{2,0,1:T(8,128)S(1)} concatenate(f32[2,5,8192]{2,0,1:T(2,128)S(1)} %copy.69, f32[2,5,8192]{2,0,1:T(2,128)S(1)} %copy.70, f32[1,5,8192]{2,0,1:T(1,128)S(1)} %copy-done.21, f32[1,5,8192]{2,0,1:T(1,128)} %stack.129, f32[1,5,8192]{2,0,1:T(1,128)} %stack.130), dimensions={0} | concatenate | bytes 2293760 | tf_op jit(solution)/shard_map/stack | solution.py:101
  32.5 0.9 broadcast_select_fusion.1
  33.8 3.0 %collective-permute-start.2 = (f32[7,5,8448]{2,0,1:T(8,128)S(1)}, f32[7,5,8448]{2,0,1:T(8,128)S(1)}, u32[]{:S(2)}, u32[]{:S(2)}) collective-permute-start(f32[7,5,8448]{2,0,1:T(8,128)S(1)} %pad_maximum_fusion.3), channel_id=1, source_target_pairs={{2,0},{4,2},{6,4},{8,6},{10,8},{12,10},{14,12},{16,14},{18,16},{20... | collective-permute-start | bytes 3548168 | tf_op jit(solution)/shard_map/ppermute | solution.py:107
  37.0 4.4 %collective-permute-start.1 = (f32[7,5,8448]{2,0,1:T(8,128)S(1)}, f32[7,5,8448]{2,0,1:T(8,128)S(1)}, u32[]{:S(2)}, u32[]{:S(2)}) collective-permute-start(f32[7,5,8448]{2,0,1:T(8,128)S(1)} %pad_maximum_fusion.2), channel_id=1, source_target_pairs={{0,2},{2,4},{4,6},{6,8},{8,10},{10,12},{12,14},{14,16},{16,18},{18... | collective-permute-start | bytes 3548168 | tf_op jit(solution)/shard_map/ppermute | solution.py:106
  41.4 1.5 %pad_maximum_fusion.4 = (f32[32,8448]{1,0:T(8,128)}, f32[32,8448]{1,0:T(8,128)}) fusion(f32[32,128]{1,0:T(8,128)S(1)} %get-tuple-element.54, f32[32,8192]{1,0:T(8,128)S(1)} %copy-done.7, f32[32,128]{1,0:T(8,128)S(1)} %get-tuple-element.47, f32[32,128]{1,0:T(8,128)S(1)} %get-tuple-element.55, f32[32,8192]{1,0:T(8,128)S(1)} %copy-done.5, ...), kind=kLoop, calls=%fused_computation.4 | loop fusion | flops 1081344 | bytes 4325376 | tf_op jit(solution)/shard_map/concatenate | solution.py:111
  43.0 0.8 copy-done.4
  43.7 1.2 pad_maximum_fusion.6
  45.3 1.1 pad_maximum_fusion.10
  46.8 1.6 %pad_maximum_fusion.8 = (f32[32,8448]{1,0:T(8,128)}, f32[32,8448]{1,0:T(8,128)}) fusion(f32[32,128]{1,0:T(8,128)S(1)} %get-tuple-element.58, f32[32,8192]{1,0:T(8,128)S(1)} %copy-done.11, f32[32,128]{1,0:T(8,128)S(1)} %get-tuple-element.51, f32[32,128]{1,0:T(8,128)S(1)} %get-tuple-element.59, f32[32,8192]{1,0:T(8,128)S(1)} %copy-done.12, ...), kind=kLoop, calls=%fused_computation.8 | loop fusion | flops 1081344 | bytes 4325376 | tf_op jit(solution)/shard_map/concatenate | solution.py:111
  48.3 21.3 %collective-permute-done.2 = f32[7,5,8448]{2,0,1:T(8,128)S(1)} collective-permute-done((f32[7,5,8448]{2,0,1:T(8,128)S(1)}, f32[7,5,8448]{2,0,1:T(8,128)S(1)}, u32[]{:S(2)}, u32[]{:S(2)}) %collective-permute-start.2) | collective-permute-done | bytes 1182752 | tf_op jit(solution)/shard_map/ppermute | solution.py:107
  69.7 0.8 fusion.16
  70.5 0.8 copy.101
  71.2 0.7 copy.103
  72.0 0.7 copy.105
  73.5 0.7 copy.111
  75.0 0.8 fusion.17
  76.5 0.7 copy.104
  78.0 0.7 copy.110
  78.8 0.7 copy.112
  80.9 5.9 %concatenate.55 = f32[48,8448]{1,0:T(8,128)S(1)} concatenate(f32[3,8448]{1,0:T(4,128)S(1)} %broadcast_in_dim.8, f32[5,8448]{1,0:T(8,128)} %bitcast.144, f32[32,8448]{1,0:T(8,128)} %get-tuple-element.68, f32[5,8448]{1,0:T(8,128)} %bitcast.138, f32[3,8448]{1,0:T(4,128)S(1)} %broadcast_in_dim.8), dimensions={0} | concatenate | bytes 3244032 | tf_op jit(solution)/shard_map/concatenate | solution.py:112
  86.8 1.9 %pad_maximum_fusion.1.vm.ve = f32[2,48,8448]{2,1,0:T(8,128)} fusion(f32[1,48,8448]{2,1,0:T(8,128)S(1)} %bitcast.128, f32[1,48,8448]{2,1,0:T(8,128)S(1)} %bitcast.130), kind=kLoop, calls=%fused_computation.1 | loop fusion | flops 811008 | bytes 6488064 | tf_op jit(solution)/shard_map/stack | solution.py:126
  88.7 5.9 %concatenate.53 = f32[48,8448]{1,0:T(8,128)S(1)} concatenate(f32[3,8448]{1,0:T(4,128)S(1)} %broadcast_in_dim.8, f32[5,8448]{1,0:T(8,128)} %bitcast.143, f32[32,8448]{1,0:T(8,128)} %get-tuple-element.67, f32[5,8448]{1,0:T(8,128)} %bitcast.137, f32[3,8448]{1,0:T(4,128)S(1)} %broadcast_in_dim.8), dimensions={0} | concatenate | bytes 3244032 | tf_op jit(solution)/shard_map/concatenate | solution.py:112
  94.6 5.9 %concatenate.51 = f32[48,8448]{1,0:T(8,128)S(1)} concatenate(f32[3,8448]{1,0:T(4,128)S(1)} %broadcast_in_dim.8, f32[5,8448]{1,0:T(8,128)} %bitcast.142, f32[32,8448]{1,0:T(8,128)} %get-tuple-element.66, f32[5,8448]{1,0:T(8,128)} %bitcast.135, f32[3,8448]{1,0:T(4,128)S(1)} %broadcast_in_dim.8), dimensions={0} | concatenate | bytes 3244032 | tf_op jit(solution)/shard_map/concatenate | solution.py:112
  100.5 1.9 %pad_maximum_fusion.um.ue = f32[2,48,8448]{2,1,0:T(8,128)} fusion(f32[1,48,8448]{2,1,0:T(8,128)S(1)} %bitcast.129, f32[1,48,8448]{2,1,0:T(8,128)S(1)} %bitcast.131), kind=kLoop, calls=%fused_computation | loop fusion | flops 811008 | bytes 6488064 | tf_op jit(solution)/shard_map/stack | solution.py:125
  102.4 8.6 %concatenate.63.tm.te = f32[48,8448]{1,0:T(8,128)} concatenate(f32[3,8448]{1,0:T(4,128)S(1)} %broadcast_in_dim.8, f32[5,8448]{1,0:T(8,128)} %bitcast.139, f32[32,8448]{1,0:T(8,128)} %pad_maximum_fusion.10, f32[5,8448]{1,0:T(8,128)} %bitcast.133, f32[3,8448]{1,0:T(4,128)S(1)} %broadcast_in_dim.8), dimensions={0} | concatenate | bytes 3244032 | tf_op jit(solution)/shard_map/concatenate | solution.py:112
  111.1 4.4 %concatenate.59.dm.de = f32[48,8448]{1,0:T(8,128)} concatenate(f32[3,8448]{1,0:T(4,128)S(1)} %broadcast_in_dim.8, f32[5,8448]{1,0:T(8,128)S(1)} %bitcast.140, f32[32,8448]{1,0:T(8,128)S(1)} %copy-done.9, f32[5,8448]{1,0:T(8,128)S(1)} %bitcast.134, f32[3,8448]{1,0:T(4,128)S(1)} %broadcast_in_dim.8), dimensions={0} | concatenate | bytes 3244032 | tf_op jit(solution)/shard_map/concatenate | solution.py:112
  115.5 4.3 %concatenate.61.hm.he = f32[48,8448]{1,0:T(8,128)} concatenate(f32[3,8448]{1,0:T(4,128)S(1)} %broadcast_in_dim.8, f32[5,8448]{1,0:T(8,128)S(1)} %bitcast.136, f32[32,8448]{1,0:T(8,128)S(1)} %copy-done.8, f32[5,8448]{1,0:T(8,128)S(1)} %bitcast.132, f32[3,8448]{1,0:T(4,128)S(1)} %broadcast_in_dim.8), dimensions={0} | concatenate | bytes 3244032 | tf_op jit(solution)/shard_map/concatenate | solution.py:112
  119.8 26.7 %shard_map.84 = (f32[2,32,8192]{2,1,0:T(8,128)}, f32[2,32,8192]{2,1,0:T(8,128)}, f32[32,8192]{1,0:T(8,128)}, f32[32,8192]{1,0:T(8,128)}) custom-call(s32[2]{0:T(128)} %pad_add_fusion.pos_ref, f32[2,48,8448]{2,1,0:T(8,128)} %pad_maximum_fusion.um.ue, f32[2,48,8448]{2,1,0:T(8,128)} %pad_maximum_fusion.um.ue, f32[2,48,8448]{2,1,0:T(8,128)} %pad_maximum_fusion.1.vm.ve, ...), custom_call_target="tpu_custom_call" | custom-call | tf_op jit(solution)/shard_map/pallas_call | solution.py:170
  (77 shorter events, 8.6 us)
Async XLA Ops:
  0.6 3.9 %copy-start.1 = (f32[2,32,8192]{2,1,0:T(8,128)S(1)}, f32[2,32,8192]{2,1,0:T(8,128)}, u32[]{:S(2)}) copy-start(f32[2,32,8192]{2,1,0:T(8,128)} %param.6) | copy-start | bytes 6291460
  3.4 1.0 copy-start.6
  5.6 9.9 %copy-start.2 = (f32[32,8192]{1,0:T(8,128)}, f32[32,8192]{1,0:T(8,128)S(1)}, u32[]{:S(2)}) copy-start(f32[32,8192]{1,0:T(8,128)S(1)} %get-tuple-element.8) | copy-start | bytes 3145732
  10.4 22.0 %collective-permute-start = (f32[7,32,5]{2,1,0:T(8,128)}, f32[7,32,5]{2,1,0:T(8,128)}, u32[]{:S(2)}, u32[]{:S(2)}) collective-permute-start(f32[7,32,5]{2,1,0:T(8,128)} %broadcast_select_fusion.2), channel_id=1, source_target_pairs={{0,1},{1,0},{2,3},{3,2},{4,5},{5,4},{6,7},{7,6},{8,9},{9,8},{10,11... | collective-permute-start | bytes 13448 | tf_op jit(solution)/shard_map/ppermute | solution.py:91
  11.6 5.7 %copy-start = (f32[2,32,8192]{2,1,0:T(8,128)S(1)}, f32[2,32,8192]{2,1,0:T(8,128)}, u32[]{:S(2)}) copy-start(f32[2,32,8192]{2,1,0:T(8,128)} %param.5) | copy-start | bytes 6291460
  18.4 6.0 %copy-start.20 = (f32[5,8192]{1,0:T(8,128)S(1)}, f32[5,8192]{1,0:T(8,128)}, u32[]{:S(2)}) copy-start(f32[5,8192]{1,0:T(8,128)} %get-tuple-element.29) | copy-start | bytes 491524
  18.4 6.7 %copy-start.19 = (f32[5,8192]{1,0:T(8,128)S(1)}, f32[5,8192]{1,0:T(8,128)}, u32[]{:S(2)}) copy-start(f32[5,8192]{1,0:T(8,128)} %get-tuple-element.26) | copy-start | bytes 491524
  18.4 8.3 %copy-start.14 = (f32[2,5,8192]{2,1,0:T(8,128)S(1)}, f32[2,5,8192]{2,1,0:T(8,128)}, u32[]{:S(2)}) copy-start(f32[2,5,8192]{2,1,0:T(8,128)} %get-tuple-element.6) | copy-start | bytes 983044
  22.6 4.4 %copy-start.13 = (f32[2,5,8192]{2,1,0:T(8,128)S(1)}, f32[2,5,8192]{2,1,0:T(8,128)}, u32[]{:S(2)}) copy-start(f32[2,5,8192]{2,1,0:T(8,128)} %get-tuple-element.7) | copy-start | bytes 983044
  27.0 0.9 copy-start.22
  27.0 1.0 copy-start.23
  27.0 1.1 copy-start.24
  28.1 1.3 copy-start.21
  33.8 7.6 %copy-start.5 = (f32[32,8192]{1,0:T(8,128)S(1)}, f32[32,8192]{1,0:T(8,128)}, u32[]{:S(2)}) copy-start(f32[32,8192]{1,0:T(8,128)} %get-tuple-element.10) | copy-start | bytes 3145732
  33.8 7.6 %copy-start.7 = (f32[32,8192]{1,0:T(8,128)S(1)}, f32[32,8192]{1,0:T(8,128)}, u32[]{:S(2)}) copy-start(f32[32,8192]{1,0:T(8,128)} %copy-done.6) | copy-start | bytes 3145732
  33.8 35.8 %collective-permute-start.2 = (f32[7,5,8448]{2,0,1:T(8,128)S(1)}, f32[7,5,8448]{2,0,1:T(8,128)S(1)}, u32[]{:S(2)}, u32[]{:S(2)}) collective-permute-start(f32[7,5,8448]{2,0,1:T(8,128)S(1)} %pad_maximum_fusion.3), channel_id=1, source_target_pairs={{2,0},{4,2},{6,4},{8,6},{10,8},{12,10},{14,12},{16,14},{18,16},{20... | collective-permute-start | bytes 3548168 | tf_op jit(solution)/shard_map/ppermute | solution.py:107
  37.0 38.0 %collective-permute-start.1 = (f32[7,5,8448]{2,0,1:T(8,128)S(1)}, f32[7,5,8448]{2,0,1:T(8,128)S(1)}, u32[]{:S(2)}, u32[]{:S(2)}) collective-permute-start(f32[7,5,8448]{2,0,1:T(8,128)S(1)} %pad_maximum_fusion.2), channel_id=1, source_target_pairs={{0,2},{2,4},{4,6},{6,8},{8,10},{10,12},{12,14},{14,16},{16,18},{18... | collective-permute-start | bytes 3548168 | tf_op jit(solution)/shard_map/ppermute | solution.py:106
  41.4 1.6 %copy-start.3 = (f32[32,8192]{1,0:T(8,128)S(1)}, f32[32,8192]{1,0:T(8,128)}, u32[]{:S(2)}) copy-start(f32[32,8192]{1,0:T(8,128)} %copy-done.2) | copy-start | bytes 3145732
  41.4 2.3 %copy-start.4 = (f32[32,8192]{1,0:T(8,128)S(1)}, f32[32,8192]{1,0:T(8,128)}, u32[]{:S(2)}) copy-start(f32[32,8192]{1,0:T(8,128)} %get-tuple-element.9) | copy-start | bytes 3145732
  43.7 1.6 %copy-start.10 = (f32[32,8192]{1,0:T(8,128)S(1)}, f32[32,8192]{1,0:T(8,128)}, u32[]{:S(2)}) copy-start(f32[32,8192]{1,0:T(8,128)} %param.9) | copy-start | bytes 3145732
  44.9 1.5 %copy-start.11 = (f32[32,8192]{1,0:T(8,128)S(1)}, f32[32,8192]{1,0:T(8,128)}, u32[]{:S(2)}) copy-start(f32[32,8192]{1,0:T(8,128)} %param.7) | copy-start | bytes 3145732
  44.9 1.9 %copy-start.12 = (f32[32,8192]{1,0:T(8,128)S(1)}, f32[32,8192]{1,0:T(8,128)}, u32[]{:S(2)}) copy-start(f32[32,8192]{1,0:T(8,128)} %param.8) | copy-start | bytes 3145732
  102.4 8.6 %copy-start.9 = (f32[32,8448]{1,0:T(8,128)S(1)}, f32[32,8448]{1,0:T(8,128)}, u32[]{:S(2)}) copy-start(f32[32,8448]{1,0:T(8,128)} %get-tuple-element.72) | copy-start | bytes 3244036
  102.4 8.6 %copy-start.16 = (f32[1,5,8448]{2,1,0:T(8,128)S(1)}, f32[1,5,8448]{2,1,0:T(8,128)}, u32[]{:S(2)}) copy-start(f32[1,5,8448]{2,1,0:T(8,128)} %copy.105) | copy-start | bytes 506884
  102.4 8.6 %copy-start.18 = (f32[1,5,8448]{2,1,0:T(8,128)S(1)}, f32[1,5,8448]{2,1,0:T(8,128)}, u32[]{:S(2)}) copy-start(f32[1,5,8448]{2,1,0:T(8,128)} %copy.106) | copy-start | bytes 506884
  111.1 4.4 %copy-start.8 = (f32[32,8448]{1,0:T(8,128)S(1)}, f32[32,8448]{1,0:T(8,128)}, u32[]{:S(2)}) copy-start(f32[32,8448]{1,0:T(8,128)} %get-tuple-element.73) | copy-start | bytes 3244036
  111.1 4.4 %copy-start.15 = (f32[1,5,8448]{2,1,0:T(8,128)S(1)}, f32[1,5,8448]{2,1,0:T(8,128)}, u32[]{:S(2)}) copy-start(f32[1,5,8448]{2,1,0:T(8,128)} %copy.103) | copy-start | bytes 506884
  111.1 4.4 %copy-start.17 = (f32[1,5,8448]{2,1,0:T(8,128)S(1)}, f32[1,5,8448]{2,1,0:T(8,128)}, u32[]{:S(2)}) copy-start(f32[1,5,8448]{2,1,0:T(8,128)} %copy.104) | copy-start | bytes 506884

commit v2 on v1

--- a/solution.py
+++ b/solution.py
@@ -81,7 +81,6 @@
 
 def exchange(fields):
     rows, cols = fields[0].shape
-    nf = len(fields)
     iy = lax.axis_index("gy")
     ny = lax.axis_size("gy")
     nx = lax.axis_size("gx")
@@ -105,12 +104,9 @@
     bottom = ext_rows(rows - RAD, rows)
     from_above = lax.ppermute(bottom, "gx", [(i, i + 1) for i in range(nx - 1)])
     from_below = lax.ppermute(top, "gx", [(i + 1, i) for i in range(nx - 1)])
-    gap = jnp.zeros((HR - RAD, cols + 2 * HC), fields[0].dtype)
-    out = []
-    for k in range(nf):
-        core = jnp.concatenate([left_block[k], fields[k], right_block[k]], axis=1)
-        out.append(jnp.concatenate([gap, from_above[k], core, from_below[k], gap], axis=0))
-    return out
+    above = jnp.pad(from_above, ((0, 0), (HR - RAD, 0), (0, 0)))
+    below = jnp.pad(from_below, ((0, 0), (0, HR - RAD), (0, 0)))
+    return left_block, right_block, above, below
 
 
 def on_device(displacement, velocity, damage, history, toughness):
@@ -121,28 +117,35 @@
     iy = lax.axis_index("gy")
     total_rows, total_cols = rows * nx, cols * ny
     fields = [displacement[0], displacement[1], velocity[0], velocity[1], damage, history, toughness]
-    ext = exchange(fields)
-    eu = jnp.stack(ext[0:2])
-    ev = jnp.stack(ext[2:4])
-    ed, eh, et = ext[4], ext[5], ext[6]
-    ext_rows = rows + 2 * HR
+    nf = len(fields)
+    col_left, col_right, above, below = exchange(fields)
     pos = jnp.stack([ix, iy]).astype(jnp.int32)
     nblocks = cols // BW
+    per = BW // HC
+    last_col_block = cols // HC - 1
     extra = 2 * HC
 
-    def kernel(pos_ref, um, ue, vm, ve, dm, de, hm, he, tm, te, uo, vo, ho, do):
+    def kernel(pos_ref, um, ul, ur, vm, vl, vr, dm, dl, dr, hm, hl, hr, tm, tl, tr,
+               cl, cr, am, ae, bm, be, uo, vo, ho, do):
         j = pl.program_id(0)
-
-        def cat(a, b):
-            return jnp.concatenate([a, b], axis=-1)
-
-        u0 = cat(um[0], ue[0])
-        u1 = cat(um[1], ue[1])
-        v0 = cat(vm[0], ve[0])
-        v1 = cat(vm[1], ve[1])
-        d = cat(dm[...], de[...])
-        h = cat(hm[...], he[...])
-        t = cat(tm[...], te[...])
+        first = j == 0
+        last = j == nblocks - 1
+
+        def window(k, main, lft, rgt):
+            lft = jnp.where(first, cl[k], lft)
+            rgt = jnp.where(last, cr[k], rgt)
+            core = jnp.concatenate([lft, main, rgt], axis=-1)
+            top = jnp.concatenate([am[k], ae[k]], axis=-1)
+            bot = jnp.concatenate([bm[k], be[k]], axis=-1)
+            return jnp.concatenate([top, core, bot], axis=0)
+
+        u0 = window(0, um[0], ul[0], ur[0])
+        u1 = window(1, um[1], ul[1], ur[1])
+        v0 = window(2, vm[0], vl[0], vr[0])
+        v1 = window(3, vm[1], vl[1], vr[1])
+        d = window(4, dm[...], dl[...], dr[...])
+        h = window(5, hm[...], hl[...], hr[...])
+        t = window(6, tm[...], tl[...], tr[...])
         shape = d.shape
         grow = lax.broadcasted_iota(jnp.int32, shape, 0) + (pos_ref[0] * rows - HR)
         gcol = lax.broadcasted_iota(jnp.int32, shape, 1) + (pos_ref[1] * cols + j * BW - HC)
@@ -160,23 +163,37 @@
         ho[...] = core(hn)
         do[...] = core(d3)
 
-    main2 = pl.BlockSpec((2, ext_rows, BW), lambda j: (0, 0, j))
-    extra2 = pl.BlockSpec((2, ext_rows, extra), lambda j: (0, 0, (j + 1) * (BW // extra)))
-    main1 = pl.BlockSpec((ext_rows, BW), lambda j: (0, j))
-    extra1 = pl.BlockSpec((ext_rows, extra), lambda j: (0, (j + 1) * (BW // extra)))
+    def lcol(j):
+        return jnp.maximum(j * per - 1, 0)
+
+    def rcol(j):
+        return jnp.minimum((j + 1) * per, last_col_block)
+
+    main2 = pl.BlockSpec((2, rows, BW), lambda j: (0, 0, j))
+    left2 = pl.BlockSpec((2, rows, HC), lambda j: (0, 0, lcol(j)))
+    right2 = pl.BlockSpec((2, rows, HC), lambda j: (0, 0, rcol(j)))
+    main1 = pl.BlockSpec((rows, BW), lambda j: (0, j))
+    left1 = pl.BlockSpec((rows, HC), lambda j: (0, lcol(j)))
+    right1 = pl.BlockSpec((rows, HC), lambda j: (0, rcol(j)))
+    colh = pl.BlockSpec((nf, rows, HC), lambda j: (0, 0, 0))
+    rowm = pl.BlockSpec((nf, HR, BW), lambda j: (0, 0, j))
+    rowe = pl.BlockSpec((nf, HR, extra), lambda j: (0, 0, (j + 1) * (BW // extra)))
     out2 = pl.BlockSpec((2, rows, BW), lambda j: (0, 0, j))
     out1 = pl.BlockSpec((rows, BW), lambda j: (0, j))
     f32 = damage.dtype
     outs = pl.pallas_call(
         kernel,
         grid=(nblocks,),
-        in_specs=[pl.BlockSpec(memory_space=pltpu.SMEM), main2, extra2, main2, extra2,
-                  main1, extra1, main1, extra1, main1, extra1],
+        in_specs=[pl.BlockSpec(memory_space=pltpu.SMEM), main2, left2, right2, main2, left2, right2,
+                  main1, left1, right1, main1, left1, right1, main1, left1, right1,
+                  colh, colh, rowm, rowe, rowm, rowe],
         out_specs=[out2, out2, out1, out1],
         out_shape=[jax.ShapeDtypeStruct((2, rows, cols), f32), jax.ShapeDtypeStruct((2, rows, cols), f32),
                    jax.ShapeDtypeStruct((rows, cols), f32), jax.ShapeDtypeStruct((rows, cols), f32)],
         interpret=INTERPRET,
-    )(pos, eu, eu, ev, ev, ed, ed, eh, eh, et, et)
+    )(pos, displacement, displacement, displacement, velocity, velocity, velocity,
+      damage, damage, damage, history, history, history, toughness, toughness, toughness,
+      col_left, col_right, above, above, below, below)
     return tuple(outs)
 
 

time: 148 us -> 98.3 us (0.66)
  local copies, waits for them, and re-layouts: 77.3 us -> 30.8 us
  other arithmetic: 11.5 us -> 3.68 us
  waiting for transfers between devices: 21.4 us -> 25.7 us
    concatenate x7 -> x0, local copies, waits for them, and re-layouts: 35.7 us -> none  [exchange(): jnp.concatenate([gap, from_above[k], core, from_below[k], gap], axis=0)]
    unnamed x74 -> x28, local copies, waits for them, and re-layouts: 16.3 us -> 4.94 us
    concatenate x4 -> x0, other arithmetic: 5.25 us -> none  [exchange(): core = jnp.concatenate([left_block[k], fields[k], right_block[k]], axis=1)]
    ppermute x1, waiting for transfers between devices: 21.3 us -> 25.7 us  [exchange(): from_below = lax.ppermute(top, 'gx', [(i + 1, i) for i in range(nx - 1)])]
    slice x5, local copies, waits for them, and re-layouts: 6.77 us -> 2.52 us  [ext_rows(): mid = jnp.stack([f[lo:hi] for f in fields])]
    pad x0 -> x4, local copies, waits for them, and re-layouts: none -> 4.22 us  [the longest x1 1.43 us: exchange(): above = jnp.pad(from_above, ((0, 0), (HR - RAD, 0), (0, 0)))]
    another operation x2 -> x0, other arithmetic: 3.79 us -> none  [the longest x1 1.92 us: on_device(): eu = jnp.stack(ext[0:2])]
    ppermute x0 -> x2, local copies, waits for them, and re-layouts: none -> 2.28 us  [the longest x1 1.82 us: exchange(): from_above = lax.ppermute(bottom, 'gx', [(i, i + 1) for i in range(nx - 1)])]
  transfers between devices with their start and end apart: 3 -> 3, of which waited for: 1 -> 1; matrix products, arithmetic and copies ran while one was open for 21% -> 22% of each run, Pallas kernels for 0% -> 0%
where the time goes in v2:
time: 98.3 us; the launch traced here: 96.4 us
  local copies, waits for them, and re-layouts  30.8 us (31%)
  Pallas kernels  27.2 us (28%)
  waiting for transfers between devices  25.7 us (26%)
  starting transfers between devices  8.31 us (8%)
  other arithmetic  3.68 us (4%)
    pallas_call x1, Pallas kernels, on_device(): pl.pallas_call(kernel, grid=(nblocks,), in_specs=[pl.BlockSpec(memory_spa...  27.2 us
    ppermute x1, waiting for transfers between devices, exchange(): from_below = lax.ppermute(top, 'gx', [(i + 1, i) for i in range(nx - 1)])  25.7 us
    another operation x8, local copies, waits for them, and re-layouts, ext_rows(): mid = jnp.stack([f[lo:hi] for f in fields])  12.4 us
    unnamed x28, local copies, waits for them, and re-layouts  4.94 us
    ppermute x1, starting transfers between devices, exchange(): from_above = lax.ppermute(bottom, 'gx', [(i, i + 1) for i in range(nx - 1)])  4.25 us
    ppermute x1, starting transfers between devices, exchange(): from_below = lax.ppermute(top, 'gx', [(i + 1, i) for i in range(nx - 1)])  2.85 us
    squeeze x1, local copies, waits for them, and re-layouts, on_device(): displacement[1]  2.8 us
    slice x5, local copies, waits for them, and re-layouts, ext_rows(): mid = jnp.stack([f[lo:hi] for f in fields])  2.52 us
  transfers between devices with their start and end apart: 3, of which 1 were waited for; matrix products, arithmetic and copies ran while one was open for 22% of the time, Pallas kernels for 0%

profile of v2, /device:TPU:89, one launch (start us, length us, event | category | flops | bytes accessed | tf_op | source)
XLA Modules:
  0.0 96.4 jit_solution(10961127749099378477)
XLA Ops:
  0.6 0.0 copy-start.1
  0.6 2.8 %slice_bitcast_fusion.2 = (f32[32,8192]{1,0:T(8,128)}, f32[32,8192]{1,0:T(8,128)S(1)}) fusion(f32[2,32,8192]{2,1,0:T(8,128)} %ur.1), kind=kLoop, calls=%fused_computation.4 | loop fusion | bytes 4194304 | tf_op jit(solution)/shard_map/squeeze | solution.py:119
  3.4 0.1 constant_dynamic-update-slice_fusion.13
  3.5 1.5 %slice_bitcast_fusion = (f32[32,8192]{1,0:T(8,128)}, f32[32,8192]{1,0:T(8,128)}) fusion(f32[2,32,8192]{2,1,0:T(8,128)S(1)} %copy-done.1), kind=kLoop, calls=%fused_computation.2 | loop fusion | bytes 4194304 | tf_op jit(solution)/shard_map/squeeze | solution.py:119
  5.0 1.0 %constant_dynamic-update-slice_fusion.12 = (f32[7,32,5]{2,1,0:T(8,128)S(1)}, f32[7,32,5]{2,1,0:T(8,128)S(1)}) fusion(f32[7,32,5]{2,1,0:T(8,128)S(1)} %get-tuple-element.30, f32[32,8192]{1,0:T(8,128)} %get-tuple-element.10, f32[7,32,5]{2,1,0:T(8,128)S(1)} %get-tuple-element.31), kind=kLoop, calls=%fused_computation.21 | loop fusion | bytes 34048
  6.0 0.8 constant_dynamic-update-slice_fusion.11
  6.8 1.0 constant_dynamic-update-slice_fusion.10
  7.8 0.1 constant_dynamic-update-slice_fusion.9
  7.9 0.1 constant_dynamic-update-slice_fusion.8
  8.0 0.1 constant_dynamic-update-slice_fusion.7
  8.0 0.7 broadcast_select_fusion.2
  8.7 1.2 %collective-permute-start = (f32[7,32,5]{2,1,0:T(8,128)}, f32[7,32,5]{2,1,0:T(8,128)S(1)}, u32[]{:S(2)}, u32[]{:S(2)}) collective-permute-start(f32[7,32,5]{2,1,0:T(8,128)} %broadcast_select_fusion.2), channel_id=1, source_target_pairs={{0,1},{1,0},{2,3},{3,2},{4,5},{5,4},{6,7},{7,6},{8,9},{9,8},{10,11... | collective-permute-start | bytes 13448 | tf_op jit(solution)/shard_map/ppermute | solution.py:90
  9.9 0.8 fusion.4
  10.7 0.7 fusion.3
  11.5 0.0 copy-done
  11.5 0.1 fusion.1
  11.5 0.9 copy-done.2
  12.4 0.1 fusion
  12.5 0.8 fusion.2
  13.3 1.1 %stack.114 = f32[1,5,8192]{2,0,1:T(1,128)S(1)} reshape(f32[5,8192]{1,0:T(8,128)} %get-tuple-element.16) | data formatting | bytes 327680 | tf_op jit(solution)/shard_map/stack | solution.py:100
  14.4 1.7 %stack.110 = f32[1,5,8192]{2,0,1:T(1,128)} reshape(f32[5,8192]{1,0:T(8,128)} %get-tuple-element.17) | data formatting | bytes 327680 | tf_op jit(solution)/shard_map/stack | solution.py:100
  16.1 1.1 %stack.115 = f32[1,5,8192]{2,0,1:T(1,128)S(1)} reshape(f32[5,8192]{1,0:T(8,128)} %get-tuple-element.14) | data formatting | bytes 327680 | tf_op jit(solution)/shard_map/stack | solution.py:100
  17.2 0.8 stack.111
  18.0 0.8 stack.116
  18.8 0.8 stack.112
  19.6 0.3 copy.65
  19.8 0.3 copy.63
  20.1 0.3 copy.66
  20.3 0.3 copy.64
  20.6 0.0 copy-start.8
  20.6 3.0 %stack.117 = f32[7,5,8192]{2,0,1:T(8,128)S(1)} concatenate(f32[2,5,8192]{2,0,1:T(2,128)S(1)} %copy.65, f32[2,5,8192]{2,0,1:T(2,128)S(1)} %copy.66, f32[1,5,8192]{2,0,1:T(1,128)S(1)} %stack.114, f32[1,5,8192]{2,0,1:T(1,128)S(1)} %stack.115, f32[1,5,8192]{2,0,1:T(1,128)} %stack.116), dimensions={0} | concatenate | bytes 2293760 | tf_op jit(solution)/shard_map/stack | solution.py:100
  23.7 3.1 %stack.113 = f32[7,5,8192]{2,0,1:T(8,128)S(1)} concatenate(f32[2,5,8192]{2,0,1:T(2,128)S(1)} %copy.63, f32[2,5,8192]{2,0,1:T(2,128)S(1)} %copy.64, f32[1,5,8192]{2,0,1:T(1,128)S(1)} %copy-done.8, f32[1,5,8192]{2,0,1:T(1,128)} %stack.111, f32[1,5,8192]{2,0,1:T(1,128)} %stack.112), dimensions={0} | concatenate | bytes 2293760 | tf_op jit(solution)/shard_map/stack | solution.py:100
  26.8 0.0 collective-permute-done
  26.8 0.1 pad_slice_fusion
  26.9 1.2 %pad_maximum_fusion.1 = f32[7,5,8448]{2,0,1:T(8,128)} fusion(f32[7,5,128]{2,0,1:T(8,128)S(1)} %copy.61, f32[7,5,8192]{2,0,1:T(8,128)S(1)} %stack.117, f32[7,5,128]{2,0,1:T(8,128)S(1)} %copy.60), kind=kLoop, calls=%fused_computation.1 | loop fusion | flops 591360 | bytes 2365440 | tf_op jit(solution)/shard_map/concatenate | solution.py:101
  28.1 2.9 %collective-permute-start.2 = (f32[7,5,8448]{2,0,1:T(8,128)}, f32[7,5,8448]{2,0,1:T(8,128)S(1)}, u32[]{:S(2)}, u32[]{:S(2)}) collective-permute-start(f32[7,5,8448]{2,0,1:T(8,128)} %pad_maximum_fusion.1), channel_id=1, source_target_pairs={{2,0},{4,2},{6,4},{8,6},{10,8},{12,10},{14,12},{16,14},{18,16},{20... | collective-permute-start | bytes 3548168 | tf_op jit(solution)/shard_map/ppermute | solution.py:106
  31.0 1.2 %pad_maximum_fusion = f32[7,5,8448]{2,0,1:T(8,128)} fusion(f32[7,5,128]{2,0,1:T(8,128)S(1)} %copy.56, f32[7,5,8192]{2,0,1:T(8,128)S(1)} %stack.113, f32[7,5,128]{2,0,1:T(8,128)S(1)} %copy.55), kind=kLoop, calls=%fused_computation | loop fusion | flops 591360 | bytes 2365440 | tf_op jit(solution)/shard_map/concatenate | solution.py:101
  32.2 4.2 %collective-permute-start.1 = (f32[7,5,8448]{2,0,1:T(8,128)}, f32[7,5,8448]{2,0,1:T(8,128)}, u32[]{:S(2)}, u32[]{:S(2)}) collective-permute-start(f32[7,5,8448]{2,0,1:T(8,128)} %pad_maximum_fusion), channel_id=1, source_target_pairs={{0,2},{2,4},{4,6},{6,8},{8,10},{10,12},{12,14},{14,16},{16,18},{18... | collective-permute-start | bytes 3548168 | tf_op jit(solution)/shard_map/ppermute | solution.py:105
  36.4 0.6 pad_add_fusion.pos_ref
  37.0 0.6 pad.17.cr
  37.7 0.7 pad.16.cl
  38.4 25.7 %collective-permute-done.2 = f32[7,5,8448]{2,0,1:T(8,128)S(1)} collective-permute-done((f32[7,5,8448]{2,0,1:T(8,128)}, f32[7,5,8448]{2,0,1:T(8,128)S(1)}, u32[]{:S(2)}, u32[]{:S(2)}) %collective-permute-start.2) | collective-permute-done | bytes 1182752 | tf_op jit(solution)/shard_map/ppermute | solution.py:106
  64.1 0.5 copy.62
  64.6 1.4 %pad.19.bm.be = f32[7,8,8448]{2,1,0:T(8,128)} pad(f32[7,5,8448]{2,1,0:T(8,128)S(1)} %copy.62, f32[]{:T(128)} %constant.14.clone.1), padding=0_0x0_3x0_0 | pad | bytes 3075076 | tf_op jit(solution)/shard_map/jit(_pad)/pad | solution.py:108
  66.0 0.0 collective-permute-done.1
  66.0 1.8 %copy.57 = f32[7,5,8448]{2,1,0:T(8,128)S(1)} copy(f32[7,5,8448]{2,0,1:T(8,128)} %collective-permute-done.1) | data formatting | bytes 2365440 | tf_op jit(solution)/shard_map/ppermute | solution.py:105
  67.8 1.4 %pad.18.am.ae = f32[7,8,8448]{2,1,0:T(8,128)} pad(f32[7,5,8448]{2,1,0:T(8,128)S(1)} %copy.57, f32[]{:T(128)} %constant.14.clone.1), padding=0_0x3_0x0_0 | pad | bytes 3075076 | tf_op jit(solution)/shard_map/jit(_pad)/pad | solution.py:107
  69.2 27.2 %shard_map.84 = (f32[2,32,8192]{2,1,0:T(8,128)}, f32[2,32,8192]{2,1,0:T(8,128)}, f32[32,8192]{1,0:T(8,128)}, f32[32,8192]{1,0:T(8,128)}) custom-call(s32[2]{0:T(128)} %pad_add_fusion.pos_ref, f32[2,32,8192]{2,1,0:T(8,128)} %ur.1, f32[2,32,8192]{2,1,0:T(8,128)} %ur.1, f32[2,32,8192]{2,1,0:T(8,128)} %ur.1, f32[2,32,8192]{2,1,0:T(8,128)} %vr.1, ...), custom_call_target="tpu_custom_call" | custom-call | tf_op jit(solution)/shard_map/pallas_call | solution.py:184
  (19 shorter events, 0.1 us)
Async XLA Ops:
  0.6 2.9 %copy-start.1 = (f32[2,32,8192]{2,1,0:T(8,128)S(1)}, f32[2,32,8192]{2,1,0:T(8,128)}, u32[]{:S(2)}) copy-start(f32[2,32,8192]{2,1,0:T(8,128)} %vr.1) | copy-start | bytes 6291460
  3.5 4.3 %copy-start.3 = (f32[32,8192]{1,0:T(8,128)S(1)}, f32[32,8192]{1,0:T(8,128)}, u32[]{:S(2)}) copy-start(f32[32,8192]{1,0:T(8,128)} %dr.1) | copy-start | bytes 3145732
  3.5 4.4 %copy-start.4 = (f32[32,8192]{1,0:T(8,128)S(1)}, f32[32,8192]{1,0:T(8,128)}, u32[]{:S(2)}) copy-start(f32[32,8192]{1,0:T(8,128)} %hr.1) | copy-start | bytes 3145732
  3.5 4.4 %copy-start.5 = (f32[32,8192]{1,0:T(8,128)S(1)}, f32[32,8192]{1,0:T(8,128)}, u32[]{:S(2)}) copy-start(f32[32,8192]{1,0:T(8,128)} %tr.1) | copy-start | bytes 3145732
  6.8 4.6 %copy-start = (f32[2,32,8192]{2,1,0:T(8,128)S(1)}, f32[2,32,8192]{2,1,0:T(8,128)}, u32[]{:S(2)}) copy-start(f32[2,32,8192]{2,1,0:T(8,128)} %ur.1) | copy-start | bytes 6291460
  8.7 18.1 %collective-permute-start = (f32[7,32,5]{2,1,0:T(8,128)}, f32[7,32,5]{2,1,0:T(8,128)S(1)}, u32[]{:S(2)}, u32[]{:S(2)}) collective-permute-start(f32[7,32,5]{2,1,0:T(8,128)} %broadcast_select_fusion.2), channel_id=1, source_target_pairs={{0,1},{1,0},{2,3},{3,2},{4,5},{5,4},{6,7},{7,6},{8,9},{9,8},{10,11... | collective-permute-start | bytes 13448 | tf_op jit(solution)/shard_map/ppermute | solution.py:90
  10.7 1.7 %copy-start.2 = (f32[2,32,8192]{2,1,0:T(8,128)S(1)}, f32[2,32,8192]{2,1,0:T(8,128)}, u32[]{:S(2)}) copy-start(f32[2,32,8192]{2,1,0:T(8,128)} %vr.1) | copy-start | bytes 6291460
  13.3 4.7 %copy-start.7 = (f32[5,8192]{1,0:T(8,128)S(1)}, f32[5,8192]{1,0:T(8,128)}, u32[]{:S(2)}) copy-start(f32[5,8192]{1,0:T(8,128)} %get-tuple-element.12) | copy-start | bytes 491524
  13.3 5.5 %copy-start.6 = (f32[5,8192]{1,0:T(8,128)S(1)}, f32[5,8192]{1,0:T(8,128)}, u32[]{:S(2)}) copy-start(f32[5,8192]{1,0:T(8,128)} %get-tuple-element.13) | copy-start | bytes 491524
  20.6 3.1 %copy-start.8 = (f32[1,5,8192]{2,0,1:T(1,128)S(1)}, f32[1,5,8192]{2,0,1:T(1,128)}, u32[]{:S(2)}) copy-start(f32[1,5,8192]{2,0,1:T(1,128)} %stack.110) | copy-start | bytes 491524
  28.1 36.0 %collective-permute-start.2 = (f32[7,5,8448]{2,0,1:T(8,128)}, f32[7,5,8448]{2,0,1:T(8,128)S(1)}, u32[]{:S(2)}, u32[]{:S(2)}) collective-permute-start(f32[7,5,8448]{2,0,1:T(8,128)} %pad_maximum_fusion.1), channel_id=1, source_target_pairs={{2,0},{4,2},{6,4},{8,6},{10,8},{12,10},{14,12},{16,14},{18,16},{20... | collective-permute-start | bytes 3548168 | tf_op jit(solution)/shard_map/ppermute | solution.py:106
  32.2 33.8 %collective-permute-start.1 = (f32[7,5,8448]{2,0,1:T(8,128)}, f32[7,5,8448]{2,0,1:T(8,128)}, u32[]{:S(2)}, u32[]{:S(2)}) collective-permute-start(f32[7,5,8448]{2,0,1:T(8,128)} %pad_maximum_fusion), channel_id=1, source_target_pairs={{0,2},{2,4},{4,6},{6,8},{8,10},{10,12},{12,14},{14,16},{16,18},{18... | collective-permute-start | bytes 3548168 | tf_op jit(solution)/shard_map/ppermute | solution.py:105

commit v3 on v2

--- a/solution.py
+++ b/solution.py
@@ -9,7 +9,6 @@
 WEIGHT_TWO = 1.0 / (1.0 - CHEB * CHEB / 2.0)
 WEIGHT_THREE = 1.0 / (1.0 - CHEB * CHEB * WEIGHT_TWO / 4.0)
 
-RAD = 5
 HR = 8
 HC = 128
 BW = 1024
@@ -79,34 +78,10 @@
     return n0, n1, vel0, vel1, hist_new, d3
 
 
-def exchange(fields):
-    rows, cols = fields[0].shape
-    iy = lax.axis_index("gy")
-    ny = lax.axis_size("gy")
-    nx = lax.axis_size("gx")
-    left = jnp.stack([f[:, :RAD] for f in fields])
-    right = jnp.stack([f[:, cols - RAD:] for f in fields])
-    if ny == 2:
-        got = lax.ppermute(jnp.where(iy == 0, right, left), "gy", [(0, 1), (1, 0)])
-        from_left = jnp.where(iy == 1, got, 0.0)
-        from_right = jnp.where(iy == 0, got, 0.0)
-    else:
-        from_left = lax.ppermute(right, "gy", [(i, i + 1) for i in range(ny - 1)])
-        from_right = lax.ppermute(left, "gy", [(i + 1, i) for i in range(ny - 1)])
-    left_block = jnp.pad(from_left, ((0, 0), (0, 0), (HC - RAD, 0)))
-    right_block = jnp.pad(from_right, ((0, 0), (0, 0), (0, HC - RAD)))
-
-    def ext_rows(lo, hi):
-        mid = jnp.stack([f[lo:hi] for f in fields])
-        return jnp.concatenate([left_block[:, lo:hi], mid, right_block[:, lo:hi]], axis=2)
-
-    top = ext_rows(0, RAD)
-    bottom = ext_rows(rows - RAD, rows)
-    from_above = lax.ppermute(bottom, "gx", [(i, i + 1) for i in range(nx - 1)])
-    from_below = lax.ppermute(top, "gx", [(i + 1, i) for i in range(nx - 1)])
-    above = jnp.pad(from_above, ((0, 0), (HR - RAD, 0), (0, 0)))
-    below = jnp.pad(from_below, ((0, 0), (0, HR - RAD), (0, 0)))
-    return left_block, right_block, above, below
+RADII = (5, 5, 5, 5, 4, 2, 3)
+OFFSETS = tuple(sum(RADII[:k]) for k in range(len(RADII)))
+STRIP = 32
+LANE_W = 5
 
 
 def on_device(displacement, velocity, damage, history, toughness):
@@ -115,43 +90,144 @@
     ny = lax.axis_size("gy")
     ix = lax.axis_index("gx")
     iy = lax.axis_index("gy")
+    assert ny == 2 and rows % 8 == 0 and cols % BW == 0
     total_rows, total_cols = rows * nx, cols * ny
-    fields = [displacement[0], displacement[1], velocity[0], velocity[1], damage, history, toughness]
-    nf = len(fields)
-    col_left, col_right, above, below = exchange(fields)
+    nf = len(RADII)
     pos = jnp.stack([ix, iy]).astype(jnp.int32)
     nblocks = cols // BW
     per = BW // HC
     last_col_block = cols // HC - 1
-    extra = 2 * HC
+    last_row_block = rows // 8 - 1
+    f32 = damage.dtype
+    rl = jnp_shift if INTERPRET else roll_shift
+
+    def roll(x, s, axis):
+        return rl(x, -s, axis)
+
+    def split(refs):
+        du, dv, dd, dh, dt = refs
+        return [du[0], du[1], dv[0], dv[1], dd[...], dh[...], dt[...]]
+
+    def pack_kernel(pos_ref, tu, tv, td, th, tt, bu, bv, bd, bh, bt,
+                    lu, lv, ld, lh, lt, ru, rv, rd, rh, rt, top_o, bot_o, col_o):
+        j = pl.program_id(0)
+        tops = split((tu, tv, td, th, tt))
+        bots = split((bu, bv, bd, bh, bt))
+        ridx = lax.broadcasted_iota(jnp.int32, (STRIP, BW), 0)
+        top = jnp.zeros((STRIP, BW), f32)
+        bot = jnp.zeros((STRIP, BW), f32)
+        pad = jnp.zeros((STRIP - 8, BW), f32)
+        for k in range(nf):
+            r, o = RADII[k], OFFSETS[k]
+            inside = (ridx >= o) & (ridx < o + r)
+            x = roll(jnp.concatenate([tops[k], pad], axis=0), o, 0)
+            top = jnp.where(inside, x, top)
+            y = roll(jnp.concatenate([bots[k], pad], axis=0), o - (8 - r), 0)
+            bot = jnp.where(inside, y, bot)
+        top_o[...] = top
+        bot_o[...] = bot
+
+        @pl.when(j == 0)
+        def _():
+            lefts = split((lu, lv, ld, lh, lt))
+            rights = split((ru, rv, rd, rh, rt))
+            lidx = lax.broadcasted_iota(jnp.int32, (rows, HC), 1)
+            col = jnp.zeros((rows, HC), f32)
+            to_right = pos_ref[1] == 0
+            for k in range(nf):
+                inside = (lidx >= LANE_W * k) & (lidx < LANE_W * (k + 1))
+                a = roll(rights[k], LANE_W * k - (HC - LANE_W), 1)
+                b = roll(lefts[k], LANE_W * k, 1)
+                col = jnp.where(inside, jnp.where(to_right, a, b), col)
+            col_o[...] = col
+
+    t2 = pl.BlockSpec((2, 8, BW), lambda j: (0, 0, j))
+    t1 = pl.BlockSpec((8, BW), lambda j: (0, j))
+    b2 = pl.BlockSpec((2, 8, BW), lambda j: (0, last_row_block, j))
+    b1 = pl.BlockSpec((8, BW), lambda j: (last_row_block, j))
+    l2 = pl.BlockSpec((2, rows, HC), lambda j: (0, 0, 0))
+    l1 = pl.BlockSpec((rows, HC), lambda j: (0, 0))
+    r2 = pl.BlockSpec((2, rows, HC), lambda j: (0, 0, last_col_block))
+    r1 = pl.BlockSpec((rows, HC), lambda j: (0, last_col_block))
+    smem = pl.BlockSpec(memory_space=pltpu.SMEM)
+    ins = (displacement, velocity, damage, history, toughness)
+    top_s, bot_s, col_s = pl.pallas_call(
+        pack_kernel,
+        grid=(nblocks,),
+        in_specs=[smem, t2, t2, t1, t1, t1, b2, b2, b1, b1, b1, l2, l2, l1, l1, l1, r2, r2, r1, r1, r1],
+        out_specs=[pl.BlockSpec((STRIP, BW), lambda j: (0, j)), pl.BlockSpec((STRIP, BW), lambda j: (0, j)),
+                   pl.BlockSpec((rows, HC), lambda j: (0, 0))],
+        out_shape=[jax.ShapeDtypeStruct((STRIP, cols), f32), jax.ShapeDtypeStruct((STRIP, cols), f32),
+                   jax.ShapeDtypeStruct((rows, HC), f32)],
+        interpret=INTERPRET,
+    )(pos, *ins, *ins, *ins, *ins)
+
+    above = lax.ppermute(bot_s, "gx", [(i, i + 1) for i in range(nx - 1)])
+    below = lax.ppermute(top_s, "gx", [(i + 1, i) for i in range(nx - 1)])
+    side = lax.ppermute(col_s, "gy", [(0, 1), (1, 0)])
+    both = ("gx", "gy")
+    corner_above = lax.ppermute(col_s[rows - 8:], both,
+                                [(i * 2 + g, (i + 1) * 2 + 1 - g) for i in range(nx - 1) for g in range(2)])
+    corner_below = lax.ppermute(col_s[:8], both,
+                                [((i + 1) * 2 + g, i * 2 + 1 - g) for i in range(nx - 1) for g in range(2)])
 
     def kernel(pos_ref, um, ul, ur, vm, vl, vr, dm, dl, dr, hm, hl, hr, tm, tl, tr,
-               cl, cr, am, ae, bm, be, uo, vo, ho, do):
+               am, al, ar, bm, bl, br, side_ref, ca_ref, cb_ref, uo, vo, ho, do):
         j = pl.program_id(0)
         first = j == 0
         last = j == nblocks - 1
-
-        def window(k, main, lft, rgt):
-            lft = jnp.where(first, cl[k], lft)
-            rgt = jnp.where(last, cr[k], rgt)
-            core = jnp.concatenate([lft, main, rgt], axis=-1)
-            top = jnp.concatenate([am[k], ae[k]], axis=-1)
-            bot = jnp.concatenate([bm[k], be[k]], axis=-1)
+        has_left = pos_ref[1] == 1
+        has_right = pos_ref[1] == 0
+        mains = split((um, vm, dm, hm, tm))
+        lefts = split((ul, vl, dl, hl, tl))
+        rights = split((ur, vr, dr, hr, tr))
+        side_v = side_ref[...]
+        ca = ca_ref[...]
+        cb = cb_ref[...]
+
+        def lane_left(x, k):
+            lidx = lax.broadcasted_iota(jnp.int32, x.shape, 1)
+            y = roll(x, HC - LANE_W - LANE_W * k, 1)
+            return jnp.where((lidx >= HC - LANE_W) & has_left, y, 0.0)
+
+        def lane_right(x, k):
+            lidx = lax.broadcasted_iota(jnp.int32, x.shape, 1)
+            y = roll(x, -LANE_W * k, 1)
+            return jnp.where((lidx < LANE_W) & has_right, y, 0.0)
+
+        def above_tile(x, k):
+            r, o = RADII[k], OFFSETS[k]
+            y = roll(x, 8 - r - o, 0)[:8]
+            ridx = lax.broadcasted_iota(jnp.int32, y.shape, 0)
+            return jnp.where(ridx >= 8 - r, y, 0.0)
+
+        def below_tile(x, k):
+            r, o = RADII[k], OFFSETS[k]
+            y = roll(x, -o, 0)[:8]
+            ridx = lax.broadcasted_iota(jnp.int32, y.shape, 0)
+            return jnp.where(ridx < r, y, 0.0)
+
+        a_m, a_l, a_r = am[...], al[...], ar[...]
+        b_m, b_l, b_r = bm[...], bl[...], br[...]
+
+        def window(k):
+            lft = jnp.where(first, lane_left(side_v, k), lefts[k])
+            rgt = jnp.where(last, lane_right(side_v, k), rights[k])
+            core = jnp.concatenate([lft, mains[k], rgt], axis=-1)
+            top = jnp.concatenate([jnp.where(first, lane_left(ca, k), above_tile(a_l, k)),
+                                   above_tile(a_m, k),
+                                   jnp.where(last, lane_right(ca, k), above_tile(a_r, k))], axis=-1)
+            bot = jnp.concatenate([jnp.where(first, lane_left(cb, k), below_tile(b_l, k)),
+                                   below_tile(b_m, k),
+                                   jnp.where(last, lane_right(cb, k), below_tile(b_r, k))], axis=-1)
             return jnp.concatenate([top, core, bot], axis=0)
 
-        u0 = window(0, um[0], ul[0], ur[0])
-        u1 = window(1, um[1], ul[1], ur[1])
-        v0 = window(2, vm[0], vl[0], vr[0])
-        v1 = window(3, vm[1], vl[1], vr[1])
-        d = window(4, dm[...], dl[...], dr[...])
-        h = window(5, hm[...], hl[...], hr[...])
-        t = window(6, tm[...], tl[...], tr[...])
+        u0, u1, v0, v1, d, h, t = [window(k) for k in range(nf)]
         shape = d.shape
         grow = lax.broadcasted_iota(jnp.int32, shape, 0) + (pos_ref[0] * rows - HR)
         gcol = lax.broadcasted_iota(jnp.int32, shape, 1) + (pos_ref[1] * cols + j * BW - HC)
         valid = (grow >= 0) & (grow < total_rows) & (gcol >= 0) & (gcol < total_cols)
-        sh = jnp_shift if INTERPRET else roll_shift
-        n0, n1, w0, w1, hn, d3 = step_fields(u0, u1, v0, v1, d, h, t, valid, sh)
+        n0, n1, w0, w1, hn, d3 = step_fields(u0, u1, v0, v1, d, h, t, valid, rl)
 
         def core(x):
             return x[HR:HR + rows, HC:HC + BW]
@@ -175,25 +251,26 @@
     main1 = pl.BlockSpec((rows, BW), lambda j: (0, j))
     left1 = pl.BlockSpec((rows, HC), lambda j: (0, lcol(j)))
     right1 = pl.BlockSpec((rows, HC), lambda j: (0, rcol(j)))
-    colh = pl.BlockSpec((nf, rows, HC), lambda j: (0, 0, 0))
-    rowm = pl.BlockSpec((nf, HR, BW), lambda j: (0, 0, j))
-    rowe = pl.BlockSpec((nf, HR, extra), lambda j: (0, 0, (j + 1) * (BW // extra)))
+    sm = pl.BlockSpec((STRIP, BW), lambda j: (0, j))
+    sl = pl.BlockSpec((STRIP, HC), lambda j: (0, lcol(j)))
+    sr = pl.BlockSpec((STRIP, HC), lambda j: (0, rcol(j)))
+    sidespec = pl.BlockSpec((rows, HC), lambda j: (0, 0))
+    cornerspec = pl.BlockSpec((8, HC), lambda j: (0, 0))
     out2 = pl.BlockSpec((2, rows, BW), lambda j: (0, 0, j))
     out1 = pl.BlockSpec((rows, BW), lambda j: (0, j))
-    f32 = damage.dtype
     outs = pl.pallas_call(
         kernel,
         grid=(nblocks,),
-        in_specs=[pl.BlockSpec(memory_space=pltpu.SMEM), main2, left2, right2, main2, left2, right2,
+        in_specs=[smem, main2, left2, right2, main2, left2, right2,
                   main1, left1, right1, main1, left1, right1, main1, left1, right1,
-                  colh, colh, rowm, rowe, rowm, rowe],
+                  sm, sl, sr, sm, sl, sr, sidespec, cornerspec, cornerspec],
         out_specs=[out2, out2, out1, out1],
         out_shape=[jax.ShapeDtypeStruct((2, rows, cols), f32), jax.ShapeDtypeStruct((2, rows, cols), f32),
                    jax.ShapeDtypeStruct((rows, cols), f32), jax.ShapeDtypeStruct((rows, cols), f32)],
         interpret=INTERPRET,
     )(pos, displacement, displacement, displacement, velocity, velocity, velocity,
       damage, damage, damage, history, history, history, toughness, toughness, toughness,
-      col_left, col_right, above, above, below, below)
+      above, above, above, below, below, below, side, corner_above, corner_below)
     return tuple(outs)
 
 

time: 98.3 us -> 67.7 us (0.69)
  local copies, waits for them, and re-layouts: 30.8 us -> 2.67 us
  waiting for transfers between devices: 25.7 us -> 14.3 us
  starting transfers between devices: 8.31 us -> 14.8 us
  Pallas kernels: 27.2 us -> 33.3 us
  other arithmetic: 3.68 us -> 0.61 us
    another operation x9 -> x0, local copies, waits for them, and re-layouts: 12.4 us -> none  [the longest x8 12.4 us: ext_rows(): mid = jnp.stack([f[lo:hi] for f in fields])]
    ppermute x3 -> x5, waiting for transfers between devices: 25.7 us -> 14.3 us  [the longest x1 9.58 us: on_device(): lax.ppermute(col_s[:8], both, [((i + 1) * 2 + g, i * 2 + 1 - g) for i in...]
    ppermute x3 -> x5, starting transfers between devices: 8.31 us -> 14.8 us  [the longest x1 5.21 us: on_device(): above = lax.ppermute(bot_s, 'gx', [(i, i + 1) for i in range(nx - 1)])]
    pallas_call x1 -> x2, Pallas kernels: 27.2 us -> 33.3 us  [the longest x1 27 us: on_device(): pl.pallas_call(kernel, grid=(nblocks,), in_specs=[smem, main2, left2, rig...]
    squeeze x2 -> x0, local copies, waits for them, and re-layouts: 4.26 us -> none  [the longest x1 2.8 us: on_device(): displacement[1]]
    pad x4 -> x0, local copies, waits for them, and re-layouts: 4.22 us -> none  [the longest x1 1.43 us: exchange(): above = jnp.pad(from_above, ((0, 0), (HR - RAD, 0), (0, 0)))]
    unnamed x28 -> x10, local copies, waits for them, and re-layouts: 4.94 us -> 1.95 us
    concatenate x2 -> x0, other arithmetic: 2.39 us -> none  [ext_rows(): jnp.concatenate([left_block[:, lo:hi], mid, right_block[:, lo:hi]], axis=2)]
  transfers between devices with their start and end apart: 3 -> 5, of which waited for: 1 -> 2; matrix products, arithmetic and copies ran while one was open for 22% -> 1% of each run, Pallas kernels for 0% -> 0%
where the time goes in v3:
time: 67.7 us; the launch traced here: 66.4 us
  Pallas kernels  33.3 us (49%)
  starting transfers between devices  14.8 us (22%)
  waiting for transfers between devices  14.3 us (21%)
  local copies, waits for them, and re-layouts  2.67 us (4%)
  between operations  0.7 us (1%)
    pallas_call x1, Pallas kernels, on_device(): pl.pallas_call(kernel, grid=(nblocks,), in_specs=[smem, main2, left2, rig...  27 us
    ppermute x1, waiting for transfers between devices, on_device(): lax.ppermute(col_s[:8], both, [((i + 1) * 2 + g, i * 2 + 1 - g) for i in...  9.58 us
    pallas_call x1, Pallas kernels, on_device(): pl.pallas_call(pack_kernel, grid=(nblocks,), in_specs=[smem, t2, t2, t1,...  6.26 us
    ppermute x1, starting transfers between devices, on_device(): above = lax.ppermute(bot_s, 'gx', [(i, i + 1) for i in range(nx - 1)])  5.21 us
    ppermute x1, starting transfers between devices, on_device(): lax.ppermute(col_s[:8], both, [((i + 1) * 2 + g, i * 2 + 1 - g) for i in...  4.72 us
    ppermute x1, waiting for transfers between devices, on_device(): lax.ppermute(col_s[rows - 8:], both, [(i * 2 + g, (i + 1) * 2 + 1 - g) fo...  4.69 us
    ppermute x1, starting transfers between devices, on_device(): lax.ppermute(col_s[rows - 8:], both, [(i * 2 + g, (i + 1) * 2 + 1 - g) fo...  2.58 us
    unnamed x10, local copies, waits for them, and re-layouts  1.95 us
  transfers between devices with their start and end apart: 5, of which 2 were waited for; matrix products, arithmetic and copies ran while one was open for 1% of the time, Pallas kernels for 0%

profile of v3, /device:TPU:89, one launch (start us, length us, event | category | flops | bytes accessed | tf_op | source)
XLA Modules:
  0.0 66.4 jit_solution(12127371112445791599)
XLA Ops:
  0.6 0.6 pad_add_fusion.pos_ref
  1.2 6.3 %shard_map.84 = (f32[32,8192]{1,0:T(8,128)}, f32[32,8192]{1,0:T(8,128)}, f32[32,128]{1,0:T(8,128)}) custom-call(s32[2]{0:T(128)} %pad_add_fusion.pos_ref, f32[2,32,8192]{2,1,0:T(8,128)} %ur.1, f32[2,32,8192]{2,1,0:T(8,128)} %vr.1, f32[32,8192]{1,0:T(8,128)} %dr.1, f32[32,8192]{1,0:T(8,128)} %hr.1, f32[32,8192]{1,0:T(8,128)} %tr.1, f32[2,32,8192]{2,1,0:T(8,128)} %ur.1, ...), custom_call_target="tpu_custom_call" | custom-call | tf_op jit(solution)/shard_map/pallas_call | solution.py:154
  7.5 5.2 %collective-permute-start = (f32[32,8192]{1,0:T(8,128)}, f32[32,8192]{1,0:T(8,128)S(1)}, u32[]{:S(2)}, u32[]{:S(2)}) collective-permute-start(f32[32,8192]{1,0:T(8,128)} %get-tuple-element.7), channel_id=1, source_target_pairs={{0,2},{2,4},{4,6},{6,8},{8,10},{10,12},{12,14},{14,16},{16,18},{18... | collective-permute-start | bytes 3145736 | tf_op jit(solution)/shard_map/ppermute | solution.py:165
  12.7 1.9 %collective-permute-start.1 = (f32[32,8192]{1,0:T(8,128)}, f32[32,8192]{1,0:T(8,128)S(1)}, u32[]{:S(2)}, u32[]{:S(2)}) collective-permute-start(f32[32,8192]{1,0:T(8,128)} %get-tuple-element.8), channel_id=1, source_target_pairs={{2,0},{4,2},{6,4},{8,6},{10,8},{12,10},{14,12},{16,14},{18,16},{20... | collective-permute-start | bytes 3145736 | tf_op jit(solution)/shard_map/ppermute | solution.py:166
  14.7 0.4 collective-permute-start.2
  15.1 0.7 %fusion = (f32[8,128]{1,0:T(8,128)S(1)}, f32[8,128]{1,0:T(8,128)S(1)}) fusion(f32[32,128]{1,0:T(8,128)} %get-tuple-element.9), kind=kLoop, calls=%fused_computation.1 | loop fusion | bytes 16384 | tf_op jit(solution)/shard_map/slice | solution.py:171
  15.8 4.7 %collective-permute-start.4 = (f32[8,128]{1,0:T(8,128)S(1)}, f32[8,128]{1,0:T(8,128)S(1)}, u32[]{:S(2)}, u32[]{:S(2)}) collective-permute-start(f32[8,128]{1,0:T(8,128)S(1)} %get-tuple-element.10), channel_id=1, source_target_pairs={{2,1},{3,0},{4,3},{5,2},{6,5},{7,4},{8,7},{9,6},{10,9},{11,8},{12,... | collective-permute-start | bytes 12296 | tf_op jit(solution)/shard_map/ppermute | solution.py:171
  20.5 2.6 %collective-permute-start.3 = (f32[8,128]{1,0:T(8,128)S(1)}, f32[8,128]{1,0:T(8,128)S(1)}, u32[]{:S(2)}, u32[]{:S(2)}) collective-permute-start(f32[8,128]{1,0:T(8,128)S(1)} %get-tuple-element.11), channel_id=1, source_target_pairs={{0,3},{1,2},{2,5},{3,4},{4,7},{5,6},{6,9},{7,8},{8,11},{9,10},{10,... | collective-permute-start | bytes 12296 | tf_op jit(solution)/shard_map/ppermute | solution.py:169
  23.1 9.6 %collective-permute-done.4.cb_ref = f32[8,128]{1,0:T(8,128)S(1)} collective-permute-done((f32[8,128]{1,0:T(8,128)S(1)}, f32[8,128]{1,0:T(8,128)S(1)}, u32[]{:S(2)}, u32[]{:S(2)}) %collective-permute-start.4) | collective-permute-done | bytes 4128 | tf_op jit(solution)/shard_map/ppermute | solution.py:171
  32.7 0.0 copy-start.3
  32.7 4.7 %collective-permute-done.3.ca_ref = f32[8,128]{1,0:T(8,128)S(1)} collective-permute-done((f32[8,128]{1,0:T(8,128)S(1)}, f32[8,128]{1,0:T(8,128)S(1)}, u32[]{:S(2)}, u32[]{:S(2)}) %collective-permute-start.3) | collective-permute-done | bytes 4128 | tf_op jit(solution)/shard_map/ppermute | solution.py:169
  37.4 0.0 copy-start.4
  37.4 0.0 collective-permute-done.2.side_ref
  37.4 0.0 copy-start.2
  37.4 0.0 collective-permute-done.am.al.ar
  37.4 0.0 copy-start
  37.4 0.0 collective-permute-done.1.bm.bl.br
  37.4 0.0 copy-done.3
  37.4 0.5 copy-done.4
  38.0 0.0 copy-done.2
  38.0 0.4 copy-done
  38.4 0.0 copy-start.1
  38.4 1.0 %copy-done.1 = f32[32,8192]{1,0:T(8,128)} copy-done((f32[32,8192]{1,0:T(8,128)}, f32[32,8192]{1,0:T(8,128)S(1)}, u32[]{:S(2)}) %copy-start.1) | copy-done | bytes 1048600
  39.4 27.0 %shard_map.85 = (f32[2,32,8192]{2,1,0:T(8,128)}, f32[2,32,8192]{2,1,0:T(8,128)}, f32[32,8192]{1,0:T(8,128)}, f32[32,8192]{1,0:T(8,128)}) custom-call(s32[2]{0:T(128)} %pad_add_fusion.pos_ref, f32[2,32,8192]{2,1,0:T(8,128)} %ur.1, f32[2,32,8192]{2,1,0:T(8,128)} %ur.1, f32[2,32,8192]{2,1,0:T(8,128)} %ur.1, f32[2,32,8192]{2,1,0:T(8,128)} %vr.1, ...), custom_call_target="tpu_custom_call" | custom-call | tf_op jit(solution)/shard_map/pallas_call | solution.py:261
Async XLA Ops:
  7.5 29.9 %collective-permute-start = (f32[32,8192]{1,0:T(8,128)}, f32[32,8192]{1,0:T(8,128)S(1)}, u32[]{:S(2)}, u32[]{:S(2)}) collective-permute-start(f32[32,8192]{1,0:T(8,128)} %get-tuple-element.7), channel_id=1, source_target_pairs={{0,2},{2,4},{4,6},{6,8},{8,10},{10,12},{12,14},{14,16},{16,18},{18... | collective-permute-start | bytes 3145736 | tf_op jit(solution)/shard_map/ppermute | solution.py:165
  12.7 24.7 %collective-permute-start.1 = (f32[32,8192]{1,0:T(8,128)}, f32[32,8192]{1,0:T(8,128)S(1)}, u32[]{:S(2)}, u32[]{:S(2)}) collective-permute-start(f32[32,8192]{1,0:T(8,128)} %get-tuple-element.8), channel_id=1, source_target_pairs={{2,0},{4,2},{6,4},{8,6},{10,8},{12,10},{14,12},{16,14},{18,16},{20... | collective-permute-start | bytes 3145736 | tf_op jit(solution)/shard_map/ppermute | solution.py:166
  14.7 22.7 %collective-permute-start.2 = (f32[32,128]{1,0:T(8,128)}, f32[32,128]{1,0:T(8,128)S(1)}, u32[]{:S(2)}, u32[]{:S(2)}) collective-permute-start(f32[32,128]{1,0:T(8,128)} %get-tuple-element.9), channel_id=1, source_target_pairs={{0,1},{1,0},{2,3},{3,2},{4,5},{5,4},{6,7},{7,6},{8,9},{9,8},{10,11... | collective-permute-start | bytes 49160 | tf_op jit(solution)/shard_map/ppermute | solution.py:167
  15.8 16.9 %collective-permute-start.4 = (f32[8,128]{1,0:T(8,128)S(1)}, f32[8,128]{1,0:T(8,128)S(1)}, u32[]{:S(2)}, u32[]{:S(2)}) collective-permute-start(f32[8,128]{1,0:T(8,128)S(1)} %get-tuple-element.10), channel_id=1, source_target_pairs={{2,1},{3,0},{4,3},{5,2},{6,5},{7,4},{8,7},{9,6},{10,9},{11,8},{12,... | collective-permute-start | bytes 12296 | tf_op jit(solution)/shard_map/ppermute | solution.py:171
  20.5 16.9 %collective-permute-start.3 = (f32[8,128]{1,0:T(8,128)S(1)}, f32[8,128]{1,0:T(8,128)S(1)}, u32[]{:S(2)}, u32[]{:S(2)}) collective-permute-start(f32[8,128]{1,0:T(8,128)S(1)} %get-tuple-element.11), channel_id=1, source_target_pairs={{0,3},{1,2},{2,5},{3,4},{4,7},{5,6},{6,9},{7,8},{8,11},{9,10},{10,... | collective-permute-start | bytes 12296 | tf_op jit(solution)/shard_map/ppermute | solution.py:169
  32.7 4.7 %copy-start.3 = (f32[8,128]{1,0:T(8,128)}, f32[8,128]{1,0:T(8,128)S(1)}, u32[]{:S(2)}) copy-start(f32[8,128]{1,0:T(8,128)S(1)} %collective-permute-done.4.cb_ref) | copy-start | bytes 12292
  37.4 0.6 copy-start.4
  37.4 0.6 copy-start.2
  37.4 1.0 %copy-start = (f32[32,8192]{1,0:T(8,128)}, f32[32,8192]{1,0:T(8,128)S(1)}, u32[]{:S(2)}) copy-start(f32[32,8192]{1,0:T(8,128)S(1)} %collective-permute-done.am.al.ar) | copy-start | bytes 3145732
  38.4 1.0 %copy-start.1 = (f32[32,8192]{1,0:T(8,128)}, f32[32,8192]{1,0:T(8,128)S(1)}, u32[]{:S(2)}) copy-start(f32[32,8192]{1,0:T(8,128)S(1)} %collective-permute-done.1.bm.bl.br) | copy-start | bytes 3145732

commit v4 on v3

--- a/solution.py
+++ b/solution.py
@@ -11,7 +11,7 @@
 
 HR = 8
 HC = 128
-BW = 1024
+BW = 2048
 INTERPRET = False
 
 
@@ -34,12 +34,7 @@
 
     degrade = (1.0 - dmg) ** 2 + 0.001
 
-    def accel(w0, w1, z0, z1):
-        eu = strain(w0, w1)
-        ev = strain(z0, z1)
-        exx = eu[0] + 0.5 * ev[0]
-        eyy = eu[1] + 0.5 * ev[1]
-        exy = eu[2] + 0.5 * ev[2]
+    def accel(exx, eyy, exy):
         trace = exx + eyy
         sxx = jnp.where(valid, degrade * (trace + 2.0 * exx), zero)
         syy = jnp.where(valid, degrade * (trace + 2.0 * eyy), zero)
@@ -48,15 +43,16 @@
         a1 = ((sh(sxy, 1, 0) - sh(sxy, -1, 0)) + (sh(syy, 1, 1) - sh(syy, -1, 1))) * 0.5
         return a0, a1
 
-    a0, a1 = accel(u0, u1, v0, v1)
+    a0, a1 = accel(*strain(u0 + 0.5 * v0, u1 + 0.5 * v1))
     h0 = jnp.where(valid, v0 + 0.1 * a0, zero)
     h1 = jnp.where(valid, v1 + 0.1 * a1, zero)
     n0 = jnp.where(valid, u0 + 0.2 * h0, zero)
     n1 = jnp.where(valid, u1 + 0.2 * h1, zero)
-    b0, b1 = accel(n0, n1, h0, h1)
+    e = strain(n0, n1)
+    eh = strain(h0, h1)
+    b0, b1 = accel(e[0] + 0.5 * eh[0], e[1] + 0.5 * eh[1], e[2] + 0.5 * eh[2])
     vel0 = h0 + 0.1 * b0
     vel1 = h1 + 0.1 * b1
-    e = strain(n0, n1)
     tr = jnp.maximum(e[0] + e[1], 0.0)
     hist_new = jnp.maximum(hist, 0.5 * tr * tr + e[0] * e[0] + e[1] * e[1] + 2.0 * e[2] * e[2])
 
@@ -65,12 +61,12 @@
     k_right = tough + sh(tough, 1, 1)
     k_left = tough + sh(tough, -1, 1)
     two_h = 2.0 * hist_new
-    denom = tough * 0.5 + two_h + k_down + k_up + k_right + k_left
+    inv_denom = 1.0 / (tough * 0.5 + two_h + k_down + k_up + k_right + k_left)
 
     def jacobi(f):
         numer = two_h + k_down * sh(f, 1, 0) + k_up * sh(f, -1, 0)
         numer = numer + k_right * sh(f, 1, 1) + k_left * sh(f, -1, 1)
-        return numer / denom
+        return numer * inv_denom
 
     d1 = jnp.where(valid, jacobi(dmg), zero)
     d2 = jnp.where(valid, dmg + WEIGHT_TWO * (jacobi(d1) - dmg), zero)
@@ -108,15 +104,17 @@
         du, dv, dd, dh, dt = refs
         return [du[0], du[1], dv[0], dv[1], dd[...], dh[...], dt[...]]
 
+    pw = cols
+
     def pack_kernel(pos_ref, tu, tv, td, th, tt, bu, bv, bd, bh, bt,
                     lu, lv, ld, lh, lt, ru, rv, rd, rh, rt, top_o, bot_o, col_o):
         j = pl.program_id(0)
         tops = split((tu, tv, td, th, tt))
         bots = split((bu, bv, bd, bh, bt))
-        ridx = lax.broadcasted_iota(jnp.int32, (STRIP, BW), 0)
-        top = jnp.zeros((STRIP, BW), f32)
-        bot = jnp.zeros((STRIP, BW), f32)
-        pad = jnp.zeros((STRIP - 8, BW), f32)
+        ridx = lax.broadcasted_iota(jnp.int32, (STRIP, pw), 0)
+        top = jnp.zeros((STRIP, pw), f32)
+        bot = jnp.zeros((STRIP, pw), f32)
+        pad = jnp.zeros((STRIP - 8, pw), f32)
         for k in range(nf):
             r, o = RADII[k], OFFSETS[k]
             inside = (ridx >= o) & (ridx < o + r)
@@ -141,10 +139,10 @@
                 col = jnp.where(inside, jnp.where(to_right, a, b), col)
             col_o[...] = col
 
-    t2 = pl.BlockSpec((2, 8, BW), lambda j: (0, 0, j))
-    t1 = pl.BlockSpec((8, BW), lambda j: (0, j))
-    b2 = pl.BlockSpec((2, 8, BW), lambda j: (0, last_row_block, j))
-    b1 = pl.BlockSpec((8, BW), lambda j: (last_row_block, j))
+    t2 = pl.BlockSpec((2, 8, pw), lambda j: (0, 0, j))
+    t1 = pl.BlockSpec((8, pw), lambda j: (0, j))
+    b2 = pl.BlockSpec((2, 8, pw), lambda j: (0, last_row_block, j))
+    b1 = pl.BlockSpec((8, pw), lambda j: (last_row_block, j))
     l2 = pl.BlockSpec((2, rows, HC), lambda j: (0, 0, 0))
     l1 = pl.BlockSpec((rows, HC), lambda j: (0, 0))
     r2 = pl.BlockSpec((2, rows, HC), lambda j: (0, 0, last_col_block))
@@ -153,9 +151,9 @@
     ins = (displacement, velocity, damage, history, toughness)
     top_s, bot_s, col_s = pl.pallas_call(
         pack_kernel,
-        grid=(nblocks,),
+        grid=(cols // pw,),
         in_specs=[smem, t2, t2, t1, t1, t1, b2, b2, b1, b1, b1, l2, l2, l1, l1, l1, r2, r2, r1, r1, r1],
-        out_specs=[pl.BlockSpec((STRIP, BW), lambda j: (0, j)), pl.BlockSpec((STRIP, BW), lambda j: (0, j)),
+        out_specs=[pl.BlockSpec((STRIP, pw), lambda j: (0, j)), pl.BlockSpec((STRIP, pw), lambda j: (0, j)),
                    pl.BlockSpec((rows, HC), lambda j: (0, 0))],
         out_shape=[jax.ShapeDtypeStruct((STRIP, cols), f32), jax.ShapeDtypeStruct((STRIP, cols), f32),
                    jax.ShapeDtypeStruct((rows, HC), f32)],

time: 67.7 us -> 60 us (0.89)
  Pallas kernels: 33.3 us -> 25.9 us
    pallas_call x1, Pallas kernels: 27 us -> 22.1 us  [on_device(): pl.pallas_call(kernel, grid=(nblocks,), in_specs=[smem, main2, left2, rig...]
    pallas_call x1, Pallas kernels: 6.26 us -> 3.78 us  [on_device(): pl.pallas_call(pack_kernel, grid=(cols // pw,), in_specs=[smem, t2, t2, t...]
where the time goes in v4:
time: 60 us; the launch traced here: 59 us
  Pallas kernels  25.9 us (43%)
  starting transfers between devices  14.8 us (25%)
  waiting for transfers between devices  14.3 us (24%)
  local copies, waits for them, and re-layouts  2.67 us (4%)
  between operations  0.7 us (1%)
  other arithmetic  0.61 us (1%)
    pallas_call x1, Pallas kernels, on_device(): pl.pallas_call(kernel, grid=(nblocks,), in_specs=[smem, main2, left2, rig...  22.1 us
    ppermute x1, waiting for transfers between devices, on_device(): lax.ppermute(col_s[:8], both, [((i + 1) * 2 + g, i * 2 + 1 - g) for i in...  9.58 us
    ppermute x1, starting transfers between devices, on_device(): above = lax.ppermute(bot_s, 'gx', [(i, i + 1) for i in range(nx - 1)])  5.21 us
    ppermute x1, starting transfers between devices, on_device(): lax.ppermute(col_s[:8], both, [((i + 1) * 2 + g, i * 2 + 1 - g) for i in...  4.72 us
    ppermute x1, waiting for transfers between devices, on_device(): lax.ppermute(col_s[rows - 8:], both, [(i * 2 + g, (i + 1) * 2 + 1 - g) fo...  4.69 us
    pallas_call x1, Pallas kernels, on_device(): pl.pallas_call(pack_kernel, grid=(cols // pw,), in_specs=[smem, t2, t2, t...  3.78 us
    ppermute x1, starting transfers between devices, on_device(): lax.ppermute(col_s[rows - 8:], both, [(i * 2 + g, (i + 1) * 2 + 1 - g) fo...  2.58 us
    unnamed x10, local copies, waits for them, and re-layouts  1.95 us
  transfers between devices with their start and end apart: 5, of which 2 were waited for; matrix products, arithmetic and copies ran while one was open for 1% of the time, Pallas kernels for 0%

profile of v4, /device:TPU:89, one launch (start us, length us, event | category | flops | bytes accessed | tf_op | source)
XLA Modules:
  0.0 59.0 jit_solution(17435974525743540119)
XLA Ops:
  0.6 0.6 %pad_add_fusion.pos_ref = s32[2]{0:T(128)} fusion(s32[1]{0:T(128)} %bitcast.1, s32[1]{0:T(128)} %bitcast), kind=kLoop, calls=%fused_computation | loop fusion | flops 2 | bytes 16 | tf_op jit(solution)/shard_map/stack | solution.py:92
  1.2 3.8 %shard_map.84 = (f32[32,8192]{1,0:T(8,128)}, f32[32,8192]{1,0:T(8,128)}, f32[32,128]{1,0:T(8,128)}) custom-call(s32[2]{0:T(128)} %pad_add_fusion.pos_ref, f32[2,32,8192]{2,1,0:T(8,128)} %ur.1, f32[2,32,8192]{2,1,0:T(8,128)} %vr.1, f32[32,8192]{1,0:T(8,128)} %dr.1, f32[32,8192]{1,0:T(8,128)} %hr.1, f32[32,8192]{1,0:T(8,128)} %tr.1, f32[2,32,8192]{2,1,0:T(8,128)} %ur.1, ...), custom_call_target="tpu_custom_call" | custom-call | tf_op jit(solution)/shard_map/pallas_call | solution.py:152
  5.0 5.2 %collective-permute-start = (f32[32,8192]{1,0:T(8,128)}, f32[32,8192]{1,0:T(8,128)S(1)}, u32[]{:S(2)}, u32[]{:S(2)}) collective-permute-start(f32[32,8192]{1,0:T(8,128)} %get-tuple-element.7), channel_id=1, source_target_pairs={{0,2},{2,4},{4,6},{6,8},{8,10},{10,12},{12,14},{14,16},{16,18},{18... | collective-permute-start | bytes 3145736 | tf_op jit(solution)/shard_map/ppermute | solution.py:163
  10.2 1.9 %collective-permute-start.1 = (f32[32,8192]{1,0:T(8,128)}, f32[32,8192]{1,0:T(8,128)S(1)}, u32[]{:S(2)}, u32[]{:S(2)}) collective-permute-start(f32[32,8192]{1,0:T(8,128)} %get-tuple-element.8), channel_id=1, source_target_pairs={{2,0},{4,2},{6,4},{8,6},{10,8},{12,10},{14,12},{16,14},{18,16},{20... | collective-permute-start | bytes 3145736 | tf_op jit(solution)/shard_map/ppermute | solution.py:164
  12.2 0.4 collective-permute-start.2
  12.6 0.7 %fusion = (f32[8,128]{1,0:T(8,128)S(1)}, f32[8,128]{1,0:T(8,128)S(1)}) fusion(f32[32,128]{1,0:T(8,128)} %get-tuple-element.9), kind=kLoop, calls=%fused_computation.1 | loop fusion | bytes 16384 | tf_op jit(solution)/shard_map/slice | solution.py:169
  13.3 4.7 %collective-permute-start.4 = (f32[8,128]{1,0:T(8,128)S(1)}, f32[8,128]{1,0:T(8,128)S(1)}, u32[]{:S(2)}, u32[]{:S(2)}) collective-permute-start(f32[8,128]{1,0:T(8,128)S(1)} %get-tuple-element.10), channel_id=1, source_target_pairs={{2,1},{3,0},{4,3},{5,2},{6,5},{7,4},{8,7},{9,6},{10,9},{11,8},{12,... | collective-permute-start | bytes 12296 | tf_op jit(solution)/shard_map/ppermute | solution.py:169
  18.0 2.6 %collective-permute-start.3 = (f32[8,128]{1,0:T(8,128)S(1)}, f32[8,128]{1,0:T(8,128)S(1)}, u32[]{:S(2)}, u32[]{:S(2)}) collective-permute-start(f32[8,128]{1,0:T(8,128)S(1)} %get-tuple-element.11), channel_id=1, source_target_pairs={{0,3},{1,2},{2,5},{3,4},{4,7},{5,6},{6,9},{7,8},{8,11},{9,10},{10,... | collective-permute-start | bytes 12296 | tf_op jit(solution)/shard_map/ppermute | solution.py:167
  20.6 9.6 %collective-permute-done.4.cb_ref = f32[8,128]{1,0:T(8,128)S(1)} collective-permute-done((f32[8,128]{1,0:T(8,128)S(1)}, f32[8,128]{1,0:T(8,128)S(1)}, u32[]{:S(2)}, u32[]{:S(2)}) %collective-permute-start.4) | collective-permute-done | bytes 4128 | tf_op jit(solution)/shard_map/ppermute | solution.py:169
  30.2 0.0 copy-start.3
  30.2 4.7 %collective-permute-done.3.ca_ref = f32[8,128]{1,0:T(8,128)S(1)} collective-permute-done((f32[8,128]{1,0:T(8,128)S(1)}, f32[8,128]{1,0:T(8,128)S(1)}, u32[]{:S(2)}, u32[]{:S(2)}) %collective-permute-start.3) | collective-permute-done | bytes 4128 | tf_op jit(solution)/shard_map/ppermute | solution.py:167
  34.9 0.0 copy-start.4
  34.9 0.0 collective-permute-done.2.side_ref
  34.9 0.0 copy-start.2
  34.9 0.0 collective-permute-done.am.al.ar
  34.9 0.0 copy-start
  34.9 0.0 collective-permute-done.1.bm.bl.br
  34.9 0.0 copy-done.3
  34.9 0.5 copy-done.4
  35.5 0.0 copy-done.2
  35.5 0.4 copy-done
  35.9 0.0 copy-start.1
  35.9 1.0 %copy-done.1 = f32[32,8192]{1,0:T(8,128)} copy-done((f32[32,8192]{1,0:T(8,128)}, f32[32,8192]{1,0:T(8,128)S(1)}, u32[]{:S(2)}) %copy-start.1) | copy-done | bytes 1048600
  36.9 22.1 %shard_map.85 = (f32[2,32,8192]{2,1,0:T(8,128)}, f32[2,32,8192]{2,1,0:T(8,128)}, f32[32,8192]{1,0:T(8,128)}, f32[32,8192]{1,0:T(8,128)}) custom-call(s32[2]{0:T(128)} %pad_add_fusion.pos_ref, f32[2,32,8192]{2,1,0:T(8,128)} %ur.1, f32[2,32,8192]{2,1,0:T(8,128)} %ur.1, f32[2,32,8192]{2,1,0:T(8,128)} %ur.1, f32[2,32,8192]{2,1,0:T(8,128)} %vr.1, ...), custom_call_target="tpu_custom_call" | custom-call | tf_op jit(solution)/shard_map/pallas_call | solution.py:259
Async XLA Ops:
  5.0 29.9 %collective-permute-start = (f32[32,8192]{1,0:T(8,128)}, f32[32,8192]{1,0:T(8,128)S(1)}, u32[]{:S(2)}, u32[]{:S(2)}) collective-permute-start(f32[32,8192]{1,0:T(8,128)} %get-tuple-element.7), channel_id=1, source_target_pairs={{0,2},{2,4},{4,6},{6,8},{8,10},{10,12},{12,14},{14,16},{16,18},{18... | collective-permute-start | bytes 3145736 | tf_op jit(solution)/shard_map/ppermute | solution.py:163
  10.2 24.7 %collective-permute-start.1 = (f32[32,8192]{1,0:T(8,128)}, f32[32,8192]{1,0:T(8,128)S(1)}, u32[]{:S(2)}, u32[]{:S(2)}) collective-permute-start(f32[32,8192]{1,0:T(8,128)} %get-tuple-element.8), channel_id=1, source_target_pairs={{2,0},{4,2},{6,4},{8,6},{10,8},{12,10},{14,12},{16,14},{18,16},{20... | collective-permute-start | bytes 3145736 | tf_op jit(solution)/shard_map/ppermute | solution.py:164
  12.2 22.7 %collective-permute-start.2 = (f32[32,128]{1,0:T(8,128)}, f32[32,128]{1,0:T(8,128)S(1)}, u32[]{:S(2)}, u32[]{:S(2)}) collective-permute-start(f32[32,128]{1,0:T(8,128)} %get-tuple-element.9), channel_id=1, source_target_pairs={{0,1},{1,0},{2,3},{3,2},{4,5},{5,4},{6,7},{7,6},{8,9},{9,8},{10,11... | collective-permute-start | bytes 49160 | tf_op jit(solution)/shard_map/ppermute | solution.py:165
  13.3 16.9 %collective-permute-start.4 = (f32[8,128]{1,0:T(8,128)S(1)}, f32[8,128]{1,0:T(8,128)S(1)}, u32[]{:S(2)}, u32[]{:S(2)}) collective-permute-start(f32[8,128]{1,0:T(8,128)S(1)} %get-tuple-element.10), channel_id=1, source_target_pairs={{2,1},{3,0},{4,3},{5,2},{6,5},{7,4},{8,7},{9,6},{10,9},{11,8},{12,... | collective-permute-start | bytes 12296 | tf_op jit(solution)/shard_map/ppermute | solution.py:169
  18.0 16.9 %collective-permute-start.3 = (f32[8,128]{1,0:T(8,128)S(1)}, f32[8,128]{1,0:T(8,128)S(1)}, u32[]{:S(2)}, u32[]{:S(2)}) collective-permute-start(f32[8,128]{1,0:T(8,128)S(1)} %get-tuple-element.11), channel_id=1, source_target_pairs={{0,3},{1,2},{2,5},{3,4},{4,7},{5,6},{6,9},{7,8},{8,11},{9,10},{10,... | collective-permute-start | bytes 12296 | tf_op jit(solution)/shard_map/ppermute | solution.py:167
  30.2 4.7 %copy-start.3 = (f32[8,128]{1,0:T(8,128)}, f32[8,128]{1,0:T(8,128)S(1)}, u32[]{:S(2)}) copy-start(f32[8,128]{1,0:T(8,128)S(1)} %collective-permute-done.4.cb_ref) | copy-start | bytes 12292
  34.9 0.6 %copy-start.4 = (f32[8,128]{1,0:T(8,128)}, f32[8,128]{1,0:T(8,128)S(1)}, u32[]{:S(2)}) copy-start(f32[8,128]{1,0:T(8,128)S(1)} %collective-permute-done.3.ca_ref) | copy-start | bytes 12292
  34.9 0.6 %copy-start.2 = (f32[32,128]{1,0:T(8,128)}, f32[32,128]{1,0:T(8,128)S(1)}, u32[]{:S(2)}) copy-start(f32[32,128]{1,0:T(8,128)S(1)} %collective-permute-done.2.side_ref) | copy-start | bytes 49156
  34.9 1.0 %copy-start = (f32[32,8192]{1,0:T(8,128)}, f32[32,8192]{1,0:T(8,128)S(1)}, u32[]{:S(2)}) copy-start(f32[32,8192]{1,0:T(8,128)S(1)} %collective-permute-done.am.al.ar) | copy-start | bytes 3145732
  35.9 1.0 %copy-start.1 = (f32[32,8192]{1,0:T(8,128)}, f32[32,8192]{1,0:T(8,128)S(1)}, u32[]{:S(2)}) copy-start(f32[32,8192]{1,0:T(8,128)S(1)} %collective-permute-done.1.bm.bl.br) | copy-start | bytes 3145732

commit v5 on v4

--- a/solution.py
+++ b/solution.py
@@ -11,7 +11,7 @@
 
 HR = 8
 HC = 128
-BW = 2048
+BW = 4096
 INTERPRET = False
 
 
@@ -111,17 +111,23 @@
         j = pl.program_id(0)
         tops = split((tu, tv, td, th, tt))
         bots = split((bu, bv, bd, bh, bt))
-        ridx = lax.broadcasted_iota(jnp.int32, (STRIP, pw), 0)
-        top = jnp.zeros((STRIP, pw), f32)
-        bot = jnp.zeros((STRIP, pw), f32)
-        pad = jnp.zeros((STRIP - 8, pw), f32)
-        for k in range(nf):
-            r, o = RADII[k], OFFSETS[k]
-            inside = (ridx >= o) & (ridx < o + r)
-            x = roll(jnp.concatenate([tops[k], pad], axis=0), o, 0)
-            top = jnp.where(inside, x, top)
-            y = roll(jnp.concatenate([bots[k], pad], axis=0), o - (8 - r), 0)
-            bot = jnp.where(inside, y, bot)
+        sidx = lax.broadcasted_iota(jnp.int32, (8, pw), 0)
+        top_groups, bot_groups = [], []
+        for g in range(STRIP // 8):
+            top = jnp.zeros((8, pw), f32)
+            bot = jnp.zeros((8, pw), f32)
+            for k in range(nf):
+                r, o = RADII[k], OFFSETS[k]
+                lo, hi = o - 8 * g, o - 8 * g + r
+                if hi <= 0 or lo >= 8:
+                    continue
+                inside = (sidx >= lo) & (sidx < hi)
+                top = jnp.where(inside, roll(tops[k], lo, 0), top)
+                bot = jnp.where(inside, roll(bots[k], lo - (8 - r), 0), bot)
+            top_groups.append(top)
+            bot_groups.append(bot)
+        top = jnp.concatenate(top_groups, axis=0)
+        bot = jnp.concatenate(bot_groups, axis=0)
         top_o[...] = top
         bot_o[...] = bot
 
@@ -193,17 +199,22 @@
             y = roll(x, -LANE_W * k, 1)
             return jnp.where((lidx < LANE_W) & has_right, y, 0.0)
 
+        def from_groups(x, k, first_row):
+            r, o = RADII[k], OFFSETS[k]
+            sidx = lax.broadcasted_iota(jnp.int32, (8,) + x.shape[1:], 0)
+            out = jnp.zeros((8,) + x.shape[1:], x.dtype)
+            for g in range(o // 8, (o + r - 1) // 8 + 1):
+                shift = first_row - o + 8 * g
+                src_row = sidx - shift
+                inside = (sidx >= first_row) & (sidx < first_row + r) & (src_row >= 0) & (src_row < 8)
+                out = jnp.where(inside, roll(x[8 * g:8 * g + 8], shift % 8, 0), out)
+            return out
+
         def above_tile(x, k):
-            r, o = RADII[k], OFFSETS[k]
-            y = roll(x, 8 - r - o, 0)[:8]
-            ridx = lax.broadcasted_iota(jnp.int32, y.shape, 0)
-            return jnp.where(ridx >= 8 - r, y, 0.0)
+            return from_groups(x, k, 8 - RADII[k])
 
         def below_tile(x, k):
-            r, o = RADII[k], OFFSETS[k]
-            y = roll(x, -o, 0)[:8]
-            ridx = lax.broadcasted_iota(jnp.int32, y.shape, 0)
-            return jnp.where(ridx < r, y, 0.0)
+            return from_groups(x, k, 0)
 
         a_m, a_l, a_r = am[...], al[...], ar[...]
         b_m, b_l, b_r = bm[...], bl[...], br[...]

time: 60 us -> 60.5 us (level)
  no operation moved by 1% of the time
where the time goes in v5:
time: 60.5 us; the launch traced here: 59.5 us
  Pallas kernels  26.4 us (44%)
  starting transfers between devices  14.8 us (24%)
  waiting for transfers between devices  14.3 us (24%)
  local copies, waits for them, and re-layouts  2.67 us (4%)
  between operations  0.7 us (1%)
  other arithmetic  0.61 us (1%)
    pallas_call x1, Pallas kernels, on_device(): pl.pallas_call(kernel, grid=(nblocks,), in_specs=[smem, main2, left2, rig...  22.7 us
    ppermute x1, waiting for transfers between devices, on_device(): lax.ppermute(col_s[:8], both, [((i + 1) * 2 + g, i * 2 + 1 - g) for i in...  9.58 us
    ppermute x1, starting transfers between devices, on_device(): above = lax.ppermute(bot_s, 'gx', [(i, i + 1) for i in range(nx - 1)])  5.21 us
    ppermute x1, starting transfers between devices, on_device(): lax.ppermute(col_s[:8], both, [((i + 1) * 2 + g, i * 2 + 1 - g) for i in...  4.72 us
    ppermute x1, waiting for transfers between devices, on_device(): lax.ppermute(col_s[rows - 8:], both, [(i * 2 + g, (i + 1) * 2 + 1 - g) fo...  4.69 us
    pallas_call x1, Pallas kernels, on_device(): pl.pallas_call(pack_kernel, grid=(cols // pw,), in_specs=[smem, t2, t2, t...  3.67 us
    ppermute x1, starting transfers between devices, on_device(): lax.ppermute(col_s[rows - 8:], both, [(i * 2 + g, (i + 1) * 2 + 1 - g) fo...  2.58 us
    unnamed x10, local copies, waits for them, and re-layouts  1.95 us
  transfers between devices with their start and end apart: 5, of which 2 were waited for; matrix products, arithmetic and copies ran while one was open for 1% of the time, Pallas kernels for 0%

profile of v5, /device:TPU:89, one launch (start us, length us, event | category | flops | bytes accessed | tf_op | source)
XLA Modules:
  0.0 59.5 jit_solution(11131919406386765588)
XLA Ops:
  0.6 0.6 %pad_add_fusion.pos_ref = s32[2]{0:T(128)} fusion(s32[1]{0:T(128)} %bitcast.1, s32[1]{0:T(128)} %bitcast), kind=kLoop, calls=%fused_computation | loop fusion | flops 2 | bytes 16 | tf_op jit(solution)/shard_map/stack | solution.py:92
  1.2 3.7 %shard_map.84 = (f32[32,8192]{1,0:T(8,128)}, f32[32,8192]{1,0:T(8,128)}, f32[32,128]{1,0:T(8,128)}) custom-call(s32[2]{0:T(128)} %pad_add_fusion.pos_ref, f32[2,32,8192]{2,1,0:T(8,128)} %ur.1, f32[2,32,8192]{2,1,0:T(8,128)} %vr.1, f32[32,8192]{1,0:T(8,128)} %dr.1, f32[32,8192]{1,0:T(8,128)} %hr.1, f32[32,8192]{1,0:T(8,128)} %tr.1, f32[2,32,8192]{2,1,0:T(8,128)} %ur.1, ...), custom_call_target="tpu_custom_call" | custom-call | tf_op jit(solution)/shard_map/pallas_call | solution.py:158
  4.9 5.2 %collective-permute-start = (f32[32,8192]{1,0:T(8,128)}, f32[32,8192]{1,0:T(8,128)S(1)}, u32[]{:S(2)}, u32[]{:S(2)}) collective-permute-start(f32[32,8192]{1,0:T(8,128)} %get-tuple-element.7), channel_id=1, source_target_pairs={{0,2},{2,4},{4,6},{6,8},{8,10},{10,12},{12,14},{14,16},{16,18},{18... | collective-permute-start | bytes 3145736 | tf_op jit(solution)/shard_map/ppermute | solution.py:169
  10.1 1.9 %collective-permute-start.1 = (f32[32,8192]{1,0:T(8,128)}, f32[32,8192]{1,0:T(8,128)S(1)}, u32[]{:S(2)}, u32[]{:S(2)}) collective-permute-start(f32[32,8192]{1,0:T(8,128)} %get-tuple-element.8), channel_id=1, source_target_pairs={{2,0},{4,2},{6,4},{8,6},{10,8},{12,10},{14,12},{16,14},{18,16},{20... | collective-permute-start | bytes 3145736 | tf_op jit(solution)/shard_map/ppermute | solution.py:170
  12.1 0.4 collective-permute-start.2
  12.5 0.7 %fusion = (f32[8,128]{1,0:T(8,128)S(1)}, f32[8,128]{1,0:T(8,128)S(1)}) fusion(f32[32,128]{1,0:T(8,128)} %get-tuple-element.9), kind=kLoop, calls=%fused_computation.1 | loop fusion | bytes 16384 | tf_op jit(solution)/shard_map/slice | solution.py:175
  13.2 4.7 %collective-permute-start.4 = (f32[8,128]{1,0:T(8,128)S(1)}, f32[8,128]{1,0:T(8,128)S(1)}, u32[]{:S(2)}, u32[]{:S(2)}) collective-permute-start(f32[8,128]{1,0:T(8,128)S(1)} %get-tuple-element.10), channel_id=1, source_target_pairs={{2,1},{3,0},{4,3},{5,2},{6,5},{7,4},{8,7},{9,6},{10,9},{11,8},{12,... | collective-permute-start | bytes 12296 | tf_op jit(solution)/shard_map/ppermute | solution.py:175
  17.9 2.6 %collective-permute-start.3 = (f32[8,128]{1,0:T(8,128)S(1)}, f32[8,128]{1,0:T(8,128)S(1)}, u32[]{:S(2)}, u32[]{:S(2)}) collective-permute-start(f32[8,128]{1,0:T(8,128)S(1)} %get-tuple-element.11), channel_id=1, source_target_pairs={{0,3},{1,2},{2,5},{3,4},{4,7},{5,6},{6,9},{7,8},{8,11},{9,10},{10,... | collective-permute-start | bytes 12296 | tf_op jit(solution)/shard_map/ppermute | solution.py:173
  20.5 9.6 %collective-permute-done.4.cb_ref = f32[8,128]{1,0:T(8,128)S(1)} collective-permute-done((f32[8,128]{1,0:T(8,128)S(1)}, f32[8,128]{1,0:T(8,128)S(1)}, u32[]{:S(2)}, u32[]{:S(2)}) %collective-permute-start.4) | collective-permute-done | bytes 4128 | tf_op jit(solution)/shard_map/ppermute | solution.py:175
  30.1 0.0 copy-start.3
  30.1 4.7 %collective-permute-done.3.ca_ref = f32[8,128]{1,0:T(8,128)S(1)} collective-permute-done((f32[8,128]{1,0:T(8,128)S(1)}, f32[8,128]{1,0:T(8,128)S(1)}, u32[]{:S(2)}, u32[]{:S(2)}) %collective-permute-start.3) | collective-permute-done | bytes 4128 | tf_op jit(solution)/shard_map/ppermute | solution.py:173
  34.8 0.0 copy-start.4
  34.8 0.0 collective-permute-done.2.side_ref
  34.8 0.0 copy-start.2
  34.8 0.0 collective-permute-done.am.al.ar
  34.8 0.0 copy-start
  34.8 0.0 collective-permute-done.1.bm.bl.br
  34.8 0.0 copy-done.3
  34.8 0.5 copy-done.4
  35.4 0.0 copy-done.2
  35.4 0.4 copy-done
  35.8 0.0 copy-start.1
  35.8 1.0 %copy-done.1 = f32[32,8192]{1,0:T(8,128)} copy-done((f32[32,8192]{1,0:T(8,128)}, f32[32,8192]{1,0:T(8,128)S(1)}, u32[]{:S(2)}) %copy-start.1) | copy-done | bytes 1048600
  36.8 22.7 %shard_map.85 = (f32[2,32,8192]{2,1,0:T(8,128)}, f32[2,32,8192]{2,1,0:T(8,128)}, f32[32,8192]{1,0:T(8,128)}, f32[32,8192]{1,0:T(8,128)}) custom-call(s32[2]{0:T(128)} %pad_add_fusion.pos_ref, f32[2,32,8192]{2,1,0:T(8,128)} %ur.1, f32[2,32,8192]{2,1,0:T(8,128)} %ur.1, f32[2,32,8192]{2,1,0:T(8,128)} %ur.1, f32[2,32,8192]{2,1,0:T(8,128)} %vr.1, ...), custom_call_target="tpu_custom_call" | custom-call | tf_op jit(solution)/shard_map/pallas_call | solution.py:270
Async XLA Ops:
  4.9 29.9 %collective-permute-start = (f32[32,8192]{1,0:T(8,128)}, f32[32,8192]{1,0:T(8,128)S(1)}, u32[]{:S(2)}, u32[]{:S(2)}) collective-permute-start(f32[32,8192]{1,0:T(8,128)} %get-tuple-element.7), channel_id=1, source_target_pairs={{0,2},{2,4},{4,6},{6,8},{8,10},{10,12},{12,14},{14,16},{16,18},{18... | collective-permute-start | bytes 3145736 | tf_op jit(solution)/shard_map/ppermute | solution.py:169
  10.1 24.7 %collective-permute-start.1 = (f32[32,8192]{1,0:T(8,128)}, f32[32,8192]{1,0:T(8,128)S(1)}, u32[]{:S(2)}, u32[]{:S(2)}) collective-permute-start(f32[32,8192]{1,0:T(8,128)} %get-tuple-element.8), channel_id=1, source_target_pairs={{2,0},{4,2},{6,4},{8,6},{10,8},{12,10},{14,12},{16,14},{18,16},{20... | collective-permute-start | bytes 3145736 | tf_op jit(solution)/shard_map/ppermute | solution.py:170
  12.1 22.7 %collective-permute-start.2 = (f32[32,128]{1,0:T(8,128)}, f32[32,128]{1,0:T(8,128)S(1)}, u32[]{:S(2)}, u32[]{:S(2)}) collective-permute-start(f32[32,128]{1,0:T(8,128)} %get-tuple-element.9), channel_id=1, source_target_pairs={{0,1},{1,0},{2,3},{3,2},{4,5},{5,4},{6,7},{7,6},{8,9},{9,8},{10,11... | collective-permute-start | bytes 49160 | tf_op jit(solution)/shard_map/ppermute | solution.py:171
  13.2 16.9 %collective-permute-start.4 = (f32[8,128]{1,0:T(8,128)S(1)}, f32[8,128]{1,0:T(8,128)S(1)}, u32[]{:S(2)}, u32[]{:S(2)}) collective-permute-start(f32[8,128]{1,0:T(8,128)S(1)} %get-tuple-element.10), channel_id=1, source_target_pairs={{2,1},{3,0},{4,3},{5,2},{6,5},{7,4},{8,7},{9,6},{10,9},{11,8},{12,... | collective-permute-start | bytes 12296 | tf_op jit(solution)/shard_map/ppermute | solution.py:175
  17.9 16.9 %collective-permute-start.3 = (f32[8,128]{1,0:T(8,128)S(1)}, f32[8,128]{1,0:T(8,128)S(1)}, u32[]{:S(2)}, u32[]{:S(2)}) collective-permute-start(f32[8,128]{1,0:T(8,128)S(1)} %get-tuple-element.11), channel_id=1, source_target_pairs={{0,3},{1,2},{2,5},{3,4},{4,7},{5,6},{6,9},{7,8},{8,11},{9,10},{10,... | collective-permute-start | bytes 12296 | tf_op jit(solution)/shard_map/ppermute | solution.py:173
  30.1 4.7 %copy-start.3 = (f32[8,128]{1,0:T(8,128)}, f32[8,128]{1,0:T(8,128)S(1)}, u32[]{:S(2)}) copy-start(f32[8,128]{1,0:T(8,128)S(1)} %collective-permute-done.4.cb_ref) | copy-start | bytes 12292
  34.8 0.6 copy-start.4
  34.8 0.6 %copy-start.2 = (f32[32,128]{1,0:T(8,128)}, f32[32,128]{1,0:T(8,128)S(1)}, u32[]{:S(2)}) copy-start(f32[32,128]{1,0:T(8,128)S(1)} %collective-permute-done.2.side_ref) | copy-start | bytes 49156
  34.8 1.0 %copy-start = (f32[32,8192]{1,0:T(8,128)}, f32[32,8192]{1,0:T(8,128)S(1)}, u32[]{:S(2)}) copy-start(f32[32,8192]{1,0:T(8,128)S(1)} %collective-permute-done.am.al.ar) | copy-start | bytes 3145732
  35.8 1.0 %copy-start.1 = (f32[32,8192]{1,0:T(8,128)}, f32[32,8192]{1,0:T(8,128)S(1)}, u32[]{:S(2)}) copy-start(f32[32,8192]{1,0:T(8,128)S(1)} %collective-permute-done.1.bm.bl.br) | copy-start | bytes 3145732

commit v6 on v4

--- a/solution.py
+++ b/solution.py
@@ -1,3 +1,5 @@
+import functools
+
 import jax
 import jax.numpy as jnp
 from jax import lax
@@ -86,7 +88,7 @@
     ny = lax.axis_size("gy")
     ix = lax.axis_index("gx")
     iy = lax.axis_index("gy")
-    assert ny == 2 and rows % 8 == 0 and cols % BW == 0
+    assert ny == 2 and rows % 8 == 0 and cols % (2 * BW) == 0
     total_rows, total_cols = rows * nx, cols * ny
     nf = len(RADII)
     pos = jnp.stack([ix, iy]).astype(jnp.int32)
@@ -105,9 +107,11 @@
         return [du[0], du[1], dv[0], dv[1], dd[...], dh[...], dt[...]]
 
     pw = cols
+    half = cols // 2
+    off = half // HC
 
     def pack_kernel(pos_ref, tu, tv, td, th, tt, bu, bv, bd, bh, bt,
-                    lu, lv, ld, lh, lt, ru, rv, rd, rh, rt, top_o, bot_o, col_o):
+                    lu, lv, ld, lh, lt, ru, rv, rd, rh, rt, top0_o, top1_o, bot0_o, bot1_o, col_o):
         j = pl.program_id(0)
         tops = split((tu, tv, td, th, tt))
         bots = split((bu, bv, bd, bh, bt))
@@ -122,8 +126,10 @@
             top = jnp.where(inside, x, top)
             y = roll(jnp.concatenate([bots[k], pad], axis=0), o - (8 - r), 0)
             bot = jnp.where(inside, y, bot)
-        top_o[...] = top
-        bot_o[...] = bot
+        top0_o[...] = top[:, :half + HC]
+        top1_o[...] = top[:, half:]
+        bot0_o[...] = bot[:, :half + HC]
+        bot1_o[...] = bot[:, half:]
 
         @pl.when(j == 0)
         def _():
@@ -149,29 +155,38 @@
     r1 = pl.BlockSpec((rows, HC), lambda j: (0, last_col_block))
     smem = pl.BlockSpec(memory_space=pltpu.SMEM)
     ins = (displacement, velocity, damage, history, toughness)
-    top_s, bot_s, col_s = pl.pallas_call(
+    top0, top1, bot0, bot1, col_s = pl.pallas_call(
         pack_kernel,
         grid=(cols // pw,),
         in_specs=[smem, t2, t2, t1, t1, t1, b2, b2, b1, b1, b1, l2, l2, l1, l1, l1, r2, r2, r1, r1, r1],
-        out_specs=[pl.BlockSpec((STRIP, pw), lambda j: (0, j)), pl.BlockSpec((STRIP, pw), lambda j: (0, j)),
+        out_specs=[pl.BlockSpec((STRIP, half + HC), lambda j: (0, 0)), pl.BlockSpec((STRIP, half), lambda j: (0, 0)),
+                   pl.BlockSpec((STRIP, half + HC), lambda j: (0, 0)), pl.BlockSpec((STRIP, half), lambda j: (0, 0)),
                    pl.BlockSpec((rows, HC), lambda j: (0, 0))],
-        out_shape=[jax.ShapeDtypeStruct((STRIP, cols), f32), jax.ShapeDtypeStruct((STRIP, cols), f32),
+        out_shape=[jax.ShapeDtypeStruct((STRIP, half + HC), f32), jax.ShapeDtypeStruct((STRIP, half), f32),
+                   jax.ShapeDtypeStruct((STRIP, half + HC), f32), jax.ShapeDtypeStruct((STRIP, half), f32),
                    jax.ShapeDtypeStruct((rows, HC), f32)],
         interpret=INTERPRET,
     )(pos, *ins, *ins, *ins, *ins)
 
-    above = lax.ppermute(bot_s, "gx", [(i, i + 1) for i in range(nx - 1)])
-    below = lax.ppermute(top_s, "gx", [(i + 1, i) for i in range(nx - 1)])
+    down = [(i, i + 1) for i in range(nx - 1)]
+    up = [(i + 1, i) for i in range(nx - 1)]
+    above0 = lax.ppermute(bot0, "gx", down)
+    below0 = lax.ppermute(top0, "gx", up)
     side = lax.ppermute(col_s, "gy", [(0, 1), (1, 0)])
     both = ("gx", "gy")
     corner_above = lax.ppermute(col_s[rows - 8:], both,
                                 [(i * 2 + g, (i + 1) * 2 + 1 - g) for i in range(nx - 1) for g in range(2)])
     corner_below = lax.ppermute(col_s[:8], both,
                                 [((i + 1) * 2 + g, i * 2 + 1 - g) for i in range(nx - 1) for g in range(2)])
-
-    def kernel(pos_ref, um, ul, ur, vm, vl, vr, dm, dl, dr, hm, hl, hr, tm, tl, tr,
-               am, al, ar, bm, bl, br, side_ref, ca_ref, cb_ref, uo, vo, ho, do):
-        j = pl.program_id(0)
+    above0, below0, side, corner_above, corner_below, bot1, top1 = lax.optimization_barrier(
+        (above0, below0, side, corner_above, corner_below, bot1, top1))
+    above1 = lax.ppermute(bot1, "gx", down)
+    below1 = lax.ppermute(top1, "gx", up)
+
+    def kernel(jbase, pos_ref, um, ul, ur, vm, vl, vr, dm, dl, dr, hm, hl, hr, tm, tl, tr,
+               am, al, ar, ap, bm, bl, br, bp, side_ref, ca_ref, cb_ref, *rest):
+        uo, vo, ho, do = rest[-4:]
+        j = pl.program_id(0) + jbase
         first = j == 0
         last = j == nblocks - 1
         has_left = pos_ref[1] == 1
@@ -207,6 +222,9 @@
 
         a_m, a_l, a_r = am[...], al[...], ar[...]
         b_m, b_l, b_r = bm[...], bl[...], br[...]
+        if jbase:
+            a_l = jnp.where(j == jbase, ap[...], a_l)
+            b_l = jnp.where(j == jbase, bp[...], b_l)
 
         def window(k):
             lft = jnp.where(first, lane_left(side_v, k), lefts[k])
@@ -243,32 +261,54 @@
     def rcol(j):
         return jnp.minimum((j + 1) * per, last_col_block)
 
-    main2 = pl.BlockSpec((2, rows, BW), lambda j: (0, 0, j))
-    left2 = pl.BlockSpec((2, rows, HC), lambda j: (0, 0, lcol(j)))
-    right2 = pl.BlockSpec((2, rows, HC), lambda j: (0, 0, rcol(j)))
-    main1 = pl.BlockSpec((rows, BW), lambda j: (0, j))
-    left1 = pl.BlockSpec((rows, HC), lambda j: (0, lcol(j)))
-    right1 = pl.BlockSpec((rows, HC), lambda j: (0, rcol(j)))
-    sm = pl.BlockSpec((STRIP, BW), lambda j: (0, j))
-    sl = pl.BlockSpec((STRIP, HC), lambda j: (0, lcol(j)))
-    sr = pl.BlockSpec((STRIP, HC), lambda j: (0, rcol(j)))
-    sidespec = pl.BlockSpec((rows, HC), lambda j: (0, 0))
-    cornerspec = pl.BlockSpec((8, HC), lambda j: (0, 0))
-    out2 = pl.BlockSpec((2, rows, BW), lambda j: (0, 0, j))
-    out1 = pl.BlockSpec((rows, BW), lambda j: (0, j))
-    outs = pl.pallas_call(
-        kernel,
-        grid=(nblocks,),
-        in_specs=[smem, main2, left2, right2, main2, left2, right2,
-                  main1, left1, right1, main1, left1, right1, main1, left1, right1,
-                  sm, sl, sr, sm, sl, sr, sidespec, cornerspec, cornerspec],
-        out_specs=[out2, out2, out1, out1],
-        out_shape=[jax.ShapeDtypeStruct((2, rows, cols), f32), jax.ShapeDtypeStruct((2, rows, cols), f32),
-                   jax.ShapeDtypeStruct((rows, cols), f32), jax.ShapeDtypeStruct((rows, cols), f32)],
-        interpret=INTERPRET,
-    )(pos, displacement, displacement, displacement, velocity, velocity, velocity,
-      damage, damage, damage, history, history, history, toughness, toughness, toughness,
-      above, above, above, below, below, below, side, corner_above, corner_below)
+    nhalf = nblocks // 2
+
+    def run_half(h, above_h, below_h, prior):
+        jb = h * nhalf
+        shift = off if h else 0
+
+        def at(f):
+            return lambda i: f(i + jb)
+
+        main2 = pl.BlockSpec((2, rows, BW), at(lambda j: (0, 0, j)))
+        left2 = pl.BlockSpec((2, rows, HC), at(lambda j: (0, 0, lcol(j))))
+        right2 = pl.BlockSpec((2, rows, HC), at(lambda j: (0, 0, rcol(j))))
+        main1 = pl.BlockSpec((rows, BW), at(lambda j: (0, j)))
+        left1 = pl.BlockSpec((rows, HC), at(lambda j: (0, lcol(j))))
+        right1 = pl.BlockSpec((rows, HC), at(lambda j: (0, rcol(j))))
+        sm = pl.BlockSpec((STRIP, BW), lambda i: (0, i))
+        sl = pl.BlockSpec((STRIP, HC), at(lambda j: (0, jnp.maximum(lcol(j) - shift, 0))))
+        sr = pl.BlockSpec((STRIP, HC), at(lambda j: (0, rcol(j) - shift)))
+        sp = pl.BlockSpec((STRIP, HC), lambda i: (0, off - 1))
+        sidespec = pl.BlockSpec((rows, HC), lambda i: (0, 0))
+        cornerspec = pl.BlockSpec((8, HC), lambda i: (0, 0))
+        out2 = pl.BlockSpec((2, rows, BW), at(lambda j: (0, 0, j)))
+        out1 = pl.BlockSpec((rows, BW), at(lambda j: (0, j)))
+        in_specs = [smem, main2, left2, right2, main2, left2, right2,
+                    main1, left1, right1, main1, left1, right1, main1, left1, right1,
+                    sm, sl, sr, sp, sm, sl, sr, sp, sidespec, cornerspec, cornerspec]
+        args = [pos, displacement, displacement, displacement, velocity, velocity, velocity,
+                damage, damage, damage, history, history, history, toughness, toughness, toughness,
+                above_h, above_h, above_h, above0, below_h, below_h, below_h, below0,
+                side, corner_above, corner_below]
+        aliases = {}
+        if prior is not None:
+            aliases = {len(args) + k: k for k in range(4)}
+            in_specs = in_specs + [pl.BlockSpec(memory_space=pl.ANY)] * 4
+            args = args + list(prior)
+        return pl.pallas_call(
+            functools.partial(kernel, jb),
+            grid=(nhalf,),
+            in_specs=in_specs,
+            out_specs=[out2, out2, out1, out1],
+            out_shape=[jax.ShapeDtypeStruct((2, rows, cols), f32), jax.ShapeDtypeStruct((2, rows, cols), f32),
+                       jax.ShapeDtypeStruct((rows, cols), f32), jax.ShapeDtypeStruct((rows, cols), f32)],
+            input_output_aliases=aliases,
+            interpret=INTERPRET,
+        )(*args)
+
+    outs = run_half(0, above0, below0, None)
+    outs = run_half(1, above1, below1, outs)
     return tuple(outs)
 
 

time: 60 us -> 68.3 us (1.14)
  the two profiles are of different devices: /device:TPU:89 before, /device:TPU:128 now
where the time goes in v6:
time: 68.3 us; the launch traced here: 68 us
  starting transfers between devices  29.7 us (43%)
  Pallas kernels  28.4 us (42%)
  waiting for transfers between devices  6.72 us (10%)
  local copies, waits for them, and re-layouts  1.71 us (3%)
  between operations  0.79 us (1%)
    pallas_call x2, Pallas kernels, run_half(): pl.pallas_call(functools.partial(kernel, jb), grid=(nhalf,), in_specs=in_...  24.9 us
    ppermute x1, starting transfers between devices, on_device(): below0 = lax.ppermute(top0, 'gx', up)  9.36 us
    ppermute x1, starting transfers between devices, on_device(): below1 = lax.ppermute(top1, 'gx', up)  9.36 us
    ppermute x1, waiting for transfers between devices, on_device(): lax.ppermute(col_s[rows - 8:], both, [(i * 2 + g, (i + 1) * 2 + 1 - g) fo...  6.14 us
    ppermute x1, starting transfers between devices, on_device(): lax.ppermute(col_s[rows - 8:], both, [(i * 2 + g, (i + 1) * 2 + 1 - g) fo...  3.64 us
    pallas_call x1, Pallas kernels, on_device(): pl.pallas_call(pack_kernel, grid=(cols // pw,), in_specs=[smem, t2, t2, t...  3.56 us
    ppermute x1, starting transfers between devices, on_device(): above0 = lax.ppermute(bot0, 'gx', down)  1.92 us
    ppermute x1, starting transfers between devices, on_device(): above1 = lax.ppermute(bot1, 'gx', down)  1.92 us
  transfers between devices with their start and end apart: 7, of which 2 were waited for; matrix products, arithmetic and copies ran while one was open for 1% of the time, Pallas kernels for 18%

profile of v6, /device:TPU:128, one launch (start us, length us, event | category | flops | bytes accessed | tf_op | source)
XLA Modules:
  0.0 68.0 jit_solution(7052522967439980017)
XLA Ops:
  0.6 0.6 pad_add_fusion.pos_ref
  1.3 3.6 %shard_map.84 = (f32[32,4224]{1,0:T(8,128)}, f32[32,4096]{1,0:T(8,128)}, f32[32,4224]{1,0:T(8,128)}, f32[32,4096]{1,0:T(8,128)}, f32[32,128]{1,0:T(8,128)}) custom-call(s32[2]{0:T(128)} %pad_add_fusion.pos_ref, f32[2,32,8192]{2,1,0:T(8,128)} %ur.3, f32[2,32,8192]{2,1,0:T(8,128)} %vr.3, f32[32,8192]{1,0:T(8,128)} %dr.3, f32[32,8192]{1,0:T(8,128)} %hr.3, ...), custom_call_target="tpu_custom_call" | custom-call | tf_op jit(solution)/shard_map/pallas_call | solution.py:158
  4.8 1.9 %collective-permute-start = (f32[32,4224]{1,0:T(8,128)}, f32[32,4224]{1,0:T(8,128)S(1)}, u32[]{:S(2)}, u32[]{:S(2)}) collective-permute-start(f32[32,4224]{1,0:T(8,128)} %get-tuple-element.20), channel_id=1, source_target_pairs={{0,2},{2,4},{4,6},{6,8},{8,10},{10,12},{12,14},{14,16},{16,18},{18... | collective-permute-start | bytes 1622024 | tf_op jit(solution)/shard_map/ppermute | solution.py:173
  6.8 9.4 %collective-permute-start.1 = (f32[32,4224]{1,0:T(8,128)}, f32[32,4224]{1,0:T(8,128)S(1)}, u32[]{:S(2)}, u32[]{:S(2)}) collective-permute-start(f32[32,4224]{1,0:T(8,128)} %get-tuple-element.21), channel_id=1, source_target_pairs={{2,0},{4,2},{6,4},{8,6},{10,8},{12,10},{14,12},{16,14},{18,16},{20... | collective-permute-start | bytes 1622024 | tf_op jit(solution)/shard_map/ppermute | solution.py:174
  16.1 1.6 %collective-permute-start.2 = (f32[32,128]{1,0:T(8,128)}, f32[32,128]{1,0:T(8,128)S(1)}, u32[]{:S(2)}, u32[]{:S(2)}) collective-permute-start(f32[32,128]{1,0:T(8,128)} %get-tuple-element.22), channel_id=1, source_target_pairs={{0,1},{1,0},{2,3},{3,2},{4,5},{5,4},{6,7},{7,6},{8,9},{9,8},{10,11... | collective-permute-start | bytes 49160 | tf_op jit(solution)/shard_map/ppermute | solution.py:175
  17.7 0.7 %fusion = (f32[8,128]{1,0:T(8,128)S(1)}, f32[8,128]{1,0:T(8,128)S(1)}) fusion(f32[32,128]{1,0:T(8,128)} %get-tuple-element.22), kind=kLoop, calls=%fused_computation.1 | loop fusion | bytes 16384 | tf_op jit(solution)/shard_map/slice | solution.py:179
  18.4 1.9 %collective-permute-start.4 = (f32[8,128]{1,0:T(8,128)S(1)}, f32[8,128]{1,0:T(8,128)S(1)}, u32[]{:S(2)}, u32[]{:S(2)}) collective-permute-start(f32[8,128]{1,0:T(8,128)S(1)} %get-tuple-element.36), channel_id=1, source_target_pairs={{2,1},{3,0},{4,3},{5,2},{6,5},{7,4},{8,7},{9,6},{10,9},{11,8},{12,... | collective-permute-start | bytes 12296 | tf_op jit(solution)/shard_map/ppermute | solution.py:179
  20.4 3.6 %collective-permute-start.3 = (f32[8,128]{1,0:T(8,128)S(1)}, f32[8,128]{1,0:T(8,128)S(1)}, u32[]{:S(2)}, u32[]{:S(2)}) collective-permute-start(f32[8,128]{1,0:T(8,128)S(1)} %get-tuple-element.37), channel_id=1, source_target_pairs={{0,3},{1,2},{2,5},{3,4},{4,7},{5,6},{6,9},{7,8},{8,11},{9,10},{10,... | collective-permute-start | bytes 12296 | tf_op jit(solution)/shard_map/ppermute | solution.py:177
  24.0 0.6 collective-permute-done.4.cb_ref
  24.6 0.0 copy-start.5
  24.6 6.1 %collective-permute-done.3.ca_ref = f32[8,128]{1,0:T(8,128)S(1)} collective-permute-done((f32[8,128]{1,0:T(8,128)S(1)}, f32[8,128]{1,0:T(8,128)S(1)}, u32[]{:S(2)}, u32[]{:S(2)}) %collective-permute-start.3) | collective-permute-done | bytes 4128 | tf_op jit(solution)/shard_map/ppermute | solution.py:177
  30.7 0.0 copy-start.6
  30.7 0.0 collective-permute-done.2.side_ref
  30.7 0.0 copy-start.4
  30.7 0.0 collective-permute-done.am.al.ar.ap
  30.7 0.0 copy-start
  30.7 0.0 collective-permute-done.1.bm.bl.br.bp
  30.8 0.0 copy-start.1
  30.8 1.9 %collective-permute-start.5 = (f32[32,4096]{1,0:T(8,128)}, f32[32,4096]{1,0:T(8,128)S(1)}, u32[]{:S(2)}, u32[]{:S(2)}) collective-permute-start(f32[32,4096]{1,0:T(8,128)} %get-tuple-element.25), channel_id=1, source_target_pairs={{0,2},{2,4},{4,6},{6,8},{8,10},{10,12},{12,14},{14,16},{16,18},{18... | collective-permute-start | bytes 1572872 | tf_op jit(solution)/shard_map/ppermute | solution.py:183
  32.7 9.4 %collective-permute-start.6 = (f32[32,4096]{1,0:T(8,128)}, f32[32,4096]{1,0:T(8,128)S(1)}, u32[]{:S(2)}, u32[]{:S(2)}) collective-permute-start(f32[32,4096]{1,0:T(8,128)} %get-tuple-element.27), channel_id=1, source_target_pairs={{2,0},{4,2},{6,4},{8,6},{10,8},{12,10},{14,12},{16,14},{18,16},{20... | collective-permute-start | bytes 1572872 | tf_op jit(solution)/shard_map/ppermute | solution.py:184
  42.1 0.0 copy-done.5
  42.1 0.0 copy-done.6
  42.1 0.0 copy-done.4
  42.1 0.0 copy-done
  42.1 0.0 copy-done.1
  42.1 12.3 %shard_map.85 = (f32[2,32,8192]{2,1,0:T(8,128)}, f32[2,32,8192]{2,1,0:T(8,128)}, f32[32,8192]{1,0:T(8,128)}, f32[32,8192]{1,0:T(8,128)}) custom-call(s32[2]{0:T(128)} %pad_add_fusion.pos_ref, f32[2,32,8192]{2,1,0:T(8,128)} %ur.3, f32[2,32,8192]{2,1,0:T(8,128)} %ur.3, f32[2,32,8192]{2,1,0:T(8,128)} %ur.3, f32[2,32,8192]{2,1,0:T(8,128)} %vr.3, ...), custom_call_target="tpu_custom_call" | custom-call | tf_op jit(solution)/shard_map/pallas_call | solution.py:299
  54.4 0.0 collective-permute-done.5.am.al.ar
  54.5 0.0 copy-start.2
  54.5 0.0 collective-permute-done.6.bm.bl.br
  54.5 0.0 copy-start.3
  54.5 0.8 %copy-done.2 = f32[32,4096]{1,0:T(8,128)} copy-done((f32[32,4096]{1,0:T(8,128)}, f32[32,4096]{1,0:T(8,128)S(1)}, u32[]{:S(2)}) %copy-start.2) | copy-done | bytes 524312
  55.3 0.2 copy-done.3
  55.5 12.6 %shard_map.86 = (f32[2,32,8192]{2,1,0:T(8,128)}, f32[2,32,8192]{2,1,0:T(8,128)}, f32[32,8192]{1,0:T(8,128)}, f32[32,8192]{1,0:T(8,128)}) custom-call(s32[2]{0:T(128)} %pad_add_fusion.pos_ref, f32[2,32,8192]{2,1,0:T(8,128)} %ur.3, f32[2,32,8192]{2,1,0:T(8,128)} %ur.3, ...), custom_call_target="tpu_custom_call", output_to_operand_aliasing={{0}: (27, {}), {1}: (28, {}), {2}: (29, {}), {3}: (30, {})} | custom-call | tf_op jit(solution)/shard_map/pallas_call | solution.py:299
Async XLA Ops:
  4.8 25.9 %collective-permute-start = (f32[32,4224]{1,0:T(8,128)}, f32[32,4224]{1,0:T(8,128)S(1)}, u32[]{:S(2)}, u32[]{:S(2)}) collective-permute-start(f32[32,4224]{1,0:T(8,128)} %get-tuple-element.20), channel_id=1, source_target_pairs={{0,2},{2,4},{4,6},{6,8},{8,10},{10,12},{12,14},{14,16},{16,18},{18... | collective-permute-start | bytes 1622024 | tf_op jit(solution)/shard_map/ppermute | solution.py:173
  6.8 24.0 %collective-permute-start.1 = (f32[32,4224]{1,0:T(8,128)}, f32[32,4224]{1,0:T(8,128)S(1)}, u32[]{:S(2)}, u32[]{:S(2)}) collective-permute-start(f32[32,4224]{1,0:T(8,128)} %get-tuple-element.21), channel_id=1, source_target_pairs={{2,0},{4,2},{6,4},{8,6},{10,8},{12,10},{14,12},{16,14},{18,16},{20... | collective-permute-start | bytes 1622024 | tf_op jit(solution)/shard_map/ppermute | solution.py:174
  16.1 14.6 %collective-permute-start.2 = (f32[32,128]{1,0:T(8,128)}, f32[32,128]{1,0:T(8,128)S(1)}, u32[]{:S(2)}, u32[]{:S(2)}) collective-permute-start(f32[32,128]{1,0:T(8,128)} %get-tuple-element.22), channel_id=1, source_target_pairs={{0,1},{1,0},{2,3},{3,2},{4,5},{5,4},{6,7},{7,6},{8,9},{9,8},{10,11... | collective-permute-start | bytes 49160 | tf_op jit(solution)/shard_map/ppermute | solution.py:175
  18.4 6.1 %collective-permute-start.4 = (f32[8,128]{1,0:T(8,128)S(1)}, f32[8,128]{1,0:T(8,128)S(1)}, u32[]{:S(2)}, u32[]{:S(2)}) collective-permute-start(f32[8,128]{1,0:T(8,128)S(1)} %get-tuple-element.36), channel_id=1, source_target_pairs={{2,1},{3,0},{4,3},{5,2},{6,5},{7,4},{8,7},{9,6},{10,9},{11,8},{12,... | collective-permute-start | bytes 12296 | tf_op jit(solution)/shard_map/ppermute | solution.py:179
  20.4 10.4 %collective-permute-start.3 = (f32[8,128]{1,0:T(8,128)S(1)}, f32[8,128]{1,0:T(8,128)S(1)}, u32[]{:S(2)}, u32[]{:S(2)}) collective-permute-start(f32[8,128]{1,0:T(8,128)S(1)} %get-tuple-element.37), channel_id=1, source_target_pairs={{0,3},{1,2},{2,5},{3,4},{4,7},{5,6},{6,9},{7,8},{8,11},{9,10},{10,... | collective-permute-start | bytes 12296 | tf_op jit(solution)/shard_map/ppermute | solution.py:177
  24.6 17.5 %copy-start.5 = (f32[8,128]{1,0:T(8,128)}, f32[8,128]{1,0:T(8,128)S(1)}, u32[]{:S(2)}) copy-start(f32[8,128]{1,0:T(8,128)S(1)} %collective-permute-done.4.cb_ref) | copy-start | bytes 12292
  30.7 11.4 %copy-start.6 = (f32[8,128]{1,0:T(8,128)}, f32[8,128]{1,0:T(8,128)S(1)}, u32[]{:S(2)}) copy-start(f32[8,128]{1,0:T(8,128)S(1)} %collective-permute-done.3.ca_ref) | copy-start | bytes 12292
  30.7 11.4 %copy-start.4 = (f32[32,128]{1,0:T(8,128)}, f32[32,128]{1,0:T(8,128)S(1)}, u32[]{:S(2)}) copy-start(f32[32,128]{1,0:T(8,128)S(1)} %collective-permute-done.2.side_ref) | copy-start | bytes 49156
  30.7 11.4 %copy-start = (f32[32,4224]{1,0:T(8,128)}, f32[32,4224]{1,0:T(8,128)S(1)}, u32[]{:S(2)}) copy-start(f32[32,4224]{1,0:T(8,128)S(1)} %collective-permute-done.am.al.ar.ap) | copy-start | bytes 1622020
  30.8 11.4 %copy-start.1 = (f32[32,4224]{1,0:T(8,128)}, f32[32,4224]{1,0:T(8,128)S(1)}, u32[]{:S(2)}) copy-start(f32[32,4224]{1,0:T(8,128)S(1)} %collective-permute-done.1.bm.bl.br.bp) | copy-start | bytes 1622020
  30.8 23.7 %collective-permute-start.5 = (f32[32,4096]{1,0:T(8,128)}, f32[32,4096]{1,0:T(8,128)S(1)}, u32[]{:S(2)}, u32[]{:S(2)}) collective-permute-start(f32[32,4096]{1,0:T(8,128)} %get-tuple-element.25), channel_id=1, source_target_pairs={{0,2},{2,4},{4,6},{6,8},{8,10},{10,12},{12,14},{14,16},{16,18},{18... | collective-permute-start | bytes 1572872 | tf_op jit(solution)/shard_map/ppermute | solution.py:183
  32.7 21.8 %collective-permute-start.6 = (f32[32,4096]{1,0:T(8,128)}, f32[32,4096]{1,0:T(8,128)S(1)}, u32[]{:S(2)}, u32[]{:S(2)}) collective-permute-start(f32[32,4096]{1,0:T(8,128)} %get-tuple-element.27), channel_id=1, source_target_pairs={{2,0},{4,2},{6,4},{8,6},{10,8},{12,10},{14,12},{16,14},{18,16},{20... | collective-permute-start | bytes 1572872 | tf_op jit(solution)/shard_map/ppermute | solution.py:184
  54.5 0.8 %copy-start.2 = (f32[32,4096]{1,0:T(8,128)}, f32[32,4096]{1,0:T(8,128)S(1)}, u32[]{:S(2)}) copy-start(f32[32,4096]{1,0:T(8,128)S(1)} %collective-permute-done.5.am.al.ar) | copy-start | bytes 1572868
  54.5 1.0 %copy-start.3 = (f32[32,4096]{1,0:T(8,128)}, f32[32,4096]{1,0:T(8,128)S(1)}, u32[]{:S(2)}) copy-start(f32[32,4096]{1,0:T(8,128)S(1)} %collective-permute-done.6.bm.bl.br) | copy-start | bytes 1572868

commit v7 on v4

--- a/solution.py
+++ b/solution.py
@@ -104,7 +104,7 @@
         du, dv, dd, dh, dt = refs
         return [du[0], du[1], dv[0], dv[1], dd[...], dh[...], dt[...]]
 
-    pw = cols
+    pw = cols // 4
 
     def pack_kernel(pos_ref, tu, tv, td, th, tt, bu, bv, bd, bh, bt,
                     lu, lv, ld, lh, lt, ru, rv, rd, rh, rt, top_o, bot_o, col_o):

time: 60 us -> 60.6 us (1.010)
    pallas_call x1, Pallas kernels: 3.78 us -> 4.44 us  [on_device(): pl.pallas_call(pack_kernel, grid=(cols // pw,), in_specs=[smem, t2, t2, t...]
where the time goes in v7:
time: 60.6 us; the launch traced here: 59.6 us
  Pallas kernels  26.5 us (44%)
  starting transfers between devices  14.8 us (24%)
  waiting for transfers between devices  14.3 us (24%)
  local copies, waits for them, and re-layouts  2.67 us (4%)
  between operations  0.7 us (1%)
  other arithmetic  0.61 us (1%)
    pallas_call x1, Pallas kernels, on_device(): pl.pallas_call(kernel, grid=(nblocks,), in_specs=[smem, main2, left2, rig...  22.1 us
    ppermute x1, waiting for transfers between devices, on_device(): lax.ppermute(col_s[:8], both, [((i + 1) * 2 + g, i * 2 + 1 - g) for i in...  9.58 us
    ppermute x1, starting transfers between devices, on_device(): above = lax.ppermute(bot_s, 'gx', [(i, i + 1) for i in range(nx - 1)])  5.21 us
    ppermute x1, starting transfers between devices, on_device(): lax.ppermute(col_s[:8], both, [((i + 1) * 2 + g, i * 2 + 1 - g) for i in...  4.72 us
    ppermute x1, waiting for transfers between devices, on_device(): lax.ppermute(col_s[rows - 8:], both, [(i * 2 + g, (i + 1) * 2 + 1 - g) fo...  4.69 us
    pallas_call x1, Pallas kernels, on_device(): pl.pallas_call(pack_kernel, grid=(cols // pw,), in_specs=[smem, t2, t2, t...  4.44 us
    ppermute x1, starting transfers between devices, on_device(): lax.ppermute(col_s[rows - 8:], both, [(i * 2 + g, (i + 1) * 2 + 1 - g) fo...  2.58 us
    unnamed x10, local copies, waits for them, and re-layouts  1.95 us
  transfers between devices with their start and end apart: 5, of which 2 were waited for; matrix products, arithmetic and copies ran while one was open for 1% of the time, Pallas kernels for 0%

profile of v7, /device:TPU:89, one launch (start us, length us, event | category | flops | bytes accessed | tf_op | source)
XLA Modules:
  0.0 59.6 jit_solution(5428804245748325596)
XLA Ops:
  0.6 0.6 %pad_add_fusion.pos_ref = s32[2]{0:T(128)} fusion(s32[1]{0:T(128)} %bitcast.1, s32[1]{0:T(128)} %bitcast), kind=kLoop, calls=%fused_computation | loop fusion | flops 2 | bytes 16 | tf_op jit(solution)/shard_map/stack | solution.py:92
  1.2 4.4 %shard_map.84 = (f32[32,8192]{1,0:T(8,128)}, f32[32,8192]{1,0:T(8,128)}, f32[32,128]{1,0:T(8,128)}) custom-call(s32[2]{0:T(128)} %pad_add_fusion.pos_ref, f32[2,32,8192]{2,1,0:T(8,128)} %ur.1, f32[2,32,8192]{2,1,0:T(8,128)} %vr.1, f32[32,8192]{1,0:T(8,128)} %dr.1, f32[32,8192]{1,0:T(8,128)} %hr.1, f32[32,8192]{1,0:T(8,128)} %tr.1, f32[2,32,8192]{2,1,0:T(8,128)} %ur.1, ...), custom_call_target="tpu_custom_call" | custom-call | tf_op jit(solution)/shard_map/pallas_call | solution.py:152
  5.7 5.2 %collective-permute-start = (f32[32,8192]{1,0:T(8,128)}, f32[32,8192]{1,0:T(8,128)S(1)}, u32[]{:S(2)}, u32[]{:S(2)}) collective-permute-start(f32[32,8192]{1,0:T(8,128)} %get-tuple-element.7), channel_id=1, source_target_pairs={{0,2},{2,4},{4,6},{6,8},{8,10},{10,12},{12,14},{14,16},{16,18},{18... | collective-permute-start | bytes 3145736 | tf_op jit(solution)/shard_map/ppermute | solution.py:163
  10.9 1.9 %collective-permute-start.1 = (f32[32,8192]{1,0:T(8,128)}, f32[32,8192]{1,0:T(8,128)S(1)}, u32[]{:S(2)}, u32[]{:S(2)}) collective-permute-start(f32[32,8192]{1,0:T(8,128)} %get-tuple-element.8), channel_id=1, source_target_pairs={{2,0},{4,2},{6,4},{8,6},{10,8},{12,10},{14,12},{16,14},{18,16},{20... | collective-permute-start | bytes 3145736 | tf_op jit(solution)/shard_map/ppermute | solution.py:164
  12.8 0.4 collective-permute-start.2
  13.2 0.7 %fusion = (f32[8,128]{1,0:T(8,128)S(1)}, f32[8,128]{1,0:T(8,128)S(1)}) fusion(f32[32,128]{1,0:T(8,128)} %get-tuple-element.9), kind=kLoop, calls=%fused_computation.1 | loop fusion | bytes 16384 | tf_op jit(solution)/shard_map/slice | solution.py:169
  14.0 4.7 %collective-permute-start.4 = (f32[8,128]{1,0:T(8,128)S(1)}, f32[8,128]{1,0:T(8,128)S(1)}, u32[]{:S(2)}, u32[]{:S(2)}) collective-permute-start(f32[8,128]{1,0:T(8,128)S(1)} %get-tuple-element.10), channel_id=1, source_target_pairs={{2,1},{3,0},{4,3},{5,2},{6,5},{7,4},{8,7},{9,6},{10,9},{11,8},{12,... | collective-permute-start | bytes 12296 | tf_op jit(solution)/shard_map/ppermute | solution.py:169
  18.7 2.6 %collective-permute-start.3 = (f32[8,128]{1,0:T(8,128)S(1)}, f32[8,128]{1,0:T(8,128)S(1)}, u32[]{:S(2)}, u32[]{:S(2)}) collective-permute-start(f32[8,128]{1,0:T(8,128)S(1)} %get-tuple-element.11), channel_id=1, source_target_pairs={{0,3},{1,2},{2,5},{3,4},{4,7},{5,6},{6,9},{7,8},{8,11},{9,10},{10,... | collective-permute-start | bytes 12296 | tf_op jit(solution)/shard_map/ppermute | solution.py:167
  21.3 9.6 %collective-permute-done.4.cb_ref = f32[8,128]{1,0:T(8,128)S(1)} collective-permute-done((f32[8,128]{1,0:T(8,128)S(1)}, f32[8,128]{1,0:T(8,128)S(1)}, u32[]{:S(2)}, u32[]{:S(2)}) %collective-permute-start.4) | collective-permute-done | bytes 4128 | tf_op jit(solution)/shard_map/ppermute | solution.py:169
  30.9 0.0 copy-start.3
  30.9 4.7 %collective-permute-done.3.ca_ref = f32[8,128]{1,0:T(8,128)S(1)} collective-permute-done((f32[8,128]{1,0:T(8,128)S(1)}, f32[8,128]{1,0:T(8,128)S(1)}, u32[]{:S(2)}, u32[]{:S(2)}) %collective-permute-start.3) | collective-permute-done | bytes 4128 | tf_op jit(solution)/shard_map/ppermute | solution.py:167
  35.5 0.0 copy-start.4
  35.6 0.0 collective-permute-done.2.side_ref
  35.6 0.0 copy-start.2
  35.6 0.0 collective-permute-done.am.al.ar
  35.6 0.0 copy-start
  35.6 0.0 collective-permute-done.1.bm.bl.br
  35.6 0.0 copy-done.3
  35.6 0.5 copy-done.4
  36.1 0.0 copy-done.2
  36.2 0.4 copy-done
  36.5 0.0 copy-start.1
  36.5 1.0 %copy-done.1 = f32[32,8192]{1,0:T(8,128)} copy-done((f32[32,8192]{1,0:T(8,128)}, f32[32,8192]{1,0:T(8,128)S(1)}, u32[]{:S(2)}) %copy-start.1) | copy-done | bytes 1048600
  37.5 22.1 %shard_map.85 = (f32[2,32,8192]{2,1,0:T(8,128)}, f32[2,32,8192]{2,1,0:T(8,128)}, f32[32,8192]{1,0:T(8,128)}, f32[32,8192]{1,0:T(8,128)}) custom-call(s32[2]{0:T(128)} %pad_add_fusion.pos_ref, f32[2,32,8192]{2,1,0:T(8,128)} %ur.1, f32[2,32,8192]{2,1,0:T(8,128)} %ur.1, f32[2,32,8192]{2,1,0:T(8,128)} %ur.1, f32[2,32,8192]{2,1,0:T(8,128)} %vr.1, ...), custom_call_target="tpu_custom_call" | custom-call | tf_op jit(solution)/shard_map/pallas_call | solution.py:259
Async XLA Ops:
  5.7 29.9 %collective-permute-start = (f32[32,8192]{1,0:T(8,128)}, f32[32,8192]{1,0:T(8,128)S(1)}, u32[]{:S(2)}, u32[]{:S(2)}) collective-permute-start(f32[32,8192]{1,0:T(8,128)} %get-tuple-element.7), channel_id=1, source_target_pairs={{0,2},{2,4},{4,6},{6,8},{8,10},{10,12},{12,14},{14,16},{16,18},{18... | collective-permute-start | bytes 3145736 | tf_op jit(solution)/shard_map/ppermute | solution.py:163
  10.9 24.7 %collective-permute-start.1 = (f32[32,8192]{1,0:T(8,128)}, f32[32,8192]{1,0:T(8,128)S(1)}, u32[]{:S(2)}, u32[]{:S(2)}) collective-permute-start(f32[32,8192]{1,0:T(8,128)} %get-tuple-element.8), channel_id=1, source_target_pairs={{2,0},{4,2},{6,4},{8,6},{10,8},{12,10},{14,12},{16,14},{18,16},{20... | collective-permute-start | bytes 3145736 | tf_op jit(solution)/shard_map/ppermute | solution.py:164
  12.8 22.7 %collective-permute-start.2 = (f32[32,128]{1,0:T(8,128)}, f32[32,128]{1,0:T(8,128)S(1)}, u32[]{:S(2)}, u32[]{:S(2)}) collective-permute-start(f32[32,128]{1,0:T(8,128)} %get-tuple-element.9), channel_id=1, source_target_pairs={{0,1},{1,0},{2,3},{3,2},{4,5},{5,4},{6,7},{7,6},{8,9},{9,8},{10,11... | collective-permute-start | bytes 49160 | tf_op jit(solution)/shard_map/ppermute | solution.py:165
  14.0 16.9 %collective-permute-start.4 = (f32[8,128]{1,0:T(8,128)S(1)}, f32[8,128]{1,0:T(8,128)S(1)}, u32[]{:S(2)}, u32[]{:S(2)}) collective-permute-start(f32[8,128]{1,0:T(8,128)S(1)} %get-tuple-element.10), channel_id=1, source_target_pairs={{2,1},{3,0},{4,3},{5,2},{6,5},{7,4},{8,7},{9,6},{10,9},{11,8},{12,... | collective-permute-start | bytes 12296 | tf_op jit(solution)/shard_map/ppermute | solution.py:169
  18.7 16.9 %collective-permute-start.3 = (f32[8,128]{1,0:T(8,128)S(1)}, f32[8,128]{1,0:T(8,128)S(1)}, u32[]{:S(2)}, u32[]{:S(2)}) collective-permute-start(f32[8,128]{1,0:T(8,128)S(1)} %get-tuple-element.11), channel_id=1, source_target_pairs={{0,3},{1,2},{2,5},{3,4},{4,7},{5,6},{6,9},{7,8},{8,11},{9,10},{10,... | collective-permute-start | bytes 12296 | tf_op jit(solution)/shard_map/ppermute | solution.py:167
  30.9 4.7 %copy-start.3 = (f32[8,128]{1,0:T(8,128)}, f32[8,128]{1,0:T(8,128)S(1)}, u32[]{:S(2)}) copy-start(f32[8,128]{1,0:T(8,128)S(1)} %collective-permute-done.4.cb_ref) | copy-start | bytes 12292
  35.5 0.6 copy-start.4
  35.6 0.6 %copy-start.2 = (f32[32,128]{1,0:T(8,128)}, f32[32,128]{1,0:T(8,128)S(1)}, u32[]{:S(2)}) copy-start(f32[32,128]{1,0:T(8,128)S(1)} %collective-permute-done.2.side_ref) | copy-start | bytes 49156
  35.6 1.0 %copy-start = (f32[32,8192]{1,0:T(8,128)}, f32[32,8192]{1,0:T(8,128)S(1)}, u32[]{:S(2)}) copy-start(f32[32,8192]{1,0:T(8,128)S(1)} %collective-permute-done.am.al.ar) | copy-start | bytes 3145732
  36.5 1.0 %copy-start.1 = (f32[32,8192]{1,0:T(8,128)}, f32[32,8192]{1,0:T(8,128)S(1)}, u32[]{:S(2)}) copy-start(f32[32,8192]{1,0:T(8,128)S(1)} %collective-permute-done.1.bm.bl.br) | copy-start | bytes 3145732

commit v8 on v6

--- a/solution.py
+++ b/solution.py
@@ -178,8 +178,8 @@
                                 [(i * 2 + g, (i + 1) * 2 + 1 - g) for i in range(nx - 1) for g in range(2)])
     corner_below = lax.ppermute(col_s[:8], both,
                                 [((i + 1) * 2 + g, i * 2 + 1 - g) for i in range(nx - 1) for g in range(2)])
-    above0, below0, side, corner_above, corner_below, bot1, top1 = lax.optimization_barrier(
-        (above0, below0, side, corner_above, corner_below, bot1, top1))
+    side, corner_above, corner_below, bot1, top1 = lax.optimization_barrier(
+        (side, corner_above, corner_below, bot1, top1))
     above1 = lax.ppermute(bot1, "gx", down)
     below1 = lax.ppermute(top1, "gx", up)
 

time: 68.3 us -> 69.7 us (1.020)
  local copies, waits for them, and re-layouts: 1.71 us -> 3.24 us
    unnamed x14, local copies, waits for them, and re-layouts: 0.99 us -> 2.54 us
where the time goes in v8:
time: 69.7 us; the launch traced here: 69.4 us
  starting transfers between devices  29.7 us (43%)
  Pallas kernels  28.4 us (41%)
  waiting for transfers between devices  6.72 us (10%)
  local copies, waits for them, and re-layouts  3.24 us (5%)
  between operations  0.77 us (1%)
    pallas_call x2, Pallas kernels, run_half(): pl.pallas_call(functools.partial(kernel, jb), grid=(nhalf,), in_specs=in_...  24.8 us
    ppermute x1, starting transfers between devices, on_device(): below0 = lax.ppermute(top0, 'gx', up)  9.36 us
    ppermute x1, starting transfers between devices, on_device(): below1 = lax.ppermute(top1, 'gx', up)  9.36 us
    ppermute x1, waiting for transfers between devices, on_device(): lax.ppermute(col_s[rows - 8:], both, [(i * 2 + g, (i + 1) * 2 + 1 - g) fo...  5.81 us
    ppermute x1, starting transfers between devices, on_device(): lax.ppermute(col_s[rows - 8:], both, [(i * 2 + g, (i + 1) * 2 + 1 - g) fo...  3.64 us
    pallas_call x1, Pallas kernels, on_device(): pl.pallas_call(pack_kernel, grid=(cols // pw,), in_specs=[smem, t2, t2, t...  3.56 us
    unnamed x14, local copies, waits for them, and re-layouts  2.54 us
    ppermute x1, starting transfers between devices, on_device(): above1 = lax.ppermute(bot1, 'gx', down)  1.92 us
  transfers between devices with their start and end apart: 7, of which 2 were waited for; matrix products, arithmetic and copies ran while one was open for 1% of the time, Pallas kernels for 18%

profile of v8, /device:TPU:128, one launch (start us, length us, event | category | flops | bytes accessed | tf_op | source)
XLA Modules:
  0.0 69.4 jit_solution(8473717629219894408)
XLA Ops:
  0.6 0.6 pad_add_fusion.pos_ref
  1.3 3.6 %shard_map.84 = (f32[32,4224]{1,0:T(8,128)}, f32[32,4096]{1,0:T(8,128)}, f32[32,4224]{1,0:T(8,128)}, f32[32,4096]{1,0:T(8,128)}, f32[32,128]{1,0:T(8,128)}) custom-call(s32[2]{0:T(128)} %pad_add_fusion.pos_ref, f32[2,32,8192]{2,1,0:T(8,128)} %ur.3, f32[2,32,8192]{2,1,0:T(8,128)} %vr.3, f32[32,8192]{1,0:T(8,128)} %dr.3, f32[32,8192]{1,0:T(8,128)} %hr.3, ...), custom_call_target="tpu_custom_call" | custom-call | tf_op jit(solution)/shard_map/pallas_call | solution.py:158
  4.8 1.6 %collective-permute-start = (f32[32,128]{1,0:T(8,128)}, f32[32,128]{1,0:T(8,128)S(1)}, u32[]{:S(2)}, u32[]{:S(2)}) collective-permute-start(f32[32,128]{1,0:T(8,128)} %get-tuple-element.18), channel_id=1, source_target_pairs={{0,1},{1,0},{2,3},{3,2},{4,5},{5,4},{6,7},{7,6},{8,9},{9,8},{10,11... | collective-permute-start | bytes 49160 | tf_op jit(solution)/shard_map/ppermute | solution.py:175
  6.4 1.9 %collective-permute-start.4 = (f32[32,4224]{1,0:T(8,128)}, f32[32,4224]{1,0:T(8,128)S(1)}, u32[]{:S(2)}, u32[]{:S(2)}) collective-permute-start(f32[32,4224]{1,0:T(8,128)} %get-tuple-element.22), channel_id=1, source_target_pairs={{0,2},{2,4},{4,6},{6,8},{8,10},{10,12},{12,14},{14,16},{16,18},{18... | collective-permute-start | bytes 1622024 | tf_op jit(solution)/shard_map/ppermute | solution.py:173
  8.3 9.4 %collective-permute-start.6 = (f32[32,4224]{1,0:T(8,128)}, f32[32,4224]{1,0:T(8,128)S(1)}, u32[]{:S(2)}, u32[]{:S(2)}) collective-permute-start(f32[32,4224]{1,0:T(8,128)} %get-tuple-element.24), channel_id=1, source_target_pairs={{2,0},{4,2},{6,4},{8,6},{10,8},{12,10},{14,12},{16,14},{18,16},{20... | collective-permute-start | bytes 1622024 | tf_op jit(solution)/shard_map/ppermute | solution.py:174
  17.7 0.7 %fusion = (f32[8,128]{1,0:T(8,128)S(1)}, f32[8,128]{1,0:T(8,128)S(1)}) fusion(f32[32,128]{1,0:T(8,128)} %get-tuple-element.18), kind=kLoop, calls=%fused_computation.1 | loop fusion | bytes 16384 | tf_op jit(solution)/shard_map/slice | solution.py:179
  18.4 1.9 %collective-permute-start.2 = (f32[8,128]{1,0:T(8,128)S(1)}, f32[8,128]{1,0:T(8,128)S(1)}, u32[]{:S(2)}, u32[]{:S(2)}) collective-permute-start(f32[8,128]{1,0:T(8,128)S(1)} %get-tuple-element.32), channel_id=1, source_target_pairs={{2,1},{3,0},{4,3},{5,2},{6,5},{7,4},{8,7},{9,6},{10,9},{11,8},{12,... | collective-permute-start | bytes 12296 | tf_op jit(solution)/shard_map/ppermute | solution.py:179
  20.3 3.6 %collective-permute-start.1 = (f32[8,128]{1,0:T(8,128)S(1)}, f32[8,128]{1,0:T(8,128)S(1)}, u32[]{:S(2)}, u32[]{:S(2)}) collective-permute-start(f32[8,128]{1,0:T(8,128)S(1)} %get-tuple-element.33), channel_id=1, source_target_pairs={{0,3},{1,2},{2,5},{3,4},{4,7},{5,6},{6,9},{7,8},{8,11},{9,10},{10,... | collective-permute-start | bytes 12296 | tf_op jit(solution)/shard_map/ppermute | solution.py:177
  24.0 0.9 %collective-permute-done.2.cb_ref = f32[8,128]{1,0:T(8,128)S(1)} collective-permute-done((f32[8,128]{1,0:T(8,128)S(1)}, f32[8,128]{1,0:T(8,128)S(1)}, u32[]{:S(2)}, u32[]{:S(2)}) %collective-permute-start.2) | collective-permute-done | bytes 4128 | tf_op jit(solution)/shard_map/ppermute | solution.py:179
  24.9 0.0 copy-start.5
  24.9 5.8 %collective-permute-done.1.ca_ref = f32[8,128]{1,0:T(8,128)S(1)} collective-permute-done((f32[8,128]{1,0:T(8,128)S(1)}, f32[8,128]{1,0:T(8,128)S(1)}, u32[]{:S(2)}, u32[]{:S(2)}) %collective-permute-start.1) | collective-permute-done | bytes 4128 | tf_op jit(solution)/shard_map/ppermute | solution.py:177
  30.7 0.0 copy-start.6
  30.7 0.0 collective-permute-done.side_ref
  30.7 0.0 copy-start.4
  30.7 1.9 %collective-permute-start.3 = (f32[32,4096]{1,0:T(8,128)}, f32[32,4096]{1,0:T(8,128)S(1)}, u32[]{:S(2)}, u32[]{:S(2)}) collective-permute-start(f32[32,4096]{1,0:T(8,128)} %get-tuple-element.21), channel_id=1, source_target_pairs={{0,2},{2,4},{4,6},{6,8},{8,10},{10,12},{12,14},{14,16},{16,18},{18... | collective-permute-start | bytes 1572872 | tf_op jit(solution)/shard_map/ppermute | solution.py:183
  32.6 9.4 %collective-permute-start.5 = (f32[32,4096]{1,0:T(8,128)}, f32[32,4096]{1,0:T(8,128)S(1)}, u32[]{:S(2)}, u32[]{:S(2)}) collective-permute-start(f32[32,4096]{1,0:T(8,128)} %get-tuple-element.23), channel_id=1, source_target_pairs={{2,0},{4,2},{6,4},{8,6},{10,8},{12,10},{14,12},{16,14},{18,16},{20... | collective-permute-start | bytes 1572872 | tf_op jit(solution)/shard_map/ppermute | solution.py:184
  42.0 0.0 collective-permute-done.4.am.al.ar.ap
  42.0 0.0 copy-start
  42.0 0.0 collective-permute-done.6.bm.bl.br.bp
  42.0 0.0 copy-done.5
  42.0 0.0 copy-done.6
  42.0 0.0 copy-done.4
  42.1 0.7 %copy-done = f32[32,4224]{1,0:T(8,128)} copy-done((f32[32,4224]{1,0:T(8,128)}, f32[32,4224]{1,0:T(8,128)S(1)}, u32[]{:S(2)}) %copy-start) | copy-done | bytes 540696
  42.8 0.0 copy-start.1
  42.8 0.8 %copy-done.1 = f32[32,4224]{1,0:T(8,128)} copy-done((f32[32,4224]{1,0:T(8,128)}, f32[32,4224]{1,0:T(8,128)S(1)}, u32[]{:S(2)}) %copy-start.1) | copy-done | bytes 540696
  43.6 12.3 %shard_map.85 = (f32[2,32,8192]{2,1,0:T(8,128)}, f32[2,32,8192]{2,1,0:T(8,128)}, f32[32,8192]{1,0:T(8,128)}, f32[32,8192]{1,0:T(8,128)}) custom-call(s32[2]{0:T(128)} %pad_add_fusion.pos_ref, f32[2,32,8192]{2,1,0:T(8,128)} %ur.3, f32[2,32,8192]{2,1,0:T(8,128)} %ur.3, f32[2,32,8192]{2,1,0:T(8,128)} %ur.3, f32[2,32,8192]{2,1,0:T(8,128)} %vr.3, ...), custom_call_target="tpu_custom_call" | custom-call | tf_op jit(solution)/shard_map/pallas_call | solution.py:299
  55.9 0.0 collective-permute-done.3.am.al.ar
  55.9 0.0 copy-start.2
  55.9 0.0 collective-permute-done.5.bm.bl.br
  55.9 0.0 copy-start.3
  55.9 0.8 %copy-done.2 = f32[32,4096]{1,0:T(8,128)} copy-done((f32[32,4096]{1,0:T(8,128)}, f32[32,4096]{1,0:T(8,128)S(1)}, u32[]{:S(2)}) %copy-start.2) | copy-done | bytes 524312
  56.7 0.2 copy-done.3
  56.9 12.6 %shard_map.86 = (f32[2,32,8192]{2,1,0:T(8,128)}, f32[2,32,8192]{2,1,0:T(8,128)}, f32[32,8192]{1,0:T(8,128)}, f32[32,8192]{1,0:T(8,128)}) custom-call(s32[2]{0:T(128)} %pad_add_fusion.pos_ref, f32[2,32,8192]{2,1,0:T(8,128)} %ur.3, f32[2,32,8192]{2,1,0:T(8,128)} %ur.3, ...), custom_call_target="tpu_custom_call", output_to_operand_aliasing={{0}: (27, {}), {1}: (28, {}), {2}: (29, {}), {3}: (30, {})} | custom-call | tf_op jit(solution)/shard_map/pallas_call | solution.py:299
Async XLA Ops:
  4.8 25.9 %collective-permute-start = (f32[32,128]{1,0:T(8,128)}, f32[32,128]{1,0:T(8,128)S(1)}, u32[]{:S(2)}, u32[]{:S(2)}) collective-permute-start(f32[32,128]{1,0:T(8,128)} %get-tuple-element.18), channel_id=1, source_target_pairs={{0,1},{1,0},{2,3},{3,2},{4,5},{5,4},{6,7},{7,6},{8,9},{9,8},{10,11... | collective-permute-start | bytes 49160 | tf_op jit(solution)/shard_map/ppermute | solution.py:175
  6.4 35.6 %collective-permute-start.4 = (f32[32,4224]{1,0:T(8,128)}, f32[32,4224]{1,0:T(8,128)S(1)}, u32[]{:S(2)}, u32[]{:S(2)}) collective-permute-start(f32[32,4224]{1,0:T(8,128)} %get-tuple-element.22), channel_id=1, source_target_pairs={{0,2},{2,4},{4,6},{6,8},{8,10},{10,12},{12,14},{14,16},{16,18},{18... | collective-permute-start | bytes 1622024 | tf_op jit(solution)/shard_map/ppermute | solution.py:173
  8.3 33.7 %collective-permute-start.6 = (f32[32,4224]{1,0:T(8,128)}, f32[32,4224]{1,0:T(8,128)S(1)}, u32[]{:S(2)}, u32[]{:S(2)}) collective-permute-start(f32[32,4224]{1,0:T(8,128)} %get-tuple-element.24), channel_id=1, source_target_pairs={{2,0},{4,2},{6,4},{8,6},{10,8},{12,10},{14,12},{16,14},{18,16},{20... | collective-permute-start | bytes 1622024 | tf_op jit(solution)/shard_map/ppermute | solution.py:174
  18.4 6.5 %collective-permute-start.2 = (f32[8,128]{1,0:T(8,128)S(1)}, f32[8,128]{1,0:T(8,128)S(1)}, u32[]{:S(2)}, u32[]{:S(2)}) collective-permute-start(f32[8,128]{1,0:T(8,128)S(1)} %get-tuple-element.32), channel_id=1, source_target_pairs={{2,1},{3,0},{4,3},{5,2},{6,5},{7,4},{8,7},{9,6},{10,9},{11,8},{12,... | collective-permute-start | bytes 12296 | tf_op jit(solution)/shard_map/ppermute | solution.py:179
  20.3 10.4 %collective-permute-start.1 = (f32[8,128]{1,0:T(8,128)S(1)}, f32[8,128]{1,0:T(8,128)S(1)}, u32[]{:S(2)}, u32[]{:S(2)}) collective-permute-start(f32[8,128]{1,0:T(8,128)S(1)} %get-tuple-element.33), channel_id=1, source_target_pairs={{0,3},{1,2},{2,5},{3,4},{4,7},{5,6},{6,9},{7,8},{8,11},{9,10},{10,... | collective-permute-start | bytes 12296 | tf_op jit(solution)/shard_map/ppermute | solution.py:177
  24.9 17.1 %copy-start.5 = (f32[8,128]{1,0:T(8,128)}, f32[8,128]{1,0:T(8,128)S(1)}, u32[]{:S(2)}) copy-start(f32[8,128]{1,0:T(8,128)S(1)} %collective-permute-done.2.cb_ref) | copy-start | bytes 12292
  30.7 11.3 %copy-start.6 = (f32[8,128]{1,0:T(8,128)}, f32[8,128]{1,0:T(8,128)S(1)}, u32[]{:S(2)}) copy-start(f32[8,128]{1,0:T(8,128)S(1)} %collective-permute-done.1.ca_ref) | copy-start | bytes 12292
  30.7 11.4 %copy-start.4 = (f32[32,128]{1,0:T(8,128)}, f32[32,128]{1,0:T(8,128)S(1)}, u32[]{:S(2)}) copy-start(f32[32,128]{1,0:T(8,128)S(1)} %collective-permute-done.side_ref) | copy-start | bytes 49156
  30.7 25.2 %collective-permute-start.3 = (f32[32,4096]{1,0:T(8,128)}, f32[32,4096]{1,0:T(8,128)S(1)}, u32[]{:S(2)}, u32[]{:S(2)}) collective-permute-start(f32[32,4096]{1,0:T(8,128)} %get-tuple-element.21), channel_id=1, source_target_pairs={{0,2},{2,4},{4,6},{6,8},{8,10},{10,12},{12,14},{14,16},{16,18},{18... | collective-permute-start | bytes 1572872 | tf_op jit(solution)/shard_map/ppermute | solution.py:183
  32.6 23.3 %collective-permute-start.5 = (f32[32,4096]{1,0:T(8,128)}, f32[32,4096]{1,0:T(8,128)S(1)}, u32[]{:S(2)}, u32[]{:S(2)}) collective-permute-start(f32[32,4096]{1,0:T(8,128)} %get-tuple-element.23), channel_id=1, source_target_pairs={{2,0},{4,2},{6,4},{8,6},{10,8},{12,10},{14,12},{16,14},{18,16},{20... | collective-permute-start | bytes 1572872 | tf_op jit(solution)/shard_map/ppermute | solution.py:184
  42.0 0.8 %copy-start = (f32[32,4224]{1,0:T(8,128)}, f32[32,4224]{1,0:T(8,128)S(1)}, u32[]{:S(2)}) copy-start(f32[32,4224]{1,0:T(8,128)S(1)} %collective-permute-done.4.am.al.ar.ap) | copy-start | bytes 1622020
  42.8 0.8 %copy-start.1 = (f32[32,4224]{1,0:T(8,128)}, f32[32,4224]{1,0:T(8,128)S(1)}, u32[]{:S(2)}) copy-start(f32[32,4224]{1,0:T(8,128)S(1)} %collective-permute-done.6.bm.bl.br.bp) | copy-start | bytes 1622020
  55.9 0.8 %copy-start.2 = (f32[32,4096]{1,0:T(8,128)}, f32[32,4096]{1,0:T(8,128)S(1)}, u32[]{:S(2)}) copy-start(f32[32,4096]{1,0:T(8,128)S(1)} %collective-permute-done.3.am.al.ar) | copy-start | bytes 1572868
  55.9 1.0 %copy-start.3 = (f32[32,4096]{1,0:T(8,128)}, f32[32,4096]{1,0:T(8,128)S(1)}, u32[]{:S(2)}) copy-start(f32[32,4096]{1,0:T(8,128)S(1)} %collective-permute-done.5.bm.bl.br) | copy-start | bytes 1572868

commit v9 on v4

--- a/solution.py
+++ b/solution.py
@@ -33,12 +33,13 @@
         return exx, eyy, exy
 
     degrade = (1.0 - dmg) ** 2 + 0.001
+    degrade2 = degrade * 2.0
 
     def accel(exx, eyy, exy):
         trace = exx + eyy
         sxx = jnp.where(valid, degrade * (trace + 2.0 * exx), zero)
         syy = jnp.where(valid, degrade * (trace + 2.0 * eyy), zero)
-        sxy = jnp.where(valid, degrade * 2.0 * exy, zero)
+        sxy = jnp.where(valid, degrade2 * exy, zero)
         a0 = ((sh(sxx, 1, 0) - sh(sxx, -1, 0)) + (sh(sxy, 1, 1) - sh(sxy, -1, 1))) * 0.5
         a1 = ((sh(sxy, 1, 0) - sh(sxy, -1, 0)) + (sh(syy, 1, 1) - sh(syy, -1, 1))) * 0.5
         return a0, a1
@@ -222,9 +223,9 @@
 
         u0, u1, v0, v1, d, h, t = [window(k) for k in range(nf)]
         shape = d.shape
-        grow = lax.broadcasted_iota(jnp.int32, shape, 0) + (pos_ref[0] * rows - HR)
-        gcol = lax.broadcasted_iota(jnp.int32, shape, 1) + (pos_ref[1] * cols + j * BW - HC)
-        valid = (grow >= 0) & (grow < total_rows) & (gcol >= 0) & (gcol < total_cols)
+        grow = lax.broadcasted_iota(jnp.int32, (shape[0], 1), 0) + (pos_ref[0] * rows - HR)
+        gcol = lax.broadcasted_iota(jnp.int32, (1, shape[1]), 1) + (pos_ref[1] * cols + j * BW - HC)
+        valid = ((grow >= 0) & (grow < total_rows)) & ((gcol >= 0) & (gcol < total_cols))
         n0, n1, w0, w1, hn, d3 = step_fields(u0, u1, v0, v1, d, h, t, valid, rl)
 
         def core(x):

time: 60 us -> 59.8 us (level)
  no operation moved by 1% of the time
where the time goes in v9:
time: 59.8 us; the launch traced here: 58.8 us
  Pallas kernels  25.7 us (43%)
  starting transfers between devices  14.8 us (25%)
  waiting for transfers between devices  14.3 us (24%)
  local copies, waits for them, and re-layouts  2.67 us (4%)
  between operations  0.7 us (1%)
  other arithmetic  0.61 us (1%)
    pallas_call x1, Pallas kernels, on_device(): pl.pallas_call(kernel, grid=(nblocks,), in_specs=[smem, main2, left2, rig...  21.9 us
    ppermute x1, waiting for transfers between devices, on_device(): lax.ppermute(col_s[:8], both, [((i + 1) * 2 + g, i * 2 + 1 - g) for i in...  9.58 us
    ppermute x1, starting transfers between devices, on_device(): above = lax.ppermute(bot_s, 'gx', [(i, i + 1) for i in range(nx - 1)])  5.21 us
    ppermute x1, starting transfers between devices, on_device(): lax.ppermute(col_s[:8], both, [((i + 1) * 2 + g, i * 2 + 1 - g) for i in...  4.72 us
    ppermute x1, waiting for transfers between devices, on_device(): lax.ppermute(col_s[rows - 8:], both, [(i * 2 + g, (i + 1) * 2 + 1 - g) fo...  4.69 us
    pallas_call x1, Pallas kernels, on_device(): pl.pallas_call(pack_kernel, grid=(cols // pw,), in_specs=[smem, t2, t2, t...  3.78 us
    ppermute x1, starting transfers between devices, on_device(): lax.ppermute(col_s[rows - 8:], both, [(i * 2 + g, (i + 1) * 2 + 1 - g) fo...  2.58 us
    unnamed x10, local copies, waits for them, and re-layouts  1.95 us
  transfers between devices with their start and end apart: 5, of which 2 were waited for; matrix products, arithmetic and copies ran while one was open for 1% of the time, Pallas kernels for 0%

profile of v9, /device:TPU:89, one launch (start us, length us, event | category | flops | bytes accessed | tf_op | source)
XLA Modules:
  0.0 58.8 jit_solution(8912356691157781071)
XLA Ops:
  0.6 0.6 %pad_add_fusion.pos_ref = s32[2]{0:T(128)} fusion(s32[1]{0:T(128)} %bitcast.1, s32[1]{0:T(128)} %bitcast), kind=kLoop, calls=%fused_computation | loop fusion | flops 2 | bytes 16 | tf_op jit(solution)/shard_map/stack | solution.py:93
  1.2 3.8 %shard_map.84 = (f32[32,8192]{1,0:T(8,128)}, f32[32,8192]{1,0:T(8,128)}, f32[32,128]{1,0:T(8,128)}) custom-call(s32[2]{0:T(128)} %pad_add_fusion.pos_ref, f32[2,32,8192]{2,1,0:T(8,128)} %ur.1, f32[2,32,8192]{2,1,0:T(8,128)} %vr.1, f32[32,8192]{1,0:T(8,128)} %dr.1, f32[32,8192]{1,0:T(8,128)} %hr.1, f32[32,8192]{1,0:T(8,128)} %tr.1, f32[2,32,8192]{2,1,0:T(8,128)} %ur.1, ...), custom_call_target="tpu_custom_call" | custom-call | tf_op jit(solution)/shard_map/pallas_call | solution.py:153
  5.0 5.2 %collective-permute-start = (f32[32,8192]{1,0:T(8,128)}, f32[32,8192]{1,0:T(8,128)S(1)}, u32[]{:S(2)}, u32[]{:S(2)}) collective-permute-start(f32[32,8192]{1,0:T(8,128)} %get-tuple-element.7), channel_id=1, source_target_pairs={{0,2},{2,4},{4,6},{6,8},{8,10},{10,12},{12,14},{14,16},{16,18},{18... | collective-permute-start | bytes 3145736 | tf_op jit(solution)/shard_map/ppermute | solution.py:164
  10.2 1.9 %collective-permute-start.1 = (f32[32,8192]{1,0:T(8,128)}, f32[32,8192]{1,0:T(8,128)S(1)}, u32[]{:S(2)}, u32[]{:S(2)}) collective-permute-start(f32[32,8192]{1,0:T(8,128)} %get-tuple-element.8), channel_id=1, source_target_pairs={{2,0},{4,2},{6,4},{8,6},{10,8},{12,10},{14,12},{16,14},{18,16},{20... | collective-permute-start | bytes 3145736 | tf_op jit(solution)/shard_map/ppermute | solution.py:165
  12.2 0.4 collective-permute-start.2
  12.6 0.7 %fusion = (f32[8,128]{1,0:T(8,128)S(1)}, f32[8,128]{1,0:T(8,128)S(1)}) fusion(f32[32,128]{1,0:T(8,128)} %get-tuple-element.9), kind=kLoop, calls=%fused_computation.1 | loop fusion | bytes 16384 | tf_op jit(solution)/shard_map/slice | solution.py:170
  13.3 4.7 %collective-permute-start.4 = (f32[8,128]{1,0:T(8,128)S(1)}, f32[8,128]{1,0:T(8,128)S(1)}, u32[]{:S(2)}, u32[]{:S(2)}) collective-permute-start(f32[8,128]{1,0:T(8,128)S(1)} %get-tuple-element.10), channel_id=1, source_target_pairs={{2,1},{3,0},{4,3},{5,2},{6,5},{7,4},{8,7},{9,6},{10,9},{11,8},{12,... | collective-permute-start | bytes 12296 | tf_op jit(solution)/shard_map/ppermute | solution.py:170
  18.0 2.6 %collective-permute-start.3 = (f32[8,128]{1,0:T(8,128)S(1)}, f32[8,128]{1,0:T(8,128)S(1)}, u32[]{:S(2)}, u32[]{:S(2)}) collective-permute-start(f32[8,128]{1,0:T(8,128)S(1)} %get-tuple-element.11), channel_id=1, source_target_pairs={{0,3},{1,2},{2,5},{3,4},{4,7},{5,6},{6,9},{7,8},{8,11},{9,10},{10,... | collective-permute-start | bytes 12296 | tf_op jit(solution)/shard_map/ppermute | solution.py:168
  20.6 9.6 %collective-permute-done.4.cb_ref = f32[8,128]{1,0:T(8,128)S(1)} collective-permute-done((f32[8,128]{1,0:T(8,128)S(1)}, f32[8,128]{1,0:T(8,128)S(1)}, u32[]{:S(2)}, u32[]{:S(2)}) %collective-permute-start.4) | collective-permute-done | bytes 4128 | tf_op jit(solution)/shard_map/ppermute | solution.py:170
  30.2 0.0 copy-start.3
  30.2 4.7 %collective-permute-done.3.ca_ref = f32[8,128]{1,0:T(8,128)S(1)} collective-permute-done((f32[8,128]{1,0:T(8,128)S(1)}, f32[8,128]{1,0:T(8,128)S(1)}, u32[]{:S(2)}, u32[]{:S(2)}) %collective-permute-start.3) | collective-permute-done | bytes 4128 | tf_op jit(solution)/shard_map/ppermute | solution.py:168
  34.9 0.0 copy-start.4
  34.9 0.0 collective-permute-done.2.side_ref
  34.9 0.0 copy-start.2
  34.9 0.0 collective-permute-done.am.al.ar
  34.9 0.0 copy-start
  34.9 0.0 collective-permute-done.1.bm.bl.br
  34.9 0.0 copy-done.3
  34.9 0.5 copy-done.4
  35.5 0.0 copy-done.2
  35.5 0.4 copy-done
  35.9 0.0 copy-start.1
  35.9 1.0 %copy-done.1 = f32[32,8192]{1,0:T(8,128)} copy-done((f32[32,8192]{1,0:T(8,128)}, f32[32,8192]{1,0:T(8,128)S(1)}, u32[]{:S(2)}) %copy-start.1) | copy-done | bytes 1048600
  36.9 21.9 %shard_map.85 = (f32[2,32,8192]{2,1,0:T(8,128)}, f32[2,32,8192]{2,1,0:T(8,128)}, f32[32,8192]{1,0:T(8,128)}, f32[32,8192]{1,0:T(8,128)}) custom-call(s32[2]{0:T(128)} %pad_add_fusion.pos_ref, f32[2,32,8192]{2,1,0:T(8,128)} %ur.1, f32[2,32,8192]{2,1,0:T(8,128)} %ur.1, f32[2,32,8192]{2,1,0:T(8,128)} %ur.1, f32[2,32,8192]{2,1,0:T(8,128)} %vr.1, ...), custom_call_target="tpu_custom_call" | custom-call | tf_op jit(solution)/shard_map/pallas_call | solution.py:260
Async XLA Ops:
  5.0 29.9 %collective-permute-start = (f32[32,8192]{1,0:T(8,128)}, f32[32,8192]{1,0:T(8,128)S(1)}, u32[]{:S(2)}, u32[]{:S(2)}) collective-permute-start(f32[32,8192]{1,0:T(8,128)} %get-tuple-element.7), channel_id=1, source_target_pairs={{0,2},{2,4},{4,6},{6,8},{8,10},{10,12},{12,14},{14,16},{16,18},{18... | collective-permute-start | bytes 3145736 | tf_op jit(solution)/shard_map/ppermute | solution.py:164
  10.2 24.7 %collective-permute-start.1 = (f32[32,8192]{1,0:T(8,128)}, f32[32,8192]{1,0:T(8,128)S(1)}, u32[]{:S(2)}, u32[]{:S(2)}) collective-permute-start(f32[32,8192]{1,0:T(8,128)} %get-tuple-element.8), channel_id=1, source_target_pairs={{2,0},{4,2},{6,4},{8,6},{10,8},{12,10},{14,12},{16,14},{18,16},{20... | collective-permute-start | bytes 3145736 | tf_op jit(solution)/shard_map/ppermute | solution.py:165
  12.2 22.7 %collective-permute-start.2 = (f32[32,128]{1,0:T(8,128)}, f32[32,128]{1,0:T(8,128)S(1)}, u32[]{:S(2)}, u32[]{:S(2)}) collective-permute-start(f32[32,128]{1,0:T(8,128)} %get-tuple-element.9), channel_id=1, source_target_pairs={{0,1},{1,0},{2,3},{3,2},{4,5},{5,4},{6,7},{7,6},{8,9},{9,8},{10,11... | collective-permute-start | bytes 49160 | tf_op jit(solution)/shard_map/ppermute | solution.py:166
  13.3 16.9 %collective-permute-start.4 = (f32[8,128]{1,0:T(8,128)S(1)}, f32[8,128]{1,0:T(8,128)S(1)}, u32[]{:S(2)}, u32[]{:S(2)}) collective-permute-start(f32[8,128]{1,0:T(8,128)S(1)} %get-tuple-element.10), channel_id=1, source_target_pairs={{2,1},{3,0},{4,3},{5,2},{6,5},{7,4},{8,7},{9,6},{10,9},{11,8},{12,... | collective-permute-start | bytes 12296 | tf_op jit(solution)/shard_map/ppermute | solution.py:170
  18.0 16.9 %collective-permute-start.3 = (f32[8,128]{1,0:T(8,128)S(1)}, f32[8,128]{1,0:T(8,128)S(1)}, u32[]{:S(2)}, u32[]{:S(2)}) collective-permute-start(f32[8,128]{1,0:T(8,128)S(1)} %get-tuple-element.11), channel_id=1, source_target_pairs={{0,3},{1,2},{2,5},{3,4},{4,7},{5,6},{6,9},{7,8},{8,11},{9,10},{10,... | collective-permute-start | bytes 12296 | tf_op jit(solution)/shard_map/ppermute | solution.py:168
  30.2 4.7 %copy-start.3 = (f32[8,128]{1,0:T(8,128)}, f32[8,128]{1,0:T(8,128)S(1)}, u32[]{:S(2)}) copy-start(f32[8,128]{1,0:T(8,128)S(1)} %collective-permute-done.4.cb_ref) | copy-start | bytes 12292
  34.9 0.6 %copy-start.4 = (f32[8,128]{1,0:T(8,128)}, f32[8,128]{1,0:T(8,128)S(1)}, u32[]{:S(2)}) copy-start(f32[8,128]{1,0:T(8,128)S(1)} %collective-permute-done.3.ca_ref) | copy-start | bytes 12292
  34.9 0.6 %copy-start.2 = (f32[32,128]{1,0:T(8,128)}, f32[32,128]{1,0:T(8,128)S(1)}, u32[]{:S(2)}) copy-start(f32[32,128]{1,0:T(8,128)S(1)} %collective-permute-done.2.side_ref) | copy-start | bytes 49156
  34.9 1.0 %copy-start = (f32[32,8192]{1,0:T(8,128)}, f32[32,8192]{1,0:T(8,128)S(1)}, u32[]{:S(2)}) copy-start(f32[32,8192]{1,0:T(8,128)S(1)} %collective-permute-done.am.al.ar) | copy-start | bytes 3145732
  35.9 1.0 %copy-start.1 = (f32[32,8192]{1,0:T(8,128)}, f32[32,8192]{1,0:T(8,128)S(1)}, u32[]{:S(2)}) copy-start(f32[32,8192]{1,0:T(8,128)S(1)} %collective-permute-done.1.bm.bl.br) | copy-start | bytes 3145732

commit v10 on v9

--- a/solution.py
+++ b/solution.py
@@ -78,6 +78,7 @@
 RADII = (5, 5, 5, 5, 4, 2, 3)
 OFFSETS = tuple(sum(RADII[:k]) for k in range(len(RADII)))
 STRIP = 32
+SENT = sum(RADII)
 LANE_W = 5
 
 
@@ -123,8 +124,8 @@
             top = jnp.where(inside, x, top)
             y = roll(jnp.concatenate([bots[k], pad], axis=0), o - (8 - r), 0)
             bot = jnp.where(inside, y, bot)
-        top_o[...] = top
-        bot_o[...] = bot
+        top_o[...] = top[:SENT]
+        bot_o[...] = bot[:SENT]
 
         @pl.when(j == 0)
         def _():
@@ -154,9 +155,9 @@
         pack_kernel,
         grid=(cols // pw,),
         in_specs=[smem, t2, t2, t1, t1, t1, b2, b2, b1, b1, b1, l2, l2, l1, l1, l1, r2, r2, r1, r1, r1],
-        out_specs=[pl.BlockSpec((STRIP, pw), lambda j: (0, j)), pl.BlockSpec((STRIP, pw), lambda j: (0, j)),
+        out_specs=[pl.BlockSpec((SENT, pw), lambda j: (0, j)), pl.BlockSpec((SENT, pw), lambda j: (0, j)),
                    pl.BlockSpec((rows, HC), lambda j: (0, 0))],
-        out_shape=[jax.ShapeDtypeStruct((STRIP, cols), f32), jax.ShapeDtypeStruct((STRIP, cols), f32),
+        out_shape=[jax.ShapeDtypeStruct((SENT, cols), f32), jax.ShapeDtypeStruct((SENT, cols), f32),
                    jax.ShapeDtypeStruct((rows, HC), f32)],
         interpret=INTERPRET,
     )(pos, *ins, *ins, *ins, *ins)
@@ -194,20 +195,24 @@
             y = roll(x, -LANE_W * k, 1)
             return jnp.where((lidx < LANE_W) & has_right, y, 0.0)
 
-        def above_tile(x, k):
+        def tile_of(ref, k, first_row):
             r, o = RADII[k], OFFSETS[k]
-            y = roll(x, 8 - r - o, 0)[:8]
+            s = min(max(o + first_row + r - 8 if first_row else o, 0), SENT - 8)
+            y = ref[s:s + 8, :]
+            shift = (first_row - (o - s)) % 8
+            if shift:
+                y = roll(y, shift, 0)
             ridx = lax.broadcasted_iota(jnp.int32, y.shape, 0)
-            return jnp.where(ridx >= 8 - r, y, 0.0)
-
-        def below_tile(x, k):
-            r, o = RADII[k], OFFSETS[k]
-            y = roll(x, -o, 0)[:8]
-            ridx = lax.broadcasted_iota(jnp.int32, y.shape, 0)
-            return jnp.where(ridx < r, y, 0.0)
-
-        a_m, a_l, a_r = am[...], al[...], ar[...]
-        b_m, b_l, b_r = bm[...], bl[...], br[...]
+            return jnp.where((ridx >= first_row) & (ridx < first_row + r), y, 0.0)
+
+        def above_tile(ref, k):
+            return tile_of(ref, k, 8 - RADII[k])
+
+        def below_tile(ref, k):
+            return tile_of(ref, k, 0)
+
+        a_m, a_l, a_r = am, al, ar
+        b_m, b_l, b_r = bm, bl, br
 
         def window(k):
             lft = jnp.where(first, lane_left(side_v, k), lefts[k])
@@ -250,9 +255,9 @@
     main1 = pl.BlockSpec((rows, BW), lambda j: (0, j))
     left1 = pl.BlockSpec((rows, HC), lambda j: (0, lcol(j)))
     right1 = pl.BlockSpec((rows, HC), lambda j: (0, rcol(j)))
-    sm = pl.BlockSpec((STRIP, BW), lambda j: (0, j))
-    sl = pl.BlockSpec((STRIP, HC), lambda j: (0, lcol(j)))
-    sr = pl.BlockSpec((STRIP, HC), lambda j: (0, rcol(j)))
+    sm = pl.BlockSpec((SENT, BW), lambda j: (0, j))
+    sl = pl.BlockSpec((SENT, HC), lambda j: (0, lcol(j)))
+    sr = pl.BlockSpec((SENT, HC), lambda j: (0, rcol(j)))
     sidespec = pl.BlockSpec((rows, HC), lambda j: (0, 0))
     cornerspec = pl.BlockSpec((8, HC), lambda j: (0, 0))
     out2 = pl.BlockSpec((2, rows, BW), lambda j: (0, 0, j))

time: 59.8 us -> 59.9 us (level)
  no operation moved by 1% of the time
where the time goes in v10:
time: 59.9 us; the launch traced here: 58.9 us
  Pallas kernels  25.8 us (43%)
  starting transfers between devices  14.8 us (25%)
  waiting for transfers between devices  14.3 us (24%)
  local copies, waits for them, and re-layouts  2.67 us (4%)
  between operations  0.7 us (1%)
  other arithmetic  0.61 us (1%)
    pallas_call x1, Pallas kernels, on_device(): pl.pallas_call(kernel, grid=(nblocks,), in_specs=[smem, main2, left2, rig...  22 us
    ppermute x1, waiting for transfers between devices, on_device(): lax.ppermute(col_s[:8], both, [((i + 1) * 2 + g, i * 2 + 1 - g) for i in...  9.58 us
    ppermute x1, starting transfers between devices, on_device(): above = lax.ppermute(bot_s, 'gx', [(i, i + 1) for i in range(nx - 1)])  5.21 us
    ppermute x1, starting transfers between devices, on_device(): lax.ppermute(col_s[:8], both, [((i + 1) * 2 + g, i * 2 + 1 - g) for i in...  4.72 us
    ppermute x1, waiting for transfers between devices, on_device(): lax.ppermute(col_s[rows - 8:], both, [(i * 2 + g, (i + 1) * 2 + 1 - g) fo...  4.69 us
    pallas_call x1, Pallas kernels, on_device(): pl.pallas_call(pack_kernel, grid=(cols // pw,), in_specs=[smem, t2, t2, t...  3.78 us
    ppermute x1, starting transfers between devices, on_device(): lax.ppermute(col_s[rows - 8:], both, [(i * 2 + g, (i + 1) * 2 + 1 - g) fo...  2.58 us
    unnamed x10, local copies, waits for them, and re-layouts  1.95 us
  transfers between devices with their start and end apart: 5, of which 2 were waited for; matrix products, arithmetic and copies ran while one was open for 1% of the time, Pallas kernels for 0%

profile of v10, /device:TPU:89, one launch (start us, length us, event | category | flops | bytes accessed | tf_op | source)
XLA Modules:
  0.0 58.9 jit_solution(18171797079669031408)
XLA Ops:
  0.6 0.6 %pad_add_fusion.pos_ref = s32[2]{0:T(128)} fusion(s32[1]{0:T(128)} %bitcast.1, s32[1]{0:T(128)} %bitcast), kind=kLoop, calls=%fused_computation | loop fusion | flops 2 | bytes 16 | tf_op jit(solution)/shard_map/stack | solution.py:94
  1.2 3.8 %shard_map.84 = (f32[29,8192]{1,0:T(8,128)}, f32[29,8192]{1,0:T(8,128)}, f32[32,128]{1,0:T(8,128)}) custom-call(s32[2]{0:T(128)} %pad_add_fusion.pos_ref, f32[2,32,8192]{2,1,0:T(8,128)} %ur.1, f32[2,32,8192]{2,1,0:T(8,128)} %vr.1, f32[32,8192]{1,0:T(8,128)} %dr.1, f32[32,8192]{1,0:T(8,128)} %hr.1, f32[32,8192]{1,0:T(8,128)} %tr.1, f32[2,32,8192]{2,1,0:T(8,128)} %ur.1, ...), custom_call_target="tpu_custom_call" | custom-call | tf_op jit(solution)/shard_map/pallas_call | solution.py:154
  5.0 5.2 %collective-permute-start = (f32[29,8192]{1,0:T(8,128)}, f32[29,8192]{1,0:T(8,128)S(1)}, u32[]{:S(2)}, u32[]{:S(2)}) collective-permute-start(f32[29,8192]{1,0:T(8,128)} %get-tuple-element.7), channel_id=1, source_target_pairs={{0,2},{2,4},{4,6},{6,8},{8,10},{10,12},{12,14},{14,16},{16,18},{18... | collective-permute-start | bytes 2850824 | tf_op jit(solution)/shard_map/ppermute | solution.py:165
  10.2 1.9 %collective-permute-start.1 = (f32[29,8192]{1,0:T(8,128)}, f32[29,8192]{1,0:T(8,128)S(1)}, u32[]{:S(2)}, u32[]{:S(2)}) collective-permute-start(f32[29,8192]{1,0:T(8,128)} %get-tuple-element.8), channel_id=1, source_target_pairs={{2,0},{4,2},{6,4},{8,6},{10,8},{12,10},{14,12},{16,14},{18,16},{20... | collective-permute-start | bytes 2850824 | tf_op jit(solution)/shard_map/ppermute | solution.py:166
  12.2 0.4 collective-permute-start.2
  12.6 0.7 %fusion = (f32[8,128]{1,0:T(8,128)S(1)}, f32[8,128]{1,0:T(8,128)S(1)}) fusion(f32[32,128]{1,0:T(8,128)} %get-tuple-element.9), kind=kLoop, calls=%fused_computation.1 | loop fusion | bytes 16384 | tf_op jit(solution)/shard_map/slice | solution.py:171
  13.3 4.7 %collective-permute-start.4 = (f32[8,128]{1,0:T(8,128)S(1)}, f32[8,128]{1,0:T(8,128)S(1)}, u32[]{:S(2)}, u32[]{:S(2)}) collective-permute-start(f32[8,128]{1,0:T(8,128)S(1)} %get-tuple-element.10), channel_id=1, source_target_pairs={{2,1},{3,0},{4,3},{5,2},{6,5},{7,4},{8,7},{9,6},{10,9},{11,8},{12,... | collective-permute-start | bytes 12296 | tf_op jit(solution)/shard_map/ppermute | solution.py:171
  18.0 2.6 %collective-permute-start.3 = (f32[8,128]{1,0:T(8,128)S(1)}, f32[8,128]{1,0:T(8,128)S(1)}, u32[]{:S(2)}, u32[]{:S(2)}) collective-permute-start(f32[8,128]{1,0:T(8,128)S(1)} %get-tuple-element.11), channel_id=1, source_target_pairs={{0,3},{1,2},{2,5},{3,4},{4,7},{5,6},{6,9},{7,8},{8,11},{9,10},{10,... | collective-permute-start | bytes 12296 | tf_op jit(solution)/shard_map/ppermute | solution.py:169
  20.6 9.6 %collective-permute-done.4.cb_ref = f32[8,128]{1,0:T(8,128)S(1)} collective-permute-done((f32[8,128]{1,0:T(8,128)S(1)}, f32[8,128]{1,0:T(8,128)S(1)}, u32[]{:S(2)}, u32[]{:S(2)}) %collective-permute-start.4) | collective-permute-done | bytes 4128 | tf_op jit(solution)/shard_map/ppermute | solution.py:171
  30.2 0.0 copy-start.3
  30.2 4.7 %collective-permute-done.3.ca_ref = f32[8,128]{1,0:T(8,128)S(1)} collective-permute-done((f32[8,128]{1,0:T(8,128)S(1)}, f32[8,128]{1,0:T(8,128)S(1)}, u32[]{:S(2)}, u32[]{:S(2)}) %collective-permute-start.3) | collective-permute-done | bytes 4128 | tf_op jit(solution)/shard_map/ppermute | solution.py:169
  34.9 0.0 copy-start.4
  34.9 0.0 collective-permute-done.2.side_ref
  34.9 0.0 copy-start.2
  34.9 0.0 collective-permute-done.am.al.ar
  34.9 0.0 copy-start
  34.9 0.0 collective-permute-done.1.bm.bl.br
  34.9 0.0 copy-done.3
  34.9 0.5 copy-done.4
  35.5 0.0 copy-done.2
  35.5 0.4 copy-done
  35.9 0.0 copy-start.1
  35.9 1.0 %copy-done.1 = f32[29,8192]{1,0:T(8,128)} copy-done((f32[29,8192]{1,0:T(8,128)}, f32[29,8192]{1,0:T(8,128)S(1)}, u32[]{:S(2)}) %copy-start.1) | copy-done | bytes 950296
  36.9 22.0 %shard_map.85 = (f32[2,32,8192]{2,1,0:T(8,128)}, f32[2,32,8192]{2,1,0:T(8,128)}, f32[32,8192]{1,0:T(8,128)}, f32[32,8192]{1,0:T(8,128)}) custom-call(s32[2]{0:T(128)} %pad_add_fusion.pos_ref, f32[2,32,8192]{2,1,0:T(8,128)} %ur.1, f32[2,32,8192]{2,1,0:T(8,128)} %ur.1, f32[2,32,8192]{2,1,0:T(8,128)} %ur.1, f32[2,32,8192]{2,1,0:T(8,128)} %vr.1, ...), custom_call_target="tpu_custom_call" | custom-call | tf_op jit(solution)/shard_map/pallas_call | solution.py:265
Async XLA Ops:
  5.0 29.9 %collective-permute-start = (f32[29,8192]{1,0:T(8,128)}, f32[29,8192]{1,0:T(8,128)S(1)}, u32[]{:S(2)}, u32[]{:S(2)}) collective-permute-start(f32[29,8192]{1,0:T(8,128)} %get-tuple-element.7), channel_id=1, source_target_pairs={{0,2},{2,4},{4,6},{6,8},{8,10},{10,12},{12,14},{14,16},{16,18},{18... | collective-permute-start | bytes 2850824 | tf_op jit(solution)/shard_map/ppermute | solution.py:165
  10.2 24.7 %collective-permute-start.1 = (f32[29,8192]{1,0:T(8,128)}, f32[29,8192]{1,0:T(8,128)S(1)}, u32[]{:S(2)}, u32[]{:S(2)}) collective-permute-start(f32[29,8192]{1,0:T(8,128)} %get-tuple-element.8), channel_id=1, source_target_pairs={{2,0},{4,2},{6,4},{8,6},{10,8},{12,10},{14,12},{16,14},{18,16},{20... | collective-permute-start | bytes 2850824 | tf_op jit(solution)/shard_map/ppermute | solution.py:166
  12.2 22.7 %collective-permute-start.2 = (f32[32,128]{1,0:T(8,128)}, f32[32,128]{1,0:T(8,128)S(1)}, u32[]{:S(2)}, u32[]{:S(2)}) collective-permute-start(f32[32,128]{1,0:T(8,128)} %get-tuple-element.9), channel_id=1, source_target_pairs={{0,1},{1,0},{2,3},{3,2},{4,5},{5,4},{6,7},{7,6},{8,9},{9,8},{10,11... | collective-permute-start | bytes 49160 | tf_op jit(solution)/shard_map/ppermute | solution.py:167
  13.3 16.9 %collective-permute-start.4 = (f32[8,128]{1,0:T(8,128)S(1)}, f32[8,128]{1,0:T(8,128)S(1)}, u32[]{:S(2)}, u32[]{:S(2)}) collective-permute-start(f32[8,128]{1,0:T(8,128)S(1)} %get-tuple-element.10), channel_id=1, source_target_pairs={{2,1},{3,0},{4,3},{5,2},{6,5},{7,4},{8,7},{9,6},{10,9},{11,8},{12,... | collective-permute-start | bytes 12296 | tf_op jit(solution)/shard_map/ppermute | solution.py:171
  18.0 16.9 %collective-permute-start.3 = (f32[8,128]{1,0:T(8,128)S(1)}, f32[8,128]{1,0:T(8,128)S(1)}, u32[]{:S(2)}, u32[]{:S(2)}) collective-permute-start(f32[8,128]{1,0:T(8,128)S(1)} %get-tuple-element.11), channel_id=1, source_target_pairs={{0,3},{1,2},{2,5},{3,4},{4,7},{5,6},{6,9},{7,8},{8,11},{9,10},{10,... | collective-permute-start | bytes 12296 | tf_op jit(solution)/shard_map/ppermute | solution.py:169
  30.2 4.7 %copy-start.3 = (f32[8,128]{1,0:T(8,128)}, f32[8,128]{1,0:T(8,128)S(1)}, u32[]{:S(2)}) copy-start(f32[8,128]{1,0:T(8,128)S(1)} %collective-permute-done.4.cb_ref) | copy-start | bytes 12292
  34.9 0.6 %copy-start.4 = (f32[8,128]{1,0:T(8,128)}, f32[8,128]{1,0:T(8,128)S(1)}, u32[]{:S(2)}) copy-start(f32[8,128]{1,0:T(8,128)S(1)} %collective-permute-done.3.ca_ref) | copy-start | bytes 12292
  34.9 0.6 %copy-start.2 = (f32[32,128]{1,0:T(8,128)}, f32[32,128]{1,0:T(8,128)S(1)}, u32[]{:S(2)}) copy-start(f32[32,128]{1,0:T(8,128)S(1)} %collective-permute-done.2.side_ref) | copy-start | bytes 49156
  34.9 1.0 %copy-start = (f32[29,8192]{1,0:T(8,128)}, f32[29,8192]{1,0:T(8,128)S(1)}, u32[]{:S(2)}) copy-start(f32[29,8192]{1,0:T(8,128)S(1)} %collective-permute-done.am.al.ar) | copy-start | bytes 2850820
  35.9 1.0 %copy-start.1 = (f32[29,8192]{1,0:T(8,128)}, f32[29,8192]{1,0:T(8,128)S(1)}, u32[]{:S(2)}) copy-start(f32[29,8192]{1,0:T(8,128)S(1)} %collective-permute-done.1.bm.bl.br) | copy-start | bytes 2850820

commit v11 on v10

--- a/solution.py
+++ b/solution.py
@@ -108,9 +108,7 @@
 
     pw = cols
 
-    def pack_kernel(pos_ref, tu, tv, td, th, tt, bu, bv, bd, bh, bt,
-                    lu, lv, ld, lh, lt, ru, rv, rd, rh, rt, top_o, bot_o, col_o):
-        j = pl.program_id(0)
+    def pack_kernel(tu, tv, td, th, tt, bu, bv, bd, bh, bt, after, top_o, bot_o):
         tops = split((tu, tv, td, th, tt))
         bots = split((bu, bv, bd, bh, bt))
         ridx = lax.broadcasted_iota(jnp.int32, (STRIP, pw), 0)
@@ -127,19 +125,19 @@
         top_o[...] = top[:SENT]
         bot_o[...] = bot[:SENT]
 
-        @pl.when(j == 0)
-        def _():
-            lefts = split((lu, lv, ld, lh, lt))
-            rights = split((ru, rv, rd, rh, rt))
-            lidx = lax.broadcasted_iota(jnp.int32, (rows, HC), 1)
-            col = jnp.zeros((rows, HC), f32)
-            to_right = pos_ref[1] == 0
-            for k in range(nf):
-                inside = (lidx >= LANE_W * k) & (lidx < LANE_W * (k + 1))
-                a = roll(rights[k], LANE_W * k - (HC - LANE_W), 1)
-                b = roll(lefts[k], LANE_W * k, 1)
-                col = jnp.where(inside, jnp.where(to_right, a, b), col)
-            col_o[...] = col
+
+    def col_kernel(pos_ref, lu, lv, ld, lh, lt, ru, rv, rd, rh, rt, col_o):
+        lefts = split((lu, lv, ld, lh, lt))
+        rights = split((ru, rv, rd, rh, rt))
+        lidx = lax.broadcasted_iota(jnp.int32, (rows, HC), 1)
+        col = jnp.zeros((rows, HC), f32)
+        to_right = pos_ref[1] == 0
+        for k in range(nf):
+            inside = (lidx >= LANE_W * k) & (lidx < LANE_W * (k + 1))
+            a = roll(rights[k], LANE_W * k - (HC - LANE_W), 1)
+            b = roll(lefts[k], LANE_W * k, 1)
+            col = jnp.where(inside, jnp.where(to_right, a, b), col)
+        col_o[...] = col
 
     t2 = pl.BlockSpec((2, 8, pw), lambda j: (0, 0, j))
     t1 = pl.BlockSpec((8, pw), lambda j: (0, j))
@@ -151,25 +149,33 @@
     r1 = pl.BlockSpec((rows, HC), lambda j: (0, last_col_block))
     smem = pl.BlockSpec(memory_space=pltpu.SMEM)
     ins = (displacement, velocity, damage, history, toughness)
-    top_s, bot_s, col_s = pl.pallas_call(
+    col_s = pl.pallas_call(
+        col_kernel,
+        grid=(1,),
+        in_specs=[smem, l2, l2, l1, l1, l1, r2, r2, r1, r1, r1],
+        out_specs=pl.BlockSpec((rows, HC), lambda j: (0, 0)),
+        out_shape=jax.ShapeDtypeStruct((rows, HC), f32),
+        interpret=INTERPRET,
+    )(pos, *ins, *ins)
+    top_s, bot_s = pl.pallas_call(
         pack_kernel,
         grid=(cols // pw,),
-        in_specs=[smem, t2, t2, t1, t1, t1, b2, b2, b1, b1, b1, l2, l2, l1, l1, l1, r2, r2, r1, r1, r1],
-        out_specs=[pl.BlockSpec((SENT, pw), lambda j: (0, j)), pl.BlockSpec((SENT, pw), lambda j: (0, j)),
-                   pl.BlockSpec((rows, HC), lambda j: (0, 0))],
-        out_shape=[jax.ShapeDtypeStruct((SENT, cols), f32), jax.ShapeDtypeStruct((SENT, cols), f32),
-                   jax.ShapeDtypeStruct((rows, HC), f32)],
+        in_specs=[t2, t2, t1, t1, t1, b2, b2, b1, b1, b1, pl.BlockSpec((8, HC), lambda j: (0, 0))],
+        out_specs=[pl.BlockSpec((SENT, pw), lambda j: (0, j)), pl.BlockSpec((SENT, pw), lambda j: (0, j))],
+        out_shape=[jax.ShapeDtypeStruct((SENT, cols), f32), jax.ShapeDtypeStruct((SENT, cols), f32)],
         interpret=INTERPRET,
-    )(pos, *ins, *ins, *ins, *ins)
-
-    above = lax.ppermute(bot_s, "gx", [(i, i + 1) for i in range(nx - 1)])
-    below = lax.ppermute(top_s, "gx", [(i + 1, i) for i in range(nx - 1)])
+    )(*ins, *ins, col_s)
+
     side = lax.ppermute(col_s, "gy", [(0, 1), (1, 0)])
     both = ("gx", "gy")
     corner_above = lax.ppermute(col_s[rows - 8:], both,
                                 [(i * 2 + g, (i + 1) * 2 + 1 - g) for i in range(nx - 1) for g in range(2)])
     corner_below = lax.ppermute(col_s[:8], both,
                                 [((i + 1) * 2 + g, i * 2 + 1 - g) for i in range(nx - 1) for g in range(2)])
+    side, corner_above, corner_below, top_s, bot_s = lax.optimization_barrier(
+        (side, corner_above, corner_below, top_s, bot_s))
+    above = lax.ppermute(bot_s, "gx", [(i, i + 1) for i in range(nx - 1)])
+    below = lax.ppermute(top_s, "gx", [(i + 1, i) for i in range(nx - 1)])
 
     def kernel(pos_ref, um, ul, ur, vm, vl, vr, dm, dl, dr, hm, hl, hr, tm, tl, tr,
                am, al, ar, bm, bl, br, side_ref, ca_ref, cb_ref, uo, vo, ho, do):

time: 59.9 us -> 72.1 us (1.20)
  waiting for transfers between devices: 14.3 us -> 27.1 us
  Pallas kernels: 25.8 us -> 27.1 us
  local copies, waits for them, and re-layouts: 2.67 us -> 1.73 us
  starting transfers between devices: 14.8 us -> 13.9 us
    ppermute x1, waiting for transfers between devices: 0.01 us -> 16.1 us  [on_device(): above = lax.ppermute(bot_s, 'gx', [(i, i + 1) for i in range(nx - 1)])]
    ppermute x1, waiting for transfers between devices: 0.01 us -> 11 us  [on_device(): below = lax.ppermute(top_s, 'gx', [(i + 1, i) for i in range(nx - 1)])]
    ppermute x1, waiting for transfers between devices: 9.58 us -> 0.01 us  [on_device(): lax.ppermute(col_s[:8], both, [((i + 1) * 2 + g, i * 2 + 1 - g) for i in...]
    ppermute x1, waiting for transfers between devices: 4.69 us -> 0.01 us  [on_device(): lax.ppermute(col_s[rows - 8:], both, [(i * 2 + g, (i + 1) * 2 + 1 - g) fo...]
    ppermute x1, starting transfers between devices: 4.72 us -> 2.99 us  [on_device(): lax.ppermute(col_s[:8], both, [((i + 1) * 2 + g, i * 2 + 1 - g) for i in...]
    pallas_call x1 -> x2, Pallas kernels: 3.78 us -> 5.13 us  [the longest x1 3.52 us: on_device(): pl.pallas_call(pack_kernel, grid=(cols // pw,), in_specs=[t2, t2, t1, t1,...]
    ppermute x1, starting transfers between devices: 5.21 us -> 3.99 us  [on_device(): above = lax.ppermute(bot_s, 'gx', [(i, i + 1) for i in range(nx - 1)])]
    ppermute x1, starting transfers between devices: 2.58 us -> 3.77 us  [on_device(): lax.ppermute(col_s[rows - 8:], both, [(i * 2 + g, (i + 1) * 2 + 1 - g) fo...]
  transfers between devices with their start and end apart: 5 -> 5, of which waited for: 2 -> 2; matrix products, arithmetic and copies ran while one was open for 1% -> 1% of each run, Pallas kernels for 0% -> 5%
where the time goes in v11:
time: 72.1 us; the launch traced here: 71.2 us
  Pallas kernels  27.1 us (38%)
  waiting for transfers between devices  27.1 us (38%)
  starting transfers between devices  13.9 us (19%)
  local copies, waits for them, and re-layouts  1.73 us (2%)
  between operations  0.73 us (1%)
    pallas_call x1, Pallas kernels, on_device(): pl.pallas_call(kernel, grid=(nblocks,), in_specs=[smem, main2, left2, rig...  22 us
    ppermute x1, waiting for transfers between devices, on_device(): above = lax.ppermute(bot_s, 'gx', [(i, i + 1) for i in range(nx - 1)])  16.1 us
    ppermute x1, waiting for transfers between devices, on_device(): below = lax.ppermute(top_s, 'gx', [(i + 1, i) for i in range(nx - 1)])  11 us
    ppermute x1, starting transfers between devices, on_device(): above = lax.ppermute(bot_s, 'gx', [(i, i + 1) for i in range(nx - 1)])  3.99 us
    ppermute x1, starting transfers between devices, on_device(): lax.ppermute(col_s[rows - 8:], both, [(i * 2 + g, (i + 1) * 2 + 1 - g) fo...  3.77 us
    pallas_call x1, Pallas kernels, on_device(): pl.pallas_call(pack_kernel, grid=(cols // pw,), in_specs=[t2, t2, t1, t1,...  3.52 us
    ppermute x1, starting transfers between devices, on_device(): lax.ppermute(col_s[:8], both, [((i + 1) * 2 + g, i * 2 + 1 - g) for i in...  2.99 us
    ppermute x1, starting transfers between devices, on_device(): below = lax.ppermute(top_s, 'gx', [(i + 1, i) for i in range(nx - 1)])  1.92 us
  transfers between devices with their start and end apart: 5, of which 2 were waited for; matrix products, arithmetic and copies ran while one was open for 1% of the time, Pallas kernels for 5%

profile of v11, /device:TPU:89, one launch (start us, length us, event | category | flops | bytes accessed | tf_op | source)
XLA Modules:
  0.0 71.2 jit_solution(12694845328010315075)
XLA Ops:
  0.6 0.6 pad_add_fusion.pos_ref
  1.2 1.6 %shard_map.84.after = f32[32,128]{1,0:T(8,128)} custom-call(s32[2]{0:T(128)} %pad_add_fusion.pos_ref, f32[2,32,8192]{2,1,0:T(8,128)} %ur.1, f32[2,32,8192]{2,1,0:T(8,128)} %vr.1, f32[32,8192]{1,0:T(8,128)} %dr.1, f32[32,8192]{1,0:T(8,128)} %hr.1, f32[32,8192]{1,0:T(8,128)} %tr.1, f32[2,32,8192]{2,1,0:T(8,128)} %ur.1, f32[2,32,8192]{2,1,0:T(8,128)} %vr.1, ...), custom_call_target="tpu_custom_call" | custom-call | tf_op jit(solution)/shard_map/pallas_call | solution.py:152
  2.9 1.2 %collective-permute-start = (f32[32,128]{1,0:T(8,128)}, f32[32,128]{1,0:T(8,128)S(1)}, u32[]{:S(2)}, u32[]{:S(2)}) collective-permute-start(f32[32,128]{1,0:T(8,128)} %shard_map.84.after), channel_id=1, source_target_pairs={{0,1},{1,0},{2,3},{3,2},{4,5},{5,4},{6,7},{7,6},{8,9},{9,8},{10,11... | collective-permute-start | bytes 49160 | tf_op jit(solution)/shard_map/ppermute | solution.py:169
  4.1 0.7 %fusion = (f32[8,128]{1,0:T(8,128)S(1)}, f32[8,128]{1,0:T(8,128)S(1)}) fusion(f32[32,128]{1,0:T(8,128)} %shard_map.84.after), kind=kLoop, calls=%fused_computation.1 | loop fusion | bytes 16384 | tf_op jit(solution)/shard_map/slice | solution.py:173
  4.8 3.0 %collective-permute-start.2 = (f32[8,128]{1,0:T(8,128)S(1)}, f32[8,128]{1,0:T(8,128)S(1)}, u32[]{:S(2)}, u32[]{:S(2)}) collective-permute-start(f32[8,128]{1,0:T(8,128)S(1)} %get-tuple-element.18), channel_id=1, source_target_pairs={{2,1},{3,0},{4,3},{5,2},{6,5},{7,4},{8,7},{9,6},{10,9},{11,8},{12,... | collective-permute-start | bytes 12296 | tf_op jit(solution)/shard_map/ppermute | solution.py:173
  7.8 3.8 %collective-permute-start.1 = (f32[8,128]{1,0:T(8,128)S(1)}, f32[8,128]{1,0:T(8,128)S(1)}, u32[]{:S(2)}, u32[]{:S(2)}) collective-permute-start(f32[8,128]{1,0:T(8,128)S(1)} %get-tuple-element.19), channel_id=1, source_target_pairs={{0,3},{1,2},{2,5},{3,4},{4,7},{5,6},{6,9},{7,8},{8,11},{9,10},{10,... | collective-permute-start | bytes 12296 | tf_op jit(solution)/shard_map/ppermute | solution.py:171
  11.6 3.5 %shard_map.85 = (f32[29,8192]{1,0:T(8,128)}, f32[29,8192]{1,0:T(8,128)}) custom-call(f32[2,32,8192]{2,1,0:T(8,128)} %ur.1, f32[2,32,8192]{2,1,0:T(8,128)} %vr.1, f32[32,8192]{1,0:T(8,128)} %dr.1, f32[32,8192]{1,0:T(8,128)} %hr.1, f32[32,8192]{1,0:T(8,128)} %tr.1, f32[2,32,8192]{2,1,0:T(8,128)} %ur.1, f32[2,32,8192]{2,1,0:T(8,128)} %vr.1, f32[32,8192]{1,0:T(8,128)} %dr.1, ...), custom_call_target="tpu_custom_call" | custom-call | tf_op jit(solution)/shard_map/pallas_call | solution.py:160
  15.1 0.0 collective-permute-done.2.cb_ref
  15.1 0.0 copy-start.3
  15.1 0.0 collective-permute-done.1.ca_ref
  15.1 0.0 copy-start.4
  15.1 0.0 collective-permute-done.side_ref
  15.1 0.0 copy-start.2
  15.1 4.0 %collective-permute-start.3 = (f32[29,8192]{1,0:T(8,128)}, f32[29,8192]{1,0:T(8,128)S(1)}, u32[]{:S(2)}, u32[]{:S(2)}) collective-permute-start(f32[29,8192]{1,0:T(8,128)} %get-tuple-element.13), channel_id=1, source_target_pairs={{0,2},{2,4},{4,6},{6,8},{8,10},{10,12},{12,14},{14,16},{16,18},{18... | collective-permute-start | bytes 2850824 | tf_op jit(solution)/shard_map/ppermute | solution.py:177
  19.1 1.9 %collective-permute-start.4 = (f32[29,8192]{1,0:T(8,128)}, f32[29,8192]{1,0:T(8,128)S(1)}, u32[]{:S(2)}, u32[]{:S(2)}) collective-permute-start(f32[29,8192]{1,0:T(8,128)} %get-tuple-element.14), channel_id=1, source_target_pairs={{2,0},{4,2},{6,4},{8,6},{10,8},{12,10},{14,12},{16,14},{18,16},{20... | collective-permute-start | bytes 2850824 | tf_op jit(solution)/shard_map/ppermute | solution.py:178
  21.1 16.1 %collective-permute-done.3.am.al.ar = f32[29,8192]{1,0:T(8,128)S(1)} collective-permute-done((f32[29,8192]{1,0:T(8,128)}, f32[29,8192]{1,0:T(8,128)S(1)}, u32[]{:S(2)}, u32[]{:S(2)}) %collective-permute-start.3) | collective-permute-done | bytes 950304 | tf_op jit(solution)/shard_map/ppermute | solution.py:177
  37.2 0.0 copy-start
  37.2 11.0 %collective-permute-done.4.bm.bl.br = f32[29,8192]{1,0:T(8,128)S(1)} collective-permute-done((f32[29,8192]{1,0:T(8,128)}, f32[29,8192]{1,0:T(8,128)S(1)}, u32[]{:S(2)}, u32[]{:S(2)}) %collective-permute-start.4) | collective-permute-done | bytes 950304 | tf_op jit(solution)/shard_map/ppermute | solution.py:178
  48.2 0.0 copy-done.3
  48.2 0.0 copy-done.4
  48.2 0.0 copy-done.2
  48.2 0.0 copy-done
  48.2 0.0 copy-start.1
  48.2 1.0 %copy-done.1 = f32[29,8192]{1,0:T(8,128)} copy-done((f32[29,8192]{1,0:T(8,128)}, f32[29,8192]{1,0:T(8,128)S(1)}, u32[]{:S(2)}) %copy-start.1) | copy-done | bytes 950296
  49.2 22.0 %shard_map.86 = (f32[2,32,8192]{2,1,0:T(8,128)}, f32[2,32,8192]{2,1,0:T(8,128)}, f32[32,8192]{1,0:T(8,128)}, f32[32,8192]{1,0:T(8,128)}) custom-call(s32[2]{0:T(128)} %pad_add_fusion.pos_ref, f32[2,32,8192]{2,1,0:T(8,128)} %ur.1, f32[2,32,8192]{2,1,0:T(8,128)} %ur.1, f32[2,32,8192]{2,1,0:T(8,128)} %ur.1, f32[2,32,8192]{2,1,0:T(8,128)} %vr.1, ...), custom_call_target="tpu_custom_call" | custom-call | tf_op jit(solution)/shard_map/pallas_call | solution.py:271
Async XLA Ops:
  2.9 12.3 %collective-permute-start = (f32[32,128]{1,0:T(8,128)}, f32[32,128]{1,0:T(8,128)S(1)}, u32[]{:S(2)}, u32[]{:S(2)}) collective-permute-start(f32[32,128]{1,0:T(8,128)} %shard_map.84.after), channel_id=1, source_target_pairs={{0,1},{1,0},{2,3},{3,2},{4,5},{5,4},{6,7},{7,6},{8,9},{9,8},{10,11... | collective-permute-start | bytes 49160 | tf_op jit(solution)/shard_map/ppermute | solution.py:169
  4.8 10.3 %collective-permute-start.2 = (f32[8,128]{1,0:T(8,128)S(1)}, f32[8,128]{1,0:T(8,128)S(1)}, u32[]{:S(2)}, u32[]{:S(2)}) collective-permute-start(f32[8,128]{1,0:T(8,128)S(1)} %get-tuple-element.18), channel_id=1, source_target_pairs={{2,1},{3,0},{4,3},{5,2},{6,5},{7,4},{8,7},{9,6},{10,9},{11,8},{12,... | collective-permute-start | bytes 12296 | tf_op jit(solution)/shard_map/ppermute | solution.py:173
  7.8 7.3 %collective-permute-start.1 = (f32[8,128]{1,0:T(8,128)S(1)}, f32[8,128]{1,0:T(8,128)S(1)}, u32[]{:S(2)}, u32[]{:S(2)}) collective-permute-start(f32[8,128]{1,0:T(8,128)S(1)} %get-tuple-element.19), channel_id=1, source_target_pairs={{0,3},{1,2},{2,5},{3,4},{4,7},{5,6},{6,9},{7,8},{8,11},{9,10},{10,... | collective-permute-start | bytes 12296 | tf_op jit(solution)/shard_map/ppermute | solution.py:171
  15.1 33.1 %copy-start.3 = (f32[8,128]{1,0:T(8,128)}, f32[8,128]{1,0:T(8,128)S(1)}, u32[]{:S(2)}) copy-start(f32[8,128]{1,0:T(8,128)S(1)} %collective-permute-done.2.cb_ref) | copy-start | bytes 12292
  15.1 33.1 %copy-start.4 = (f32[8,128]{1,0:T(8,128)}, f32[8,128]{1,0:T(8,128)S(1)}, u32[]{:S(2)}) copy-start(f32[8,128]{1,0:T(8,128)S(1)} %collective-permute-done.1.ca_ref) | copy-start | bytes 12292
  15.1 33.1 %copy-start.2 = (f32[32,128]{1,0:T(8,128)}, f32[32,128]{1,0:T(8,128)S(1)}, u32[]{:S(2)}) copy-start(f32[32,128]{1,0:T(8,128)S(1)} %collective-permute-done.side_ref) | copy-start | bytes 49156
  15.1 22.0 %collective-permute-start.3 = (f32[29,8192]{1,0:T(8,128)}, f32[29,8192]{1,0:T(8,128)S(1)}, u32[]{:S(2)}, u32[]{:S(2)}) collective-permute-start(f32[29,8192]{1,0:T(8,128)} %get-tuple-element.13), channel_id=1, source_target_pairs={{0,2},{2,4},{4,6},{6,8},{8,10},{10,12},{12,14},{14,16},{16,18},{18... | collective-permute-start | bytes 2850824 | tf_op jit(solution)/shard_map/ppermute | solution.py:177
  19.1 29.1 %collective-permute-start.4 = (f32[29,8192]{1,0:T(8,128)}, f32[29,8192]{1,0:T(8,128)S(1)}, u32[]{:S(2)}, u32[]{:S(2)}) collective-permute-start(f32[29,8192]{1,0:T(8,128)} %get-tuple-element.14), channel_id=1, source_target_pairs={{2,0},{4,2},{6,4},{8,6},{10,8},{12,10},{14,12},{16,14},{18,16},{20... | collective-permute-start | bytes 2850824 | tf_op jit(solution)/shard_map/ppermute | solution.py:178
  37.2 11.0 %copy-start = (f32[29,8192]{1,0:T(8,128)}, f32[29,8192]{1,0:T(8,128)S(1)}, u32[]{:S(2)}) copy-start(f32[29,8192]{1,0:T(8,128)S(1)} %collective-permute-done.3.am.al.ar) | copy-start | bytes 2850820
  48.2 1.0 %copy-start.1 = (f32[29,8192]{1,0:T(8,128)}, f32[29,8192]{1,0:T(8,128)S(1)}, u32[]{:S(2)}) copy-start(f32[29,8192]{1,0:T(8,128)S(1)} %collective-permute-done.4.bm.bl.br) | copy-start | bytes 2850820

commit v12 on v11

--- a/solution.py
+++ b/solution.py
@@ -108,7 +108,7 @@
 
     pw = cols
 
-    def pack_kernel(tu, tv, td, th, tt, bu, bv, bd, bh, bt, after, top_o, bot_o):
+    def pack_kernel(tu, tv, td, th, tt, bu, bv, bd, bh, bt, top_o, bot_o):
         tops = split((tu, tv, td, th, tt))
         bots = split((bu, bv, bd, bh, bt))
         ridx = lax.broadcasted_iota(jnp.int32, (STRIP, pw), 0)
@@ -149,6 +149,14 @@
     r1 = pl.BlockSpec((rows, HC), lambda j: (0, last_col_block))
     smem = pl.BlockSpec(memory_space=pltpu.SMEM)
     ins = (displacement, velocity, damage, history, toughness)
+    top_s, bot_s = pl.pallas_call(
+        pack_kernel,
+        grid=(cols // pw,),
+        in_specs=[t2, t2, t1, t1, t1, b2, b2, b1, b1, b1],
+        out_specs=[pl.BlockSpec((SENT, pw), lambda j: (0, j)), pl.BlockSpec((SENT, pw), lambda j: (0, j))],
+        out_shape=[jax.ShapeDtypeStruct((SENT, cols), f32), jax.ShapeDtypeStruct((SENT, cols), f32)],
+        interpret=INTERPRET,
+    )(*ins, *ins)
     col_s = pl.pallas_call(
         col_kernel,
         grid=(1,),
@@ -157,25 +165,15 @@
         out_shape=jax.ShapeDtypeStruct((rows, HC), f32),
         interpret=INTERPRET,
     )(pos, *ins, *ins)
-    top_s, bot_s = pl.pallas_call(
-        pack_kernel,
-        grid=(cols // pw,),
-        in_specs=[t2, t2, t1, t1, t1, b2, b2, b1, b1, b1, pl.BlockSpec((8, HC), lambda j: (0, 0))],
-        out_specs=[pl.BlockSpec((SENT, pw), lambda j: (0, j)), pl.BlockSpec((SENT, pw), lambda j: (0, j))],
-        out_shape=[jax.ShapeDtypeStruct((SENT, cols), f32), jax.ShapeDtypeStruct((SENT, cols), f32)],
-        interpret=INTERPRET,
-    )(*ins, *ins, col_s)
-
+
+    above = lax.ppermute(bot_s, "gx", [(i, i + 1) for i in range(nx - 1)])
+    below = lax.ppermute(top_s, "gx", [(i + 1, i) for i in range(nx - 1)])
     side = lax.ppermute(col_s, "gy", [(0, 1), (1, 0)])
     both = ("gx", "gy")
     corner_above = lax.ppermute(col_s[rows - 8:], both,
                                 [(i * 2 + g, (i + 1) * 2 + 1 - g) for i in range(nx - 1) for g in range(2)])
     corner_below = lax.ppermute(col_s[:8], both,
                                 [((i + 1) * 2 + g, i * 2 + 1 - g) for i in range(nx - 1) for g in range(2)])
-    side, corner_above, corner_below, top_s, bot_s = lax.optimization_barrier(
-        (side, corner_above, corner_below, top_s, bot_s))
-    above = lax.ppermute(bot_s, "gx", [(i, i + 1) for i in range(nx - 1)])
-    below = lax.ppermute(top_s, "gx", [(i + 1, i) for i in range(nx - 1)])
 
     def kernel(pos_ref, um, ul, ur, vm, vl, vr, dm, dl, dr, hm, hl, hr, tm, tl, tr,
                am, al, ar, bm, bl, br, side_ref, ca_ref, cb_ref, uo, vo, ho, do):

time: 72.1 us -> 59 us (0.82)
  waiting for transfers between devices: 27.1 us -> 12.1 us
  local copies, waits for them, and re-layouts: 1.73 us -> 2.67 us
  starting transfers between devices: 13.9 us -> 14.7 us
    ppermute x1, waiting for transfers between devices: 16.1 us -> 0.01 us  [on_device(): above = lax.ppermute(bot_s, 'gx', [(i, i + 1) for i in range(nx - 1)])]
    ppermute x1, waiting for transfers between devices: 11 us -> 0.01 us  [on_device(): below = lax.ppermute(top_s, 'gx', [(i + 1, i) for i in range(nx - 1)])]
    ppermute x1, waiting for transfers between devices: 0.01 us -> 7.43 us  [on_device(): lax.ppermute(col_s[:8], both, [((i + 1) * 2 + g, i * 2 + 1 - g) for i in...]
    ppermute x1, waiting for transfers between devices: 0.01 us -> 4.69 us  [on_device(): lax.ppermute(col_s[rows - 8:], both, [(i * 2 + g, (i + 1) * 2 + 1 - g) fo...]
    ppermute x1, starting transfers between devices: 2.99 us -> 4.72 us  [on_device(): lax.ppermute(col_s[:8], both, [((i + 1) * 2 + g, i * 2 + 1 - g) for i in...]
    ppermute x1, starting transfers between devices: 3.99 us -> 5.2 us  [on_device(): above = lax.ppermute(bot_s, 'gx', [(i, i + 1) for i in range(nx - 1)])]
    ppermute x1, starting transfers between devices: 3.77 us -> 2.58 us  [on_device(): lax.ppermute(col_s[rows - 8:], both, [(i * 2 + g, (i + 1) * 2 + 1 - g) fo...]
    unnamed x10, local copies, waits for them, and re-layouts: 1.01 us -> 1.95 us
  transfers between devices with their start and end apart: 5 -> 5, of which waited for: 2 -> 2; matrix products, arithmetic and copies ran while one was open for 1% -> 2% of each run, Pallas kernels for 5% -> 3%
where the time goes in v12:
time: 59 us; the launch traced here: 58 us
  Pallas kernels  27.1 us (46%)
  starting transfers between devices  14.7 us (25%)
  waiting for transfers between devices  12.1 us (21%)
  local copies, waits for them, and re-layouts  2.67 us (5%)
  between operations  0.7 us (1%)
  other arithmetic  0.61 us (1%)
    pallas_call x1, Pallas kernels, on_device(): pl.pallas_call(kernel, grid=(nblocks,), in_specs=[smem, main2, left2, rig...  22 us
    ppermute x1, waiting for transfers between devices, on_device(): lax.ppermute(col_s[:8], both, [((i + 1) * 2 + g, i * 2 + 1 - g) for i in...  7.43 us
    ppermute x1, starting transfers between devices, on_device(): above = lax.ppermute(bot_s, 'gx', [(i, i + 1) for i in range(nx - 1)])  5.2 us
    ppermute x1, starting transfers between devices, on_device(): lax.ppermute(col_s[:8], both, [((i + 1) * 2 + g, i * 2 + 1 - g) for i in...  4.72 us
    ppermute x1, waiting for transfers between devices, on_device(): lax.ppermute(col_s[rows - 8:], both, [(i * 2 + g, (i + 1) * 2 + 1 - g) fo...  4.69 us
    pallas_call x1, Pallas kernels, on_device(): pl.pallas_call(pack_kernel, grid=(cols // pw,), in_specs=[t2, t2, t1, t1,...  3.51 us
    ppermute x1, starting transfers between devices, on_device(): lax.ppermute(col_s[rows - 8:], both, [(i * 2 + g, (i + 1) * 2 + 1 - g) fo...  2.58 us
    unnamed x10, local copies, waits for them, and re-layouts  1.95 us
  transfers between devices with their start and end apart: 5, of which 2 were waited for; matrix products, arithmetic and copies ran while one was open for 2% of the time, Pallas kernels for 3%

profile of v12, /device:TPU:89, one launch (start us, length us, event | category | flops | bytes accessed | tf_op | source)
XLA Modules:
  0.0 58.0 jit_solution(10341602358718346222)
XLA Ops:
  0.6 3.5 %shard_map.84 = (f32[29,8192]{1,0:T(8,128)}, f32[29,8192]{1,0:T(8,128)}) custom-call(f32[2,32,8192]{2,1,0:T(8,128)} %ur.1, f32[2,32,8192]{2,1,0:T(8,128)} %vr.1, f32[32,8192]{1,0:T(8,128)} %dr.1, f32[32,8192]{1,0:T(8,128)} %hr.1, f32[32,8192]{1,0:T(8,128)} %tr.1, f32[2,32,8192]{2,1,0:T(8,128)} %ur.1, f32[2,32,8192]{2,1,0:T(8,128)} %vr.1, f32[32,8192]{1,0:T(8,128)} %dr.1, ...), custom_call_target="tpu_custom_call" | custom-call | tf_op jit(solution)/shard_map/pallas_call | solution.py:152
  4.1 5.2 %collective-permute-start = (f32[29,8192]{1,0:T(8,128)}, f32[29,8192]{1,0:T(8,128)S(1)}, u32[]{:S(2)}, u32[]{:S(2)}) collective-permute-start(f32[29,8192]{1,0:T(8,128)} %get-tuple-element.6), channel_id=1, source_target_pairs={{0,2},{2,4},{4,6},{6,8},{8,10},{10,12},{12,14},{14,16},{16,18},{18... | collective-permute-start | bytes 2850824 | tf_op jit(solution)/shard_map/ppermute | solution.py:169
  9.4 1.9 %collective-permute-start.1 = (f32[29,8192]{1,0:T(8,128)}, f32[29,8192]{1,0:T(8,128)S(1)}, u32[]{:S(2)}, u32[]{:S(2)}) collective-permute-start(f32[29,8192]{1,0:T(8,128)} %get-tuple-element.7), channel_id=1, source_target_pairs={{2,0},{4,2},{6,4},{8,6},{10,8},{12,10},{14,12},{16,14},{18,16},{20... | collective-permute-start | bytes 2850824 | tf_op jit(solution)/shard_map/ppermute | solution.py:170
  11.3 0.6 %pad_add_fusion.pos_ref = s32[2]{0:T(128)} fusion(s32[1]{0:T(128)} %bitcast.1, s32[1]{0:T(128)} %bitcast), kind=kLoop, calls=%fused_computation | loop fusion | flops 2 | bytes 16 | tf_op jit(solution)/shard_map/stack | solution.py:94
  11.9 1.6 %shard_map.85 = f32[32,128]{1,0:T(8,128)} custom-call(s32[2]{0:T(128)} %pad_add_fusion.pos_ref, f32[2,32,8192]{2,1,0:T(8,128)} %ur.1, f32[2,32,8192]{2,1,0:T(8,128)} %vr.1, f32[32,8192]{1,0:T(8,128)} %dr.1, f32[32,8192]{1,0:T(8,128)} %hr.1, f32[32,8192]{1,0:T(8,128)} %tr.1, f32[2,32,8192]{2,1,0:T(8,128)} %ur.1, f32[2,32,8192]{2,1,0:T(8,128)} %vr.1, ...), custom_call_target="tpu_custom_call" | custom-call | tf_op jit(solution)/shard_map/pallas_call | solution.py:160
  13.5 0.3 collective-permute-start.2
  13.8 0.7 %fusion = (f32[8,128]{1,0:T(8,128)S(1)}, f32[8,128]{1,0:T(8,128)S(1)}) fusion(f32[32,128]{1,0:T(8,128)} %shard_map.85), kind=kLoop, calls=%fused_computation.1 | loop fusion | bytes 16384 | tf_op jit(solution)/shard_map/slice | solution.py:175
  14.5 4.7 %collective-permute-start.4 = (f32[8,128]{1,0:T(8,128)S(1)}, f32[8,128]{1,0:T(8,128)S(1)}, u32[]{:S(2)}, u32[]{:S(2)}) collective-permute-start(f32[8,128]{1,0:T(8,128)S(1)} %get-tuple-element.8), channel_id=1, source_target_pairs={{2,1},{3,0},{4,3},{5,2},{6,5},{7,4},{8,7},{9,6},{10,9},{11,8},{12,... | collective-permute-start | bytes 12296 | tf_op jit(solution)/shard_map/ppermute | solution.py:175
  19.3 2.6 %collective-permute-start.3 = (f32[8,128]{1,0:T(8,128)S(1)}, f32[8,128]{1,0:T(8,128)S(1)}, u32[]{:S(2)}, u32[]{:S(2)}) collective-permute-start(f32[8,128]{1,0:T(8,128)S(1)} %get-tuple-element.9), channel_id=1, source_target_pairs={{0,3},{1,2},{2,5},{3,4},{4,7},{5,6},{6,9},{7,8},{8,11},{9,10},{10,... | collective-permute-start | bytes 12296 | tf_op jit(solution)/shard_map/ppermute | solution.py:173
  21.9 7.4 %collective-permute-done.4.cb_ref = f32[8,128]{1,0:T(8,128)S(1)} collective-permute-done((f32[8,128]{1,0:T(8,128)S(1)}, f32[8,128]{1,0:T(8,128)S(1)}, u32[]{:S(2)}, u32[]{:S(2)}) %collective-permute-start.4) | collective-permute-done | bytes 4128 | tf_op jit(solution)/shard_map/ppermute | solution.py:175
  29.3 0.0 copy-start.3
  29.3 4.7 %collective-permute-done.3.ca_ref = f32[8,128]{1,0:T(8,128)S(1)} collective-permute-done((f32[8,128]{1,0:T(8,128)S(1)}, f32[8,128]{1,0:T(8,128)S(1)}, u32[]{:S(2)}, u32[]{:S(2)}) %collective-permute-start.3) | collective-permute-done | bytes 4128 | tf_op jit(solution)/shard_map/ppermute | solution.py:173
  34.0 0.0 copy-start.4
  34.0 0.0 collective-permute-done.2.side_ref
  34.0 0.0 copy-start.2
  34.0 0.0 collective-permute-done.am.al.ar
  34.0 0.0 copy-start
  34.0 0.0 collective-permute-done.1.bm.bl.br
  34.0 0.0 copy-done.3
  34.0 0.5 copy-done.4
  34.6 0.0 copy-done.2
  34.6 0.4 copy-done
  35.0 0.0 copy-start.1
  35.0 1.0 %copy-done.1 = f32[29,8192]{1,0:T(8,128)} copy-done((f32[29,8192]{1,0:T(8,128)}, f32[29,8192]{1,0:T(8,128)S(1)}, u32[]{:S(2)}) %copy-start.1) | copy-done | bytes 950296
  36.0 22.0 %shard_map.86 = (f32[2,32,8192]{2,1,0:T(8,128)}, f32[2,32,8192]{2,1,0:T(8,128)}, f32[32,8192]{1,0:T(8,128)}, f32[32,8192]{1,0:T(8,128)}) custom-call(s32[2]{0:T(128)} %pad_add_fusion.pos_ref, f32[2,32,8192]{2,1,0:T(8,128)} %ur.1, f32[2,32,8192]{2,1,0:T(8,128)} %ur.1, f32[2,32,8192]{2,1,0:T(8,128)} %ur.1, f32[2,32,8192]{2,1,0:T(8,128)} %vr.1, ...), custom_call_target="tpu_custom_call" | custom-call | tf_op jit(solution)/shard_map/pallas_call | solution.py:269
Async XLA Ops:
  4.1 29.9 %collective-permute-start = (f32[29,8192]{1,0:T(8,128)}, f32[29,8192]{1,0:T(8,128)S(1)}, u32[]{:S(2)}, u32[]{:S(2)}) collective-permute-start(f32[29,8192]{1,0:T(8,128)} %get-tuple-element.6), channel_id=1, source_target_pairs={{0,2},{2,4},{4,6},{6,8},{8,10},{10,12},{12,14},{14,16},{16,18},{18... | collective-permute-start | bytes 2850824 | tf_op jit(solution)/shard_map/ppermute | solution.py:169
  9.4 24.7 %collective-permute-start.1 = (f32[29,8192]{1,0:T(8,128)}, f32[29,8192]{1,0:T(8,128)S(1)}, u32[]{:S(2)}, u32[]{:S(2)}) collective-permute-start(f32[29,8192]{1,0:T(8,128)} %get-tuple-element.7), channel_id=1, source_target_pairs={{2,0},{4,2},{6,4},{8,6},{10,8},{12,10},{14,12},{16,14},{18,16},{20... | collective-permute-start | bytes 2850824 | tf_op jit(solution)/shard_map/ppermute | solution.py:170
  13.5 20.5 %collective-permute-start.2 = (f32[32,128]{1,0:T(8,128)}, f32[32,128]{1,0:T(8,128)S(1)}, u32[]{:S(2)}, u32[]{:S(2)}) collective-permute-start(f32[32,128]{1,0:T(8,128)} %shard_map.85), channel_id=1, source_target_pairs={{0,1},{1,0},{2,3},{3,2},{4,5},{5,4},{6,7},{7,6},{8,9},{9,8},{10,11... | collective-permute-start | bytes 49160 | tf_op jit(solution)/shard_map/ppermute | solution.py:171
  14.5 14.8 %collective-permute-start.4 = (f32[8,128]{1,0:T(8,128)S(1)}, f32[8,128]{1,0:T(8,128)S(1)}, u32[]{:S(2)}, u32[]{:S(2)}) collective-permute-start(f32[8,128]{1,0:T(8,128)S(1)} %get-tuple-element.8), channel_id=1, source_target_pairs={{2,1},{3,0},{4,3},{5,2},{6,5},{7,4},{8,7},{9,6},{10,9},{11,8},{12,... | collective-permute-start | bytes 12296 | tf_op jit(solution)/shard_map/ppermute | solution.py:175
  19.3 14.7 %collective-permute-start.3 = (f32[8,128]{1,0:T(8,128)S(1)}, f32[8,128]{1,0:T(8,128)S(1)}, u32[]{:S(2)}, u32[]{:S(2)}) collective-permute-start(f32[8,128]{1,0:T(8,128)S(1)} %get-tuple-element.9), channel_id=1, source_target_pairs={{0,3},{1,2},{2,5},{3,4},{4,7},{5,6},{6,9},{7,8},{8,11},{9,10},{10,... | collective-permute-start | bytes 12296 | tf_op jit(solution)/shard_map/ppermute | solution.py:173
  29.3 4.7 %copy-start.3 = (f32[8,128]{1,0:T(8,128)}, f32[8,128]{1,0:T(8,128)S(1)}, u32[]{:S(2)}) copy-start(f32[8,128]{1,0:T(8,128)S(1)} %collective-permute-done.4.cb_ref) | copy-start | bytes 12292
  34.0 0.6 %copy-start.4 = (f32[8,128]{1,0:T(8,128)}, f32[8,128]{1,0:T(8,128)S(1)}, u32[]{:S(2)}) copy-start(f32[8,128]{1,0:T(8,128)S(1)} %collective-permute-done.3.ca_ref) | copy-start | bytes 12292
  34.0 0.6 %copy-start.2 = (f32[32,128]{1,0:T(8,128)}, f32[32,128]{1,0:T(8,128)S(1)}, u32[]{:S(2)}) copy-start(f32[32,128]{1,0:T(8,128)S(1)} %collective-permute-done.2.side_ref) | copy-start | bytes 49156
  34.0 1.0 %copy-start = (f32[29,8192]{1,0:T(8,128)}, f32[29,8192]{1,0:T(8,128)S(1)}, u32[]{:S(2)}) copy-start(f32[29,8192]{1,0:T(8,128)S(1)} %collective-permute-done.am.al.ar) | copy-start | bytes 2850820
  35.0 1.0 %copy-start.1 = (f32[29,8192]{1,0:T(8,128)}, f32[29,8192]{1,0:T(8,128)S(1)}, u32[]{:S(2)}) copy-start(f32[29,8192]{1,0:T(8,128)S(1)} %collective-permute-done.1.bm.bl.br) | copy-start | bytes 2850820

commit v13 on v12

--- a/solution.py
+++ b/solution.py
@@ -1,3 +1,5 @@
+import functools
+
 import jax
 import jax.numpy as jnp
 from jax import lax
@@ -108,22 +110,17 @@
 
     pw = cols
 
-    def pack_kernel(tu, tv, td, th, tt, bu, bv, bd, bh, bt, top_o, bot_o):
-        tops = split((tu, tv, td, th, tt))
-        bots = split((bu, bv, bd, bh, bt))
+    def strip_kernel(first_row_of, u_ref, v_ref, d_ref, h_ref, t_ref, out_o):
+        tiles = split((u_ref, v_ref, d_ref, h_ref, t_ref))
         ridx = lax.broadcasted_iota(jnp.int32, (STRIP, pw), 0)
-        top = jnp.zeros((STRIP, pw), f32)
-        bot = jnp.zeros((STRIP, pw), f32)
+        acc = jnp.zeros((STRIP, pw), f32)
         pad = jnp.zeros((STRIP - 8, pw), f32)
         for k in range(nf):
             r, o = RADII[k], OFFSETS[k]
             inside = (ridx >= o) & (ridx < o + r)
-            x = roll(jnp.concatenate([tops[k], pad], axis=0), o, 0)
-            top = jnp.where(inside, x, top)
-            y = roll(jnp.concatenate([bots[k], pad], axis=0), o - (8 - r), 0)
-            bot = jnp.where(inside, y, bot)
-        top_o[...] = top[:SENT]
-        bot_o[...] = bot[:SENT]
+            x = roll(jnp.concatenate([tiles[k], pad], axis=0), o - first_row_of(r), 0)
+            acc = jnp.where(inside, x, acc)
+        out_o[...] = acc[:SENT]
 
 
     def col_kernel(pos_ref, lu, lv, ld, lh, lt, ru, rv, rd, rh, rt, col_o):
@@ -149,14 +146,18 @@
     r1 = pl.BlockSpec((rows, HC), lambda j: (0, last_col_block))
     smem = pl.BlockSpec(memory_space=pltpu.SMEM)
     ins = (displacement, velocity, damage, history, toughness)
-    top_s, bot_s = pl.pallas_call(
-        pack_kernel,
-        grid=(cols // pw,),
-        in_specs=[t2, t2, t1, t1, t1, b2, b2, b1, b1, b1],
-        out_specs=[pl.BlockSpec((SENT, pw), lambda j: (0, j)), pl.BlockSpec((SENT, pw), lambda j: (0, j))],
-        out_shape=[jax.ShapeDtypeStruct((SENT, cols), f32), jax.ShapeDtypeStruct((SENT, cols), f32)],
-        interpret=INTERPRET,
-    )(*ins, *ins)
+    def strip(first_row_of, s2, s1):
+        return pl.pallas_call(
+            functools.partial(strip_kernel, first_row_of),
+            grid=(cols // pw,),
+            in_specs=[s2, s2, s1, s1, s1],
+            out_specs=pl.BlockSpec((SENT, pw), lambda j: (0, j)),
+            out_shape=jax.ShapeDtypeStruct((SENT, cols), f32),
+            interpret=INTERPRET,
+        )(*ins)
+
+    bot_s = strip(lambda r: 8 - r, b2, b1)
+    top_s = strip(lambda r: 0, t2, t1)
     col_s = pl.pallas_call(
         col_kernel,
         grid=(1,),

time: 59 us -> 58.2 us (0.986)
  the two profiles are of different devices: /device:TPU:89 before, /device:TPU:128 now
where the time goes in v13:
time: 58.2 us; the launch traced here: 57.9 us
  Pallas kernels  28.8 us (49%)
  starting transfers between devices  18.3 us (31%)
  waiting for transfers between devices  6.75 us (12%)
  local copies, waits for them, and re-layouts  2.69 us (5%)
  between operations  0.7 us (1%)
  other arithmetic  0.61 us (1%)
    pallas_call x1, Pallas kernels, on_device(): pl.pallas_call(kernel, grid=(nblocks,), in_specs=[smem, main2, left2, rig...  22 us
    ppermute x1, starting transfers between devices, on_device(): below = lax.ppermute(top_s, 'gx', [(i + 1, i) for i in range(nx - 1)])  9.35 us
    ppermute x1, waiting for transfers between devices, on_device(): lax.ppermute(col_s[:8], both, [((i + 1) * 2 + g, i * 2 + 1 - g) for i in...  5.72 us
    pallas_call x2, Pallas kernels, strip(): pl.pallas_call(functools.partial(strip_kernel, first_row_of), grid=(cols...  5.22 us
    ppermute x1, starting transfers between devices, on_device(): lax.ppermute(col_s[rows - 8:], both, [(i * 2 + g, (i + 1) * 2 + 1 - g) fo...  3.64 us
    unnamed x10, local copies, waits for them, and re-layouts  1.97 us
    ppermute x1, starting transfers between devices, on_device(): lax.ppermute(col_s[:8], both, [((i + 1) * 2 + g, i * 2 + 1 - g) for i in...  1.91 us
    ppermute x1, starting transfers between devices, on_device(): above = lax.ppermute(bot_s, 'gx', [(i, i + 1) for i in range(nx - 1)])  1.91 us
  transfers between devices with their start and end apart: 5, of which 2 were waited for; matrix products, arithmetic and copies ran while one was open for 2% of the time, Pallas kernels for 7%

profile of v13, /device:TPU:128, one launch (start us, length us, event | category | flops | bytes accessed | tf_op | source)
XLA Modules:
  0.0 57.9 jit_solution(12842986368854540116)
XLA Ops:
  0.6 2.6 %shard_map.84 = f32[29,8192]{1,0:T(8,128)} custom-call(f32[2,32,8192]{2,1,0:T(8,128)} %ur.1, f32[2,32,8192]{2,1,0:T(8,128)} %vr.1, f32[32,8192]{1,0:T(8,128)} %dr.1, f32[32,8192]{1,0:T(8,128)} %hr.1, f32[32,8192]{1,0:T(8,128)} %tr.1), custom_call_target="tpu_custom_call" | custom-call | tf_op jit(solution)/shard_map/pallas_call | solution.py:150
  3.2 1.9 %collective-permute-start = (f32[29,8192]{1,0:T(8,128)}, f32[29,8192]{1,0:T(8,128)S(1)}, u32[]{:S(2)}, u32[]{:S(2)}) collective-permute-start(f32[29,8192]{1,0:T(8,128)} %shard_map.84), channel_id=1, source_target_pairs={{0,2},{2,4},{4,6},{6,8},{8,10},{10,12},{12,14},{14,16},{16,18},{18... | collective-permute-start | bytes 2850824 | tf_op jit(solution)/shard_map/ppermute | solution.py:170
  5.2 2.6 %shard_map.85 = f32[29,8192]{1,0:T(8,128)} custom-call(f32[2,32,8192]{2,1,0:T(8,128)} %ur.1, f32[2,32,8192]{2,1,0:T(8,128)} %vr.1, f32[32,8192]{1,0:T(8,128)} %dr.1, f32[32,8192]{1,0:T(8,128)} %hr.1, f32[32,8192]{1,0:T(8,128)} %tr.1), custom_call_target="tpu_custom_call" | custom-call | tf_op jit(solution)/shard_map/pallas_call | solution.py:150
  7.8 9.4 %collective-permute-start.1 = (f32[29,8192]{1,0:T(8,128)}, f32[29,8192]{1,0:T(8,128)S(1)}, u32[]{:S(2)}, u32[]{:S(2)}) collective-permute-start(f32[29,8192]{1,0:T(8,128)} %shard_map.85), channel_id=1, source_target_pairs={{2,0},{4,2},{6,4},{8,6},{10,8},{12,10},{14,12},{16,14},{18,16},{20... | collective-permute-start | bytes 2850824 | tf_op jit(solution)/shard_map/ppermute | solution.py:171
  17.1 0.6 %pad_add_fusion.pos_ref = s32[2]{0:T(128)} fusion(s32[1]{0:T(128)} %bitcast.1, s32[1]{0:T(128)} %bitcast), kind=kLoop, calls=%fused_computation | loop fusion | flops 2 | bytes 16 | tf_op jit(solution)/shard_map/stack | solution.py:96
  17.7 1.6 %shard_map.86 = f32[32,128]{1,0:T(8,128)} custom-call(s32[2]{0:T(128)} %pad_add_fusion.pos_ref, f32[2,32,8192]{2,1,0:T(8,128)} %ur.1, f32[2,32,8192]{2,1,0:T(8,128)} %vr.1, f32[32,8192]{1,0:T(8,128)} %dr.1, f32[32,8192]{1,0:T(8,128)} %hr.1, f32[32,8192]{1,0:T(8,128)} %tr.1, f32[2,32,8192]{2,1,0:T(8,128)} %ur.1, f32[2,32,8192]{2,1,0:T(8,128)} %vr.1, ...), custom_call_target="tpu_custom_call" | custom-call | tf_op jit(solution)/shard_map/pallas_call | solution.py:161
  19.4 1.5 %collective-permute-start.2 = (f32[32,128]{1,0:T(8,128)}, f32[32,128]{1,0:T(8,128)S(1)}, u32[]{:S(2)}, u32[]{:S(2)}) collective-permute-start(f32[32,128]{1,0:T(8,128)} %shard_map.86), channel_id=1, source_target_pairs={{0,1},{1,0},{2,3},{3,2},{4,5},{5,4},{6,7},{7,6},{8,9},{9,8},{10,11... | collective-permute-start | bytes 49160 | tf_op jit(solution)/shard_map/ppermute | solution.py:172
  20.8 0.7 %fusion = (f32[8,128]{1,0:T(8,128)S(1)}, f32[8,128]{1,0:T(8,128)S(1)}) fusion(f32[32,128]{1,0:T(8,128)} %shard_map.86), kind=kLoop, calls=%fused_computation.1 | loop fusion | bytes 16384 | tf_op jit(solution)/shard_map/slice | solution.py:176
  21.6 1.9 %collective-permute-start.4 = (f32[8,128]{1,0:T(8,128)S(1)}, f32[8,128]{1,0:T(8,128)S(1)}, u32[]{:S(2)}, u32[]{:S(2)}) collective-permute-start(f32[8,128]{1,0:T(8,128)S(1)} %get-tuple-element.4), channel_id=1, source_target_pairs={{2,1},{3,0},{4,3},{5,2},{6,5},{7,4},{8,7},{9,6},{10,9},{11,8},{12,... | collective-permute-start | bytes 12296 | tf_op jit(solution)/shard_map/ppermute | solution.py:176
  23.5 3.6 %collective-permute-start.3 = (f32[8,128]{1,0:T(8,128)S(1)}, f32[8,128]{1,0:T(8,128)S(1)}, u32[]{:S(2)}, u32[]{:S(2)}) collective-permute-start(f32[8,128]{1,0:T(8,128)S(1)} %get-tuple-element.5), channel_id=1, source_target_pairs={{0,3},{1,2},{2,5},{3,4},{4,7},{5,6},{6,9},{7,8},{8,11},{9,10},{10,... | collective-permute-start | bytes 12296 | tf_op jit(solution)/shard_map/ppermute | solution.py:174
  27.1 5.7 %collective-permute-done.4.cb_ref = f32[8,128]{1,0:T(8,128)S(1)} collective-permute-done((f32[8,128]{1,0:T(8,128)S(1)}, f32[8,128]{1,0:T(8,128)S(1)}, u32[]{:S(2)}, u32[]{:S(2)}) %collective-permute-start.4) | collective-permute-done | bytes 4128 | tf_op jit(solution)/shard_map/ppermute | solution.py:176
  32.9 0.0 copy-start.3
  32.9 1.0 %collective-permute-done.3.ca_ref = f32[8,128]{1,0:T(8,128)S(1)} collective-permute-done((f32[8,128]{1,0:T(8,128)S(1)}, f32[8,128]{1,0:T(8,128)S(1)}, u32[]{:S(2)}, u32[]{:S(2)}) %collective-permute-start.3) | collective-permute-done | bytes 4128 | tf_op jit(solution)/shard_map/ppermute | solution.py:174
  33.9 0.0 copy-start.4
  33.9 0.0 collective-permute-done.2.side_ref
  33.9 0.0 copy-start.2
  33.9 0.0 collective-permute-done.am.al.ar
  33.9 0.0 copy-start
  33.9 0.0 collective-permute-done.1.bm.bl.br
  33.9 0.0 copy-done.3
  33.9 0.5 copy-done.4
  34.5 0.0 copy-done.2
  34.5 0.4 copy-done
  34.9 0.0 copy-start.1
  34.9 1.0 %copy-done.1 = f32[29,8192]{1,0:T(8,128)} copy-done((f32[29,8192]{1,0:T(8,128)}, f32[29,8192]{1,0:T(8,128)S(1)}, u32[]{:S(2)}) %copy-start.1) | copy-done | bytes 950296
  35.9 22.0 %shard_map.87 = (f32[2,32,8192]{2,1,0:T(8,128)}, f32[2,32,8192]{2,1,0:T(8,128)}, f32[32,8192]{1,0:T(8,128)}, f32[32,8192]{1,0:T(8,128)}) custom-call(s32[2]{0:T(128)} %pad_add_fusion.pos_ref, f32[2,32,8192]{2,1,0:T(8,128)} %ur.1, f32[2,32,8192]{2,1,0:T(8,128)} %ur.1, f32[2,32,8192]{2,1,0:T(8,128)} %ur.1, f32[2,32,8192]{2,1,0:T(8,128)} %vr.1, ...), custom_call_target="tpu_custom_call" | custom-call | tf_op jit(solution)/shard_map/pallas_call | solution.py:270
Async XLA Ops:
  3.2 30.6 %collective-permute-start = (f32[29,8192]{1,0:T(8,128)}, f32[29,8192]{1,0:T(8,128)S(1)}, u32[]{:S(2)}, u32[]{:S(2)}) collective-permute-start(f32[29,8192]{1,0:T(8,128)} %shard_map.84), channel_id=1, source_target_pairs={{0,2},{2,4},{4,6},{6,8},{8,10},{10,12},{12,14},{14,16},{16,18},{18... | collective-permute-start | bytes 2850824 | tf_op jit(solution)/shard_map/ppermute | solution.py:170
  7.8 26.1 %collective-permute-start.1 = (f32[29,8192]{1,0:T(8,128)}, f32[29,8192]{1,0:T(8,128)S(1)}, u32[]{:S(2)}, u32[]{:S(2)}) collective-permute-start(f32[29,8192]{1,0:T(8,128)} %shard_map.85), channel_id=1, source_target_pairs={{2,0},{4,2},{6,4},{8,6},{10,8},{12,10},{14,12},{16,14},{18,16},{20... | collective-permute-start | bytes 2850824 | tf_op jit(solution)/shard_map/ppermute | solution.py:171
  19.4 14.5 %collective-permute-start.2 = (f32[32,128]{1,0:T(8,128)}, f32[32,128]{1,0:T(8,128)S(1)}, u32[]{:S(2)}, u32[]{:S(2)}) collective-permute-start(f32[32,128]{1,0:T(8,128)} %shard_map.86), channel_id=1, source_target_pairs={{0,1},{1,0},{2,3},{3,2},{4,5},{5,4},{6,7},{7,6},{8,9},{9,8},{10,11... | collective-permute-start | bytes 49160 | tf_op jit(solution)/shard_map/ppermute | solution.py:172
  21.6 11.3 %collective-permute-start.4 = (f32[8,128]{1,0:T(8,128)S(1)}, f32[8,128]{1,0:T(8,128)S(1)}, u32[]{:S(2)}, u32[]{:S(2)}) collective-permute-start(f32[8,128]{1,0:T(8,128)S(1)} %get-tuple-element.4), channel_id=1, source_target_pairs={{2,1},{3,0},{4,3},{5,2},{6,5},{7,4},{8,7},{9,6},{10,9},{11,8},{12,... | collective-permute-start | bytes 12296 | tf_op jit(solution)/shard_map/ppermute | solution.py:176
  23.5 10.4 %collective-permute-start.3 = (f32[8,128]{1,0:T(8,128)S(1)}, f32[8,128]{1,0:T(8,128)S(1)}, u32[]{:S(2)}, u32[]{:S(2)}) collective-permute-start(f32[8,128]{1,0:T(8,128)S(1)} %get-tuple-element.5), channel_id=1, source_target_pairs={{0,3},{1,2},{2,5},{3,4},{4,7},{5,6},{6,9},{7,8},{8,11},{9,10},{10,... | collective-permute-start | bytes 12296 | tf_op jit(solution)/shard_map/ppermute | solution.py:174
  32.9 1.1 %copy-start.3 = (f32[8,128]{1,0:T(8,128)}, f32[8,128]{1,0:T(8,128)S(1)}, u32[]{:S(2)}) copy-start(f32[8,128]{1,0:T(8,128)S(1)} %collective-permute-done.4.cb_ref) | copy-start | bytes 12292
  33.9 0.6 %copy-start.4 = (f32[8,128]{1,0:T(8,128)}, f32[8,128]{1,0:T(8,128)S(1)}, u32[]{:S(2)}) copy-start(f32[8,128]{1,0:T(8,128)S(1)} %collective-permute-done.3.ca_ref) | copy-start | bytes 12292
  33.9 0.6 %copy-start.2 = (f32[32,128]{1,0:T(8,128)}, f32[32,128]{1,0:T(8,128)S(1)}, u32[]{:S(2)}) copy-start(f32[32,128]{1,0:T(8,128)S(1)} %collective-permute-done.2.side_ref) | copy-start | bytes 49156
  33.9 1.0 %copy-start = (f32[29,8192]{1,0:T(8,128)}, f32[29,8192]{1,0:T(8,128)S(1)}, u32[]{:S(2)}) copy-start(f32[29,8192]{1,0:T(8,128)S(1)} %collective-permute-done.am.al.ar) | copy-start | bytes 2850820
  34.9 1.0 %copy-start.1 = (f32[29,8192]{1,0:T(8,128)}, f32[29,8192]{1,0:T(8,128)S(1)}, u32[]{:S(2)}) copy-start(f32[29,8192]{1,0:T(8,128)S(1)} %collective-permute-done.1.bm.bl.br) | copy-start | bytes 2850820

commit v14 on v13

--- a/solution.py
+++ b/solution.py
@@ -108,7 +108,7 @@
         du, dv, dd, dh, dt = refs
         return [du[0], du[1], dv[0], dv[1], dd[...], dh[...], dt[...]]
 
-    pw = cols
+    pw = cols // 2
 
     def strip_kernel(first_row_of, u_ref, v_ref, d_ref, h_ref, t_ref, out_o):
         tiles = split((u_ref, v_ref, d_ref, h_ref, t_ref))

time: 58.2 us -> 57.9 us (level)
  the two profiles are of different devices: /device:TPU:128 before, /device:TPU:89 now
where the time goes in v14:
time: 57.9 us; the launch traced here: 56.8 us
  Pallas kernels  28.3 us (49%)
  starting transfers between devices  14.7 us (25%)
  waiting for transfers between devices  9.77 us (17%)
  local copies, waits for them, and re-layouts  2.69 us (5%)
  between operations  0.69 us (1%)
  other arithmetic  0.61 us (1%)
    pallas_call x1, Pallas kernels, on_device(): pl.pallas_call(kernel, grid=(nblocks,), in_specs=[smem, main2, left2, rig...  22 us
    ppermute x1, waiting for transfers between devices, on_device(): lax.ppermute(col_s[rows - 8:], both, [(i * 2 + g, (i + 1) * 2 + 1 - g) fo...  7 us
    ppermute x1, starting transfers between devices, on_device(): above = lax.ppermute(bot_s, 'gx', [(i, i + 1) for i in range(nx - 1)])  5.2 us
    pallas_call x2, Pallas kernels, strip(): pl.pallas_call(functools.partial(strip_kernel, first_row_of), grid=(cols...  4.73 us
    ppermute x1, starting transfers between devices, on_device(): lax.ppermute(col_s[:8], both, [((i + 1) * 2 + g, i * 2 + 1 - g) for i in...  4.72 us
    ppermute x1, waiting for transfers between devices, on_device(): lax.ppermute(col_s[:8], both, [((i + 1) * 2 + g, i * 2 + 1 - g) for i in...  2.74 us
    ppermute x1, starting transfers between devices, on_device(): lax.ppermute(col_s[rows - 8:], both, [(i * 2 + g, (i + 1) * 2 + 1 - g) fo...  2.58 us
    unnamed x10, local copies, waits for them, and re-layouts  1.97 us
  transfers between devices with their start and end apart: 5, of which 2 were waited for; matrix products, arithmetic and copies ran while one was open for 2% of the time, Pallas kernels for 7%

profile of v14, /device:TPU:89, one launch (start us, length us, event | category | flops | bytes accessed | tf_op | source)
XLA Modules:
  0.0 56.8 jit_solution(17586900489969243140)
XLA Ops:
  0.6 2.4 %shard_map.84 = f32[29,8192]{1,0:T(8,128)} custom-call(f32[2,32,8192]{2,1,0:T(8,128)} %ur.1, f32[2,32,8192]{2,1,0:T(8,128)} %vr.1, f32[32,8192]{1,0:T(8,128)} %dr.1, f32[32,8192]{1,0:T(8,128)} %hr.1, f32[32,8192]{1,0:T(8,128)} %tr.1), custom_call_target="tpu_custom_call" | custom-call | tf_op jit(solution)/shard_map/pallas_call | solution.py:150
  3.0 5.2 %collective-permute-start = (f32[29,8192]{1,0:T(8,128)}, f32[29,8192]{1,0:T(8,128)S(1)}, u32[]{:S(2)}, u32[]{:S(2)}) collective-permute-start(f32[29,8192]{1,0:T(8,128)} %shard_map.84), channel_id=1, source_target_pairs={{0,2},{2,4},{4,6},{6,8},{8,10},{10,12},{12,14},{14,16},{16,18},{18... | collective-permute-start | bytes 2850824 | tf_op jit(solution)/shard_map/ppermute | solution.py:170
  8.2 2.4 %shard_map.85 = f32[29,8192]{1,0:T(8,128)} custom-call(f32[2,32,8192]{2,1,0:T(8,128)} %ur.1, f32[2,32,8192]{2,1,0:T(8,128)} %vr.1, f32[32,8192]{1,0:T(8,128)} %dr.1, f32[32,8192]{1,0:T(8,128)} %hr.1, f32[32,8192]{1,0:T(8,128)} %tr.1), custom_call_target="tpu_custom_call" | custom-call | tf_op jit(solution)/shard_map/pallas_call | solution.py:150
  10.6 1.9 %collective-permute-start.1 = (f32[29,8192]{1,0:T(8,128)}, f32[29,8192]{1,0:T(8,128)S(1)}, u32[]{:S(2)}, u32[]{:S(2)}) collective-permute-start(f32[29,8192]{1,0:T(8,128)} %shard_map.85), channel_id=1, source_target_pairs={{2,0},{4,2},{6,4},{8,6},{10,8},{12,10},{14,12},{16,14},{18,16},{20... | collective-permute-start | bytes 2850824 | tf_op jit(solution)/shard_map/ppermute | solution.py:171
  12.5 0.6 %pad_add_fusion.pos_ref = s32[2]{0:T(128)} fusion(s32[1]{0:T(128)} %bitcast.1, s32[1]{0:T(128)} %bitcast), kind=kLoop, calls=%fused_computation | loop fusion | flops 2 | bytes 16 | tf_op jit(solution)/shard_map/stack | solution.py:96
  13.1 1.6 %shard_map.86 = f32[32,128]{1,0:T(8,128)} custom-call(s32[2]{0:T(128)} %pad_add_fusion.pos_ref, f32[2,32,8192]{2,1,0:T(8,128)} %ur.1, f32[2,32,8192]{2,1,0:T(8,128)} %vr.1, f32[32,8192]{1,0:T(8,128)} %dr.1, f32[32,8192]{1,0:T(8,128)} %hr.1, f32[32,8192]{1,0:T(8,128)} %tr.1, f32[2,32,8192]{2,1,0:T(8,128)} %ur.1, f32[2,32,8192]{2,1,0:T(8,128)} %vr.1, ...), custom_call_target="tpu_custom_call" | custom-call | tf_op jit(solution)/shard_map/pallas_call | solution.py:161
  14.7 0.3 collective-permute-start.2
  15.0 0.7 %fusion = (f32[8,128]{1,0:T(8,128)S(1)}, f32[8,128]{1,0:T(8,128)S(1)}) fusion(f32[32,128]{1,0:T(8,128)} %shard_map.86), kind=kLoop, calls=%fused_computation.1 | loop fusion | bytes 16384 | tf_op jit(solution)/shard_map/slice | solution.py:176
  15.8 4.7 %collective-permute-start.4 = (f32[8,128]{1,0:T(8,128)S(1)}, f32[8,128]{1,0:T(8,128)S(1)}, u32[]{:S(2)}, u32[]{:S(2)}) collective-permute-start(f32[8,128]{1,0:T(8,128)S(1)} %get-tuple-element.4), channel_id=1, source_target_pairs={{2,1},{3,0},{4,3},{5,2},{6,5},{7,4},{8,7},{9,6},{10,9},{11,8},{12,... | collective-permute-start | bytes 12296 | tf_op jit(solution)/shard_map/ppermute | solution.py:176
  20.5 2.6 %collective-permute-start.3 = (f32[8,128]{1,0:T(8,128)S(1)}, f32[8,128]{1,0:T(8,128)S(1)}, u32[]{:S(2)}, u32[]{:S(2)}) collective-permute-start(f32[8,128]{1,0:T(8,128)S(1)} %get-tuple-element.5), channel_id=1, source_target_pairs={{0,3},{1,2},{2,5},{3,4},{4,7},{5,6},{6,9},{7,8},{8,11},{9,10},{10,... | collective-permute-start | bytes 12296 | tf_op jit(solution)/shard_map/ppermute | solution.py:174
  23.1 2.7 %collective-permute-done.4.cb_ref = f32[8,128]{1,0:T(8,128)S(1)} collective-permute-done((f32[8,128]{1,0:T(8,128)S(1)}, f32[8,128]{1,0:T(8,128)S(1)}, u32[]{:S(2)}, u32[]{:S(2)}) %collective-permute-start.4) | collective-permute-done | bytes 4128 | tf_op jit(solution)/shard_map/ppermute | solution.py:176
  25.8 0.0 copy-start.3
  25.8 7.0 %collective-permute-done.3.ca_ref = f32[8,128]{1,0:T(8,128)S(1)} collective-permute-done((f32[8,128]{1,0:T(8,128)S(1)}, f32[8,128]{1,0:T(8,128)S(1)}, u32[]{:S(2)}, u32[]{:S(2)}) %collective-permute-start.3) | collective-permute-done | bytes 4128 | tf_op jit(solution)/shard_map/ppermute | solution.py:174
  32.8 0.0 copy-start.4
  32.8 0.0 collective-permute-done.2.side_ref
  32.8 0.0 copy-start.2
  32.8 0.0 collective-permute-done.am.al.ar
  32.8 0.0 copy-start
  32.8 0.0 collective-permute-done.1.bm.bl.br
  32.9 0.0 copy-done.3
  32.9 0.5 copy-done.4
  33.4 0.0 copy-done.2
  33.4 0.4 copy-done
  33.8 0.0 copy-start.1
  33.8 1.0 %copy-done.1 = f32[29,8192]{1,0:T(8,128)} copy-done((f32[29,8192]{1,0:T(8,128)}, f32[29,8192]{1,0:T(8,128)S(1)}, u32[]{:S(2)}) %copy-start.1) | copy-done | bytes 950296
  34.8 22.0 %shard_map.87 = (f32[2,32,8192]{2,1,0:T(8,128)}, f32[2,32,8192]{2,1,0:T(8,128)}, f32[32,8192]{1,0:T(8,128)}, f32[32,8192]{1,0:T(8,128)}) custom-call(s32[2]{0:T(128)} %pad_add_fusion.pos_ref, f32[2,32,8192]{2,1,0:T(8,128)} %ur.1, f32[2,32,8192]{2,1,0:T(8,128)} %ur.1, f32[2,32,8192]{2,1,0:T(8,128)} %ur.1, f32[2,32,8192]{2,1,0:T(8,128)} %vr.1, ...), custom_call_target="tpu_custom_call" | custom-call | tf_op jit(solution)/shard_map/pallas_call | solution.py:270
Async XLA Ops:
  3.0 29.8 %collective-permute-start = (f32[29,8192]{1,0:T(8,128)}, f32[29,8192]{1,0:T(8,128)S(1)}, u32[]{:S(2)}, u32[]{:S(2)}) collective-permute-start(f32[29,8192]{1,0:T(8,128)} %shard_map.84), channel_id=1, source_target_pairs={{0,2},{2,4},{4,6},{6,8},{8,10},{10,12},{12,14},{14,16},{16,18},{18... | collective-permute-start | bytes 2850824 | tf_op jit(solution)/shard_map/ppermute | solution.py:170
  10.6 22.3 %collective-permute-start.1 = (f32[29,8192]{1,0:T(8,128)}, f32[29,8192]{1,0:T(8,128)S(1)}, u32[]{:S(2)}, u32[]{:S(2)}) collective-permute-start(f32[29,8192]{1,0:T(8,128)} %shard_map.85), channel_id=1, source_target_pairs={{2,0},{4,2},{6,4},{8,6},{10,8},{12,10},{14,12},{16,14},{18,16},{20... | collective-permute-start | bytes 2850824 | tf_op jit(solution)/shard_map/ppermute | solution.py:171
  14.7 18.1 %collective-permute-start.2 = (f32[32,128]{1,0:T(8,128)}, f32[32,128]{1,0:T(8,128)S(1)}, u32[]{:S(2)}, u32[]{:S(2)}) collective-permute-start(f32[32,128]{1,0:T(8,128)} %shard_map.86), channel_id=1, source_target_pairs={{0,1},{1,0},{2,3},{3,2},{4,5},{5,4},{6,7},{7,6},{8,9},{9,8},{10,11... | collective-permute-start | bytes 49160 | tf_op jit(solution)/shard_map/ppermute | solution.py:172
  15.8 10.1 %collective-permute-start.4 = (f32[8,128]{1,0:T(8,128)S(1)}, f32[8,128]{1,0:T(8,128)S(1)}, u32[]{:S(2)}, u32[]{:S(2)}) collective-permute-start(f32[8,128]{1,0:T(8,128)S(1)} %get-tuple-element.4), channel_id=1, source_target_pairs={{2,1},{3,0},{4,3},{5,2},{6,5},{7,4},{8,7},{9,6},{10,9},{11,8},{12,... | collective-permute-start | bytes 12296 | tf_op jit(solution)/shard_map/ppermute | solution.py:176
  20.5 12.3 %collective-permute-start.3 = (f32[8,128]{1,0:T(8,128)S(1)}, f32[8,128]{1,0:T(8,128)S(1)}, u32[]{:S(2)}, u32[]{:S(2)}) collective-permute-start(f32[8,128]{1,0:T(8,128)S(1)} %get-tuple-element.5), channel_id=1, source_target_pairs={{0,3},{1,2},{2,5},{3,4},{4,7},{5,6},{6,9},{7,8},{8,11},{9,10},{10,... | collective-permute-start | bytes 12296 | tf_op jit(solution)/shard_map/ppermute | solution.py:174
  25.8 7.1 %copy-start.3 = (f32[8,128]{1,0:T(8,128)}, f32[8,128]{1,0:T(8,128)S(1)}, u32[]{:S(2)}) copy-start(f32[8,128]{1,0:T(8,128)S(1)} %collective-permute-done.4.cb_ref) | copy-start | bytes 12292
  32.8 0.6 %copy-start.4 = (f32[8,128]{1,0:T(8,128)}, f32[8,128]{1,0:T(8,128)S(1)}, u32[]{:S(2)}) copy-start(f32[8,128]{1,0:T(8,128)S(1)} %collective-permute-done.3.ca_ref) | copy-start | bytes 12292
  32.8 0.6 %copy-start.2 = (f32[32,128]{1,0:T(8,128)}, f32[32,128]{1,0:T(8,128)S(1)}, u32[]{:S(2)}) copy-start(f32[32,128]{1,0:T(8,128)S(1)} %collective-permute-done.2.side_ref) | copy-start | bytes 49156
  32.8 1.0 %copy-start = (f32[29,8192]{1,0:T(8,128)}, f32[29,8192]{1,0:T(8,128)S(1)}, u32[]{:S(2)}) copy-start(f32[29,8192]{1,0:T(8,128)S(1)} %collective-permute-done.am.al.ar) | copy-start | bytes 2850820
  33.8 1.0 %copy-start.1 = (f32[29,8192]{1,0:T(8,128)}, f32[29,8192]{1,0:T(8,128)S(1)}, u32[]{:S(2)}) copy-start(f32[29,8192]{1,0:T(8,128)S(1)} %collective-permute-done.1.bm.bl.br) | copy-start | bytes 2850820

commit v15 on v14

--- a/solution.py
+++ b/solution.py
@@ -108,7 +108,7 @@
         du, dv, dd, dh, dt = refs
         return [du[0], du[1], dv[0], dv[1], dd[...], dh[...], dt[...]]
 
-    pw = cols // 2
+    pw = cols // 4
 
     def strip_kernel(first_row_of, u_ref, v_ref, d_ref, h_ref, t_ref, out_o):
         tiles = split((u_ref, v_ref, d_ref, h_ref, t_ref))

time: 57.9 us -> 60.3 us (1.041)
  the two profiles are of different devices: /device:TPU:89 before, /device:TPU:128 now
where the time goes in v15:
time: 60.3 us; the launch traced here: 59.8 us
  Pallas kernels  30.8 us (51%)
  starting transfers between devices  18.3 us (30%)
  waiting for transfers between devices  6.75 us (11%)
  local copies, waits for them, and re-layouts  2.69 us (4%)
  between operations  0.7 us (1%)
  other arithmetic  0.61 us (1%)
    pallas_call x1, Pallas kernels, on_device(): pl.pallas_call(kernel, grid=(nblocks,), in_specs=[smem, main2, left2, rig...  22 us
    ppermute x1, starting transfers between devices, on_device(): below = lax.ppermute(top_s, 'gx', [(i + 1, i) for i in range(nx - 1)])  9.35 us
    pallas_call x2, Pallas kernels, strip(): pl.pallas_call(functools.partial(strip_kernel, first_row_of), grid=(cols...  7.17 us
    ppermute x1, waiting for transfers between devices, on_device(): lax.ppermute(col_s[:8], both, [((i + 1) * 2 + g, i * 2 + 1 - g) for i in...  4.74 us
    ppermute x1, starting transfers between devices, on_device(): lax.ppermute(col_s[rows - 8:], both, [(i * 2 + g, (i + 1) * 2 + 1 - g) fo...  3.64 us
    ppermute x1, waiting for transfers between devices, on_device(): lax.ppermute(col_s[rows - 8:], both, [(i * 2 + g, (i + 1) * 2 + 1 - g) fo...  2 us
    unnamed x10, local copies, waits for them, and re-layouts  1.97 us
    ppermute x1, starting transfers between devices, on_device(): lax.ppermute(col_s[:8], both, [((i + 1) * 2 + g, i * 2 + 1 - g) for i in...  1.91 us
  transfers between devices with their start and end apart: 5, of which 2 were waited for; matrix products, arithmetic and copies ran while one was open for 2% of the time, Pallas kernels for 9%

profile of v15, /device:TPU:128, one launch (start us, length us, event | category | flops | bytes accessed | tf_op | source)
XLA Modules:
  0.0 59.8 jit_solution(10418147855023493907)
XLA Ops:
  0.6 3.6 %shard_map.84 = f32[29,8192]{1,0:T(8,128)} custom-call(f32[2,32,8192]{2,1,0:T(8,128)} %ur.1, f32[2,32,8192]{2,1,0:T(8,128)} %vr.1, f32[32,8192]{1,0:T(8,128)} %dr.1, f32[32,8192]{1,0:T(8,128)} %hr.1, f32[32,8192]{1,0:T(8,128)} %tr.1), custom_call_target="tpu_custom_call" | custom-call | tf_op jit(solution)/shard_map/pallas_call | solution.py:150
  4.2 1.9 %collective-permute-start = (f32[29,8192]{1,0:T(8,128)}, f32[29,8192]{1,0:T(8,128)S(1)}, u32[]{:S(2)}, u32[]{:S(2)}) collective-permute-start(f32[29,8192]{1,0:T(8,128)} %shard_map.84), channel_id=1, source_target_pairs={{0,2},{2,4},{4,6},{6,8},{8,10},{10,12},{12,14},{14,16},{16,18},{18... | collective-permute-start | bytes 2850824 | tf_op jit(solution)/shard_map/ppermute | solution.py:170
  6.1 3.6 %shard_map.85 = f32[29,8192]{1,0:T(8,128)} custom-call(f32[2,32,8192]{2,1,0:T(8,128)} %ur.1, f32[2,32,8192]{2,1,0:T(8,128)} %vr.1, f32[32,8192]{1,0:T(8,128)} %dr.1, f32[32,8192]{1,0:T(8,128)} %hr.1, f32[32,8192]{1,0:T(8,128)} %tr.1), custom_call_target="tpu_custom_call" | custom-call | tf_op jit(solution)/shard_map/pallas_call | solution.py:150
  9.7 9.4 %collective-permute-start.1 = (f32[29,8192]{1,0:T(8,128)}, f32[29,8192]{1,0:T(8,128)S(1)}, u32[]{:S(2)}, u32[]{:S(2)}) collective-permute-start(f32[29,8192]{1,0:T(8,128)} %shard_map.85), channel_id=1, source_target_pairs={{2,0},{4,2},{6,4},{8,6},{10,8},{12,10},{14,12},{16,14},{18,16},{20... | collective-permute-start | bytes 2850824 | tf_op jit(solution)/shard_map/ppermute | solution.py:171
  19.1 0.6 %pad_add_fusion.pos_ref = s32[2]{0:T(128)} fusion(s32[1]{0:T(128)} %bitcast.1, s32[1]{0:T(128)} %bitcast), kind=kLoop, calls=%fused_computation | loop fusion | flops 2 | bytes 16 | tf_op jit(solution)/shard_map/stack | solution.py:96
  19.7 1.6 %shard_map.86 = f32[32,128]{1,0:T(8,128)} custom-call(s32[2]{0:T(128)} %pad_add_fusion.pos_ref, f32[2,32,8192]{2,1,0:T(8,128)} %ur.1, f32[2,32,8192]{2,1,0:T(8,128)} %vr.1, f32[32,8192]{1,0:T(8,128)} %dr.1, f32[32,8192]{1,0:T(8,128)} %hr.1, f32[32,8192]{1,0:T(8,128)} %tr.1, f32[2,32,8192]{2,1,0:T(8,128)} %ur.1, f32[2,32,8192]{2,1,0:T(8,128)} %vr.1, ...), custom_call_target="tpu_custom_call" | custom-call | tf_op jit(solution)/shard_map/pallas_call | solution.py:161
  21.3 1.5 %collective-permute-start.2 = (f32[32,128]{1,0:T(8,128)}, f32[32,128]{1,0:T(8,128)S(1)}, u32[]{:S(2)}, u32[]{:S(2)}) collective-permute-start(f32[32,128]{1,0:T(8,128)} %shard_map.86), channel_id=1, source_target_pairs={{0,1},{1,0},{2,3},{3,2},{4,5},{5,4},{6,7},{7,6},{8,9},{9,8},{10,11... | collective-permute-start | bytes 49160 | tf_op jit(solution)/shard_map/ppermute | solution.py:172
  22.8 0.7 %fusion = (f32[8,128]{1,0:T(8,128)S(1)}, f32[8,128]{1,0:T(8,128)S(1)}) fusion(f32[32,128]{1,0:T(8,128)} %shard_map.86), kind=kLoop, calls=%fused_computation.1 | loop fusion | bytes 16384 | tf_op jit(solution)/shard_map/slice | solution.py:176
  23.5 1.9 %collective-permute-start.4 = (f32[8,128]{1,0:T(8,128)S(1)}, f32[8,128]{1,0:T(8,128)S(1)}, u32[]{:S(2)}, u32[]{:S(2)}) collective-permute-start(f32[8,128]{1,0:T(8,128)S(1)} %get-tuple-element.4), channel_id=1, source_target_pairs={{2,1},{3,0},{4,3},{5,2},{6,5},{7,4},{8,7},{9,6},{10,9},{11,8},{12,... | collective-permute-start | bytes 12296 | tf_op jit(solution)/shard_map/ppermute | solution.py:176
  25.4 3.6 %collective-permute-start.3 = (f32[8,128]{1,0:T(8,128)S(1)}, f32[8,128]{1,0:T(8,128)S(1)}, u32[]{:S(2)}, u32[]{:S(2)}) collective-permute-start(f32[8,128]{1,0:T(8,128)S(1)} %get-tuple-element.5), channel_id=1, source_target_pairs={{0,3},{1,2},{2,5},{3,4},{4,7},{5,6},{6,9},{7,8},{8,11},{9,10},{10,... | collective-permute-start | bytes 12296 | tf_op jit(solution)/shard_map/ppermute | solution.py:174
  29.1 4.7 %collective-permute-done.4.cb_ref = f32[8,128]{1,0:T(8,128)S(1)} collective-permute-done((f32[8,128]{1,0:T(8,128)S(1)}, f32[8,128]{1,0:T(8,128)S(1)}, u32[]{:S(2)}, u32[]{:S(2)}) %collective-permute-start.4) | collective-permute-done | bytes 4128 | tf_op jit(solution)/shard_map/ppermute | solution.py:176
  33.8 0.0 copy-start.3
  33.8 2.0 %collective-permute-done.3.ca_ref = f32[8,128]{1,0:T(8,128)S(1)} collective-permute-done((f32[8,128]{1,0:T(8,128)S(1)}, f32[8,128]{1,0:T(8,128)S(1)}, u32[]{:S(2)}, u32[]{:S(2)}) %collective-permute-start.3) | collective-permute-done | bytes 4128 | tf_op jit(solution)/shard_map/ppermute | solution.py:174
  35.8 0.0 copy-start.4
  35.8 0.0 collective-permute-done.2.side_ref
  35.8 0.0 copy-start.2
  35.8 0.0 collective-permute-done.am.al.ar
  35.9 0.0 copy-start
  35.9 0.0 collective-permute-done.1.bm.bl.br
  35.9 0.0 copy-done.3
  35.9 0.5 copy-done.4
  36.4 0.0 copy-done.2
  36.4 0.4 copy-done
  36.8 0.0 copy-start.1
  36.8 1.0 %copy-done.1 = f32[29,8192]{1,0:T(8,128)} copy-done((f32[29,8192]{1,0:T(8,128)}, f32[29,8192]{1,0:T(8,128)S(1)}, u32[]{:S(2)}) %copy-start.1) | copy-done | bytes 950296
  37.8 22.0 %shard_map.87 = (f32[2,32,8192]{2,1,0:T(8,128)}, f32[2,32,8192]{2,1,0:T(8,128)}, f32[32,8192]{1,0:T(8,128)}, f32[32,8192]{1,0:T(8,128)}) custom-call(s32[2]{0:T(128)} %pad_add_fusion.pos_ref, f32[2,32,8192]{2,1,0:T(8,128)} %ur.1, f32[2,32,8192]{2,1,0:T(8,128)} %ur.1, f32[2,32,8192]{2,1,0:T(8,128)} %ur.1, f32[2,32,8192]{2,1,0:T(8,128)} %vr.1, ...), custom_call_target="tpu_custom_call" | custom-call | tf_op jit(solution)/shard_map/pallas_call | solution.py:270
Async XLA Ops:
  4.2 31.6 %collective-permute-start = (f32[29,8192]{1,0:T(8,128)}, f32[29,8192]{1,0:T(8,128)S(1)}, u32[]{:S(2)}, u32[]{:S(2)}) collective-permute-start(f32[29,8192]{1,0:T(8,128)} %shard_map.84), channel_id=1, source_target_pairs={{0,2},{2,4},{4,6},{6,8},{8,10},{10,12},{12,14},{14,16},{16,18},{18... | collective-permute-start | bytes 2850824 | tf_op jit(solution)/shard_map/ppermute | solution.py:170
  9.7 26.1 %collective-permute-start.1 = (f32[29,8192]{1,0:T(8,128)}, f32[29,8192]{1,0:T(8,128)S(1)}, u32[]{:S(2)}, u32[]{:S(2)}) collective-permute-start(f32[29,8192]{1,0:T(8,128)} %shard_map.85), channel_id=1, source_target_pairs={{2,0},{4,2},{6,4},{8,6},{10,8},{12,10},{14,12},{16,14},{18,16},{20... | collective-permute-start | bytes 2850824 | tf_op jit(solution)/shard_map/ppermute | solution.py:171
  21.3 14.5 %collective-permute-start.2 = (f32[32,128]{1,0:T(8,128)}, f32[32,128]{1,0:T(8,128)S(1)}, u32[]{:S(2)}, u32[]{:S(2)}) collective-permute-start(f32[32,128]{1,0:T(8,128)} %shard_map.86), channel_id=1, source_target_pairs={{0,1},{1,0},{2,3},{3,2},{4,5},{5,4},{6,7},{7,6},{8,9},{9,8},{10,11... | collective-permute-start | bytes 49160 | tf_op jit(solution)/shard_map/ppermute | solution.py:172
  23.5 10.3 %collective-permute-start.4 = (f32[8,128]{1,0:T(8,128)S(1)}, f32[8,128]{1,0:T(8,128)S(1)}, u32[]{:S(2)}, u32[]{:S(2)}) collective-permute-start(f32[8,128]{1,0:T(8,128)S(1)} %get-tuple-element.4), channel_id=1, source_target_pairs={{2,1},{3,0},{4,3},{5,2},{6,5},{7,4},{8,7},{9,6},{10,9},{11,8},{12,... | collective-permute-start | bytes 12296 | tf_op jit(solution)/shard_map/ppermute | solution.py:176
  25.4 10.4 %collective-permute-start.3 = (f32[8,128]{1,0:T(8,128)S(1)}, f32[8,128]{1,0:T(8,128)S(1)}, u32[]{:S(2)}, u32[]{:S(2)}) collective-permute-start(f32[8,128]{1,0:T(8,128)S(1)} %get-tuple-element.5), channel_id=1, source_target_pairs={{0,3},{1,2},{2,5},{3,4},{4,7},{5,6},{6,9},{7,8},{8,11},{9,10},{10,... | collective-permute-start | bytes 12296 | tf_op jit(solution)/shard_map/ppermute | solution.py:174
  33.8 2.0 %copy-start.3 = (f32[8,128]{1,0:T(8,128)}, f32[8,128]{1,0:T(8,128)S(1)}, u32[]{:S(2)}) copy-start(f32[8,128]{1,0:T(8,128)S(1)} %collective-permute-done.4.cb_ref) | copy-start | bytes 12292
  35.8 0.6 copy-start.4
  35.8 0.6 %copy-start.2 = (f32[32,128]{1,0:T(8,128)}, f32[32,128]{1,0:T(8,128)S(1)}, u32[]{:S(2)}) copy-start(f32[32,128]{1,0:T(8,128)S(1)} %collective-permute-done.2.side_ref) | copy-start | bytes 49156
  35.9 1.0 %copy-start = (f32[29,8192]{1,0:T(8,128)}, f32[29,8192]{1,0:T(8,128)S(1)}, u32[]{:S(2)}) copy-start(f32[29,8192]{1,0:T(8,128)S(1)} %collective-permute-done.am.al.ar) | copy-start | bytes 2850820
  36.8 1.0 %copy-start.1 = (f32[29,8192]{1,0:T(8,128)}, f32[29,8192]{1,0:T(8,128)S(1)}, u32[]{:S(2)}) copy-start(f32[29,8192]{1,0:T(8,128)S(1)} %collective-permute-done.1.bm.bl.br) | copy-start | bytes 2850820
